TPU v7x, 32 devices: a whole 2x2x4 slice. The times are simulated.
32 devices in a mesh: grp: 8 (over z, x), leaf: 4 (over y, core).
Axes of the slice: x: 2, y: 2, z: 4, core: 2. Of those that a mesh axis runs over, the one named last changes fastest.
Arguments:
- inputs: float32 [65536, 64], P(('grp', 'leaf')), may hold values from -6 to 6
- freqs: float32 [64, 256], replicated, may hold values from -0.75 to 0.75
- phases: float32 [256], replicated, may hold values from -3.140625 to 3.140625
- sample_weight: float32 [65536], P(('grp', 'leaf')), as said below
- stored: float32 [32, 256, 256], P(('grp', 'leaf')), as said below
- root: int32 [32], replicated, may hold values from 0 to 31, each once
Outputs:
- factor: float32 [256, 256], replicated
- basis: float32 [65536, 256], P(('grp', 'leaf'))
Inputs may be any that keep to these rules, and one draw needn't show every extreme that they name: `root`: each device index once, in the order grp first, leaf second; only the first entry is read. `stored`: each slot is upper triangular with a positive diagonal. `sample_weight`: positive row weights.
All inputs are finite; a program needn't handle non-finite values.
Results may differ from a plain program's by a relative error of at most 0.0003.
Values sent between devices are 32-bit elements; how exact they have to be, the bound alone decides.
No kernel may reach another device: no remote copies, remote signals or barrier semaphores. Data moves between devices by JAX's collectives and lax.ppermute only.
A program may use at most 64 MiB of HBM per device.

v0:
```python
import math

import jax
import jax.numpy as jnp
from jax import lax
from jax.sharding import PartitionSpec as P


def partner(array, axis, distance):
    return lax.ppermute(array, axis, [(i, i ^ 1 << distance) for i in range(lax.axis_size(axis))])


def spread(array, axis, root):
    mine = lax.axis_index(axis) == root
    return lax.psum(jnp.where(mine, array, jnp.zeros_like(array)), axis)


def per_device(inputs, freqs, phases, sample_weight, stored, root):
    total_rows = inputs.shape[0] * lax.axis_size("grp") * lax.axis_size("leaf")
    norm_scale = 1.0 / math.sqrt(total_rows)
    proj = jnp.dot(inputs, freqs, precision=lax.Precision.HIGHEST) + phases[None, :]
    features = jnp.sqrt(sample_weight)[:, None] * jnp.cos(proj) * norm_scale
    gram = lax.dot_general(
        features, features, (((0,), (0,)), ((), ())), precision=lax.Precision.HIGHEST
    )
    running = stored[0]
    payload = gram
    for bit_leaf in range(lax.axis_size("leaf").bit_length() - 1):
        payload = payload + partner(payload, "leaf", bit_leaf)
    for bit_grp in range(lax.axis_size("grp").bit_length() - 1):
        payload = payload + partner(payload, "grp", bit_grp)
    gram = payload
    carried = spread(running, ("grp", "leaf"), root[0])
    gram = jnp.dot(carried.T, carried, precision=lax.Precision.HIGHEST) + gram
    lower = jnp.linalg.cholesky(gram)
    solved = jax.scipy.linalg.solve_triangular(lower, features.T, lower=True)
    basis = solved.T * math.sqrt(total_rows)
    return (lower.T, basis)


def solution(mesh):
    return jax.shard_map(
        per_device,
        mesh=mesh,
        in_specs=(
            P(("grp", "leaf"), None),
            P(),
            P(),
            P(("grp", "leaf")),
            P(("grp", "leaf"), None, None),
            P(),
        ),
        out_specs=(P(), P(("grp", "leaf"), None)),
        check_vma=False,
    )
```

profile of v0, /device:TPU:0, one launch (start us, length us, event | category | flops | bytes accessed | tf_op | source)
XLA Modules:
  0.0 246.1 jit_solution(17475438517466494014)
XLA Ops:
  8.2 9.5 %fusion.2 = f32[2048,256]{1,0:T(8,128)S(1)} fusion(f32[2048,64]{0,1:T(8,128)S(1)} %copy-done, f32[64,256]{1,0:T(8,128)} %param.7, f32[256]{0:T(256)} %param.8, f32[2048]{0:T(1024)S(1)} %sqrt.3), kind=kOutput, calls=%fused_computation.5 | convolution fusion | flops 404226048 | bytes 2696192 | tf_op jit(solution)/shard_map/dot_general | solution.py:21
  17.8 3.6 %fusion.16 = f32[256,256]{0,1:T(8,128)S(1)} fusion(f32[2048,256]{1,0:T(8,128)S(1)} %fusion.2), kind=kOutput, calls=%fused_computation.39 | convolution fusion | flops 1610612736 | bytes 2359296 | tf_op jit(solution)/shard_map/dot_general | solution.py:23
  22.0 1.2 collective-permute-done
  23.2 2.9 %collective-permute-start.1 = (f32[256,256]{0,1:T(8,128)S(1)}, f32[256,256]{0,1:T(8,128)S(1)}, u32[]{:S(2)}, u32[]{:S(2)}) collective-permute-start(f32[256,256]{0,1:T(8,128)S(1)} %add.59), channel_id=1, source_target_pairs={{0,2},{1,3},{2,0},{3,1},{4,6},{5,7},{6,4},{7,5},{8,10},{9,11},{10,... | collective-permute-start | bytes 786440 | tf_op jit(solution)/shard_map/ppermute | solution.py:10
  26.1 6.6 %collective-permute-done.1 = f32[256,256]{0,1:T(8,128)S(1)} collective-permute-done((f32[256,256]{0,1:T(8,128)S(1)}, f32[256,256]{0,1:T(8,128)S(1)}, u32[]{:S(2)}, u32[]{:S(2)}) %collective-permute-start.1) | collective-permute-done | bytes 262176 | tf_op jit(solution)/shard_map/ppermute | solution.py:10
  32.8 1.8 collective-permute-start.2
  34.6 6.1 %collective-permute-done.2 = f32[256,256]{0,1:T(8,128)S(1)} collective-permute-done((f32[256,256]{0,1:T(8,128)S(1)}, f32[256,256]{0,1:T(8,128)S(1)}, u32[]{:S(2)}, u32[]{:S(2)}) %collective-permute-start.2) | collective-permute-done | bytes 262176 | tf_op jit(solution)/shard_map/ppermute | solution.py:10
  40.6 1.6 collective-permute-start.3
  43.0 4.6 %collective-permute-done.3 = f32[256,256]{0,1:T(8,128)S(1)} collective-permute-done((f32[256,256]{0,1:T(8,128)S(1)}, f32[256,256]{0,1:T(8,128)S(1)}, u32[]{:S(2)}, u32[]{:S(2)}) %collective-permute-start.3) | collective-permute-done | bytes 262176 | tf_op jit(solution)/shard_map/ppermute | solution.py:10
  47.7 2.3 collective-permute-start.4
  50.0 121.1 %all-reduce.3.cloned.1.call-done = f32[256,256]{1,0:T(8,128)} async-done(((f32[256,256]{1,0:T(8,128)}), f32[256,256]{1,0:T(8,128)}) %all-reduce.3.cloned.1.call-update) | async-done | bytes 262160 | tf_op jit(solution)/shard_map/psum | solution.py:15
  171.1 1.6 fusion.15
  173.0 11.7 %cholesky.49 = f32[128,128]{1,0:T(8,128)S(1)} custom-call(f32[128,128]{1,0:T(8,128)S(1)} %cholesky.115), custom_call_target="Cholesky" | custom-call | tf_op jit(solution)/shard_map/jit(cholesky)/cholesky | solution.py:35
  184.7 9.8 %custom-call.15 = f32[1,128,128]{1,2,0:T(8,128)S(1)} custom-call(f32[1,128,128]{2,1,0:T(8,128)S(1)} %get-tuple-element.27), custom_call_target="InvertDiagBlocksLowerTriangular" | custom-call | tf_op jit(solution)/shard_map/jit(cholesky)/cholesky | solution.py:35
  195.1 11.7 %cholesky.103 = f32[128,128]{1,0:T(8,128)S(1)} custom-call(f32[128,128]{1,0:T(8,128)S(1)} %convolution_subtract_fusion.1), custom_call_target="Cholesky" | custom-call | tf_op jit(solution)/shard_map/jit(cholesky)/cholesky | solution.py:35
  208.8 0.8 copy.12
  209.7 3.9 %while.1 = (s32[]{:T(128)}, f32[256,256]{1,0:T(8,128)S(1)}, s32[2,2]{1,0:T(2,128)S(1)}, f32[2,128,128]{2,1,0:T(8,128)S(1)}, s32[]{:T(128)}) while((s32[]{:T(128)}, f32[256,256]{1,0:T(8,128)S(1)}, s32[2,2]{1,0:T(2,128)S(1)}, f32[2,128,128]{2,1,0:T(8,128)S(1)}, s32[]{:T(128)}) %tuple.29), condition=%wide.while_cond, body=%wide.while_body.sunk | while | flops 2 | bytes 131189 | solution.py:36
  210.3 1.3 bitcast_dynamic-update-slice_fusion.2
  212.3 1.3 bitcast_dynamic-update-slice_fusion.2
  213.6 19.7 %custom-call.16 = f32[2,128,128]{1,2,0:T(8,128)S(1)} custom-call(f32[2,128,128]{2,1,0:T(8,128)S(1)} %get-tuple-element.9), custom_call_target="InvertDiagBlocksLowerTriangular" | custom-call | tf_op jit(solution)/shard_map/jit(_solve_triangular)/triangular_solve | solution.py:36
  233.3 1.1 fusion.4
  234.4 1.8 convolution_subtract_fusion
  236.2 1.1 fusion.10
  237.5 1.8 copy.13
  (35 shorter events, 5.4 us)
Async XLA Ops:
  7.2 1.1 copy-start
  7.2 163.9 %all-reduce.3.cloned.1.call-start = ((), (), s32[]{:S(2)}) async-start(), calls=%async_computation | async-start | bytes 524288 | tf_op jit(solution)/shard_map/psum | solution.py:15
  21.4 20.8 %copy-start.2 = (s32[32]{0:T(128)S(1)}, s32[32]{0:T(128)}, u32[]{:S(2)}) copy-start(s32[32]{0:T(128)} %param.11) | copy-start | bytes 388
  21.4 20.9 %copy-start.1 = (f32[1,256,256]{2,1,0:T(8,128)S(1)}, f32[1,256,256]{2,1,0:T(8,128)}, u32[]{:S(2)}) copy-start(f32[1,256,256]{2,1,0:T(8,128)} %param.10) | copy-start | bytes 786436
  21.4 1.7 collective-permute-start
  23.2 9.5 %collective-permute-start.1 = (f32[256,256]{0,1:T(8,128)S(1)}, f32[256,256]{0,1:T(8,128)S(1)}, u32[]{:S(2)}, u32[]{:S(2)}) collective-permute-start(f32[256,256]{0,1:T(8,128)S(1)} %add.59), channel_id=1, source_target_pairs={{0,2},{1,3},{2,0},{3,1},{4,6},{5,7},{6,4},{7,5},{8,10},{9,11},{10,... | collective-permute-start | bytes 786440 | tf_op jit(solution)/shard_map/ppermute | solution.py:10
  32.8 7.8 %collective-permute-start.2 = (f32[256,256]{0,1:T(8,128)S(1)}, f32[256,256]{0,1:T(8,128)S(1)}, u32[]{:S(2)}, u32[]{:S(2)}) collective-permute-start(f32[256,256]{0,1:T(8,128)S(1)} %add.60), channel_id=1, source_target_pairs={{0,4},{4,0},{8,12},{12,8},{16,20},{20,16},{24,28},{28,24},{1,5},{5... | collective-permute-start | bytes 786440 | tf_op jit(solution)/shard_map/ppermute | solution.py:10
  40.6 7.0 %collective-permute-start.3 = (f32[256,256]{0,1:T(8,128)S(1)}, f32[256,256]{0,1:T(8,128)S(1)}, u32[]{:S(2)}, u32[]{:S(2)}) collective-permute-start(f32[256,256]{0,1:T(8,128)S(1)} %add.61), channel_id=1, source_target_pairs={{0,8},{4,12},{8,0},{12,4},{16,24},{20,28},{24,16},{28,20},{1,9},{5... | collective-permute-start | bytes 786440 | tf_op jit(solution)/shard_map/ppermute | solution.py:10
  47.7 125.1 %collective-permute-start.4 = (f32[256,256]{0,1:T(8,128)S(1)}, f32[256,256]{0,1:T(8,128)S(1)}, u32[]{:S(2)}, u32[]{:S(2)}) collective-permute-start(f32[256,256]{0,1:T(8,128)S(1)} %add.62), channel_id=1, source_target_pairs={{0,16},{4,20},{8,24},{12,28},{16,0},{20,4},{24,8},{28,12},{1,17},{... | collective-permute-start | bytes 786440 | tf_op jit(solution)/shard_map/ppermute | solution.py:10
Sparse Core Ops, SparseCore 0:
  43.2 127.8 all-reduce.2
where the time goes:
time: 246 us
  waiting for transfers between devices  140 us (57%)
  other arithmetic  54.8 us (22%)
  matrix products  19.2 us (8%)
  between operations  15.6 us (6%)
  starting transfers between devices  9.21 us (4%)
  local copies, waits for them, and re-layouts  7.77 us (3%)
    psum x1, waiting for transfers between devices, spread(): return lax.psum(jnp.where(mine, array, jnp.zeros_like(array)), axis)  121 us
    another operation x6, other arithmetic, per_device(): lower = jnp.linalg.cholesky(gram)  34 us
    another operation x3, other arithmetic, per_device(): solved = jax.scipy.linalg.solve_triangular(lower, features.T, lower=True)  19.7 us
    ppermute x5, waiting for transfers between devices, partner(): lax.ppermute(array, axis, [(i, i ^ 1 << distance) for i in range(lax.axis...  18.4 us
    dot_general x1, matrix products, per_device(): jnp.dot(inputs, freqs, precision=lax.Precision.HIGHEST) + phases[None, :]  9.54 us
    ppermute x5, starting transfers between devices, partner(): lax.ppermute(array, axis, [(i, i ^ 1 << distance) for i in range(lax.axis...  9.17 us
  transfers between devices with their start and end apart: 6, of which 5 were waited for; matrix products, arithmetic and copies ran while one was open for 1% of the time, Pallas kernels for 0%

commit v1 on v0

--- a/solution.py
+++ b/solution.py
@@ -10,11 +10,6 @@
     return lax.ppermute(array, axis, [(i, i ^ 1 << distance) for i in range(lax.axis_size(axis))])
 
 
-def spread(array, axis, root):
-    mine = lax.axis_index(axis) == root
-    return lax.psum(jnp.where(mine, array, jnp.zeros_like(array)), axis)
-
-
 def per_device(inputs, freqs, phases, sample_weight, stored, root):
     total_rows = inputs.shape[0] * lax.axis_size("grp") * lax.axis_size("leaf")
     norm_scale = 1.0 / math.sqrt(total_rows)
@@ -23,15 +18,17 @@
     gram = lax.dot_general(
         features, features, (((0,), (0,)), ((), ())), precision=lax.Precision.HIGHEST
     )
-    running = stored[0]
+    slot = lax.axis_index("grp") * lax.axis_size("leaf") + lax.axis_index("leaf")
+    running = jnp.where(slot == root[0], stored[0], jnp.zeros_like(stored[0]))
+    gram = gram + lax.dot_general(
+        running, running, (((0,), (0,)), ((), ())), precision=lax.Precision.HIGHEST
+    )
     payload = gram
     for bit_leaf in range(lax.axis_size("leaf").bit_length() - 1):
         payload = payload + partner(payload, "leaf", bit_leaf)
     for bit_grp in range(lax.axis_size("grp").bit_length() - 1):
         payload = payload + partner(payload, "grp", bit_grp)
     gram = payload
-    carried = spread(running, ("grp", "leaf"), root[0])
-    gram = jnp.dot(carried.T, carried, precision=lax.Precision.HIGHEST) + gram
     lower = jnp.linalg.cholesky(gram)
     solved = jax.scipy.linalg.solve_triangular(lower, features.T, lower=True)
     basis = solved.T * math.sqrt(total_rows)

time: 246 us -> 121 us (0.49)
  waiting for transfers between devices: 140 us -> 29.6 us
  between operations: 15.6 us -> 2.17 us
    psum x1 -> x0, waiting for transfers between devices: 121 us -> none  [spread(): return lax.psum(jnp.where(mine, array, jnp.zeros_like(array)), axis)]
    ppermute x5, waiting for transfers between devices: 18.4 us -> 29.6 us  [partner(): lax.ppermute(array, axis, [(i, i ^ 1 << distance) for i in range(lax.axis...]
  transfers between devices with their start and end apart: 6 -> 5, of which waited for: 5 -> 5; matrix products, arithmetic and copies ran while one was open for 1% -> 0% of each run, Pallas kernels for 0% -> 0%
where the time goes in v1:
time: 121 us
  other arithmetic  54 us (45%)
  waiting for transfers between devices  29.6 us (24%)
  matrix products  18.2 us (15%)
  starting transfers between devices  9.17 us (8%)
  local copies, waits for them, and re-layouts  8.04 us (7%)
  between operations  2.17 us (2%)
    another operation x6, other arithmetic, per_device(): lower = jnp.linalg.cholesky(gram)  34 us
    ppermute x5, waiting for transfers between devices, partner(): lax.ppermute(array, axis, [(i, i ^ 1 << distance) for i in range(lax.axis...  29.6 us
    another operation x3, other arithmetic, per_device(): solved = jax.scipy.linalg.solve_triangular(lower, features.T, lower=True)  19.7 us
    dot_general x1, matrix products, per_device(): jnp.dot(inputs, freqs, precision=lax.Precision.HIGHEST) + phases[None, :]  9.54 us
    ppermute x5, starting transfers between devices, partner(): lax.ppermute(array, axis, [(i, i ^ 1 << distance) for i in range(lax.axis...  9.17 us
    another operation x3, matrix products, per_device(): solved = jax.scipy.linalg.solve_triangular(lower, features.T, lower=True)  3.97 us
    another operation x6, local copies, waits for them, and re-layouts  3.9 us
    dot_general x1, matrix products, per_device(): lax.dot_general(features, features, (((0,), (0,)), ((), ())), precision=l...  3.63 us
  transfers between devices with their start and end apart: 5, of which 5 were waited for; matrix products, arithmetic and copies ran while one was open for 0% of the time, Pallas kernels for 0%

profile of v1, /device:TPU:0, one launch (start us, length us, event | category | flops | bytes accessed | tf_op | source)
XLA Modules:
  0.0 121.2 jit_solution(16363458404373452900)
XLA Ops:
  0.6 0.8 sqrt.3
  1.7 9.5 %fusion.2 = f32[2048,256]{1,0:T(8,128)S(1)} fusion(f32[2048,64]{0,1:T(8,128)S(1)} %copy-done, f32[64,256]{1,0:T(8,128)} %param.7, f32[256]{0:T(256)} %param.8, f32[2048]{0:T(1024)S(1)} %sqrt.3), kind=kOutput, calls=%fused_computation.5 | convolution fusion | flops 404226048 | bytes 2696192 | tf_op jit(solution)/shard_map/dot_general | solution.py:16
  11.3 3.6 %fusion.20 = f32[256,256]{0,1:T(8,128)S(1)} fusion(f32[2048,256]{1,0:T(8,128)S(1)} %fusion.2), kind=kOutput, calls=%fused_computation.42 | convolution fusion | flops 1610612736 | bytes 2359296 | tf_op jit(solution)/shard_map/dot_general | solution.py:18
  16.1 1.2 collective-permute-done
  17.3 2.9 %collective-permute-start.1 = (f32[256,256]{0,1:T(8,128)S(1)}, f32[256,256]{0,1:T(8,128)S(1)}, u32[]{:S(2)}, u32[]{:S(2)}) collective-permute-start(f32[256,256]{0,1:T(8,128)S(1)} %add.58), channel_id=1, source_target_pairs={{0,2},{1,3},{2,0},{3,1},{4,6},{5,7},{6,4},{7,5},{8,10},{9,11},{10,... | collective-permute-start | bytes 786440 | tf_op jit(solution)/shard_map/ppermute | solution.py:10
  20.3 6.6 %collective-permute-done.1 = f32[256,256]{0,1:T(8,128)S(1)} collective-permute-done((f32[256,256]{0,1:T(8,128)S(1)}, f32[256,256]{0,1:T(8,128)S(1)}, u32[]{:S(2)}, u32[]{:S(2)}) %collective-permute-start.1) | collective-permute-done | bytes 262176 | tf_op jit(solution)/shard_map/ppermute | solution.py:10
  26.9 1.8 %collective-permute-start.2 = (f32[256,256]{0,1:T(8,128)S(1)}, f32[256,256]{0,1:T(8,128)S(1)}, u32[]{:S(2)}, u32[]{:S(2)}) collective-permute-start(f32[256,256]{0,1:T(8,128)S(1)} %add.59), channel_id=1, source_target_pairs={{0,4},{4,0},{8,12},{12,8},{16,20},{20,16},{24,28},{28,24},{1,5},{5... | collective-permute-start | bytes 786440 | tf_op jit(solution)/shard_map/ppermute | solution.py:10
  28.7 6.1 %collective-permute-done.2 = f32[256,256]{0,1:T(8,128)S(1)} collective-permute-done((f32[256,256]{0,1:T(8,128)S(1)}, f32[256,256]{0,1:T(8,128)S(1)}, u32[]{:S(2)}, u32[]{:S(2)}) %collective-permute-start.2) | collective-permute-done | bytes 262176 | tf_op jit(solution)/shard_map/ppermute | solution.py:10
  34.8 1.6 %collective-permute-start.3 = (f32[256,256]{0,1:T(8,128)S(1)}, f32[256,256]{0,1:T(8,128)S(1)}, u32[]{:S(2)}, u32[]{:S(2)}) collective-permute-start(f32[256,256]{0,1:T(8,128)S(1)} %add.60), channel_id=1, source_target_pairs={{0,8},{4,12},{8,0},{12,4},{16,24},{20,28},{24,16},{28,20},{1,9},{5... | collective-permute-start | bytes 786440 | tf_op jit(solution)/shard_map/ppermute | solution.py:10
  36.4 5.4 %collective-permute-done.3 = f32[256,256]{0,1:T(8,128)S(1)} collective-permute-done((f32[256,256]{0,1:T(8,128)S(1)}, f32[256,256]{0,1:T(8,128)S(1)}, u32[]{:S(2)}, u32[]{:S(2)}) %collective-permute-start.3) | collective-permute-done | bytes 262176 | tf_op jit(solution)/shard_map/ppermute | solution.py:10
  41.8 2.3 %collective-permute-start.4 = (f32[256,256]{0,1:T(8,128)S(1)}, f32[256,256]{0,1:T(8,128)S(1)}, u32[]{:S(2)}, u32[]{:S(2)}) collective-permute-start(f32[256,256]{0,1:T(8,128)S(1)} %add.61), channel_id=1, source_target_pairs={{0,16},{4,20},{8,24},{12,28},{16,0},{20,4},{24,8},{28,12},{1,17},{... | collective-permute-start | bytes 786440 | tf_op jit(solution)/shard_map/ppermute | solution.py:10
  44.1 10.3 %collective-permute-done.4 = f32[256,256]{0,1:T(8,128)S(1)} collective-permute-done((f32[256,256]{0,1:T(8,128)S(1)}, f32[256,256]{0,1:T(8,128)S(1)}, u32[]{:S(2)}, u32[]{:S(2)}) %collective-permute-start.4) | collective-permute-done | bytes 262176 | tf_op jit(solution)/shard_map/ppermute | solution.py:10
  54.7 11.7 %cholesky.49 = f32[128,128]{1,0:T(8,128)S(1)} custom-call(f32[128,128]{1,0:T(8,128)S(1)} %cholesky.115), custom_call_target="Cholesky" | custom-call | tf_op jit(solution)/shard_map/jit(cholesky)/cholesky | solution.py:32
  66.4 9.8 %custom-call.15 = f32[1,128,128]{1,2,0:T(8,128)S(1)} custom-call(f32[1,128,128]{2,1,0:T(8,128)S(1)} %get-tuple-element.27), custom_call_target="InvertDiagBlocksLowerTriangular" | custom-call | tf_op jit(solution)/shard_map/jit(cholesky)/cholesky | solution.py:32
  76.8 11.7 %cholesky.103 = f32[128,128]{1,0:T(8,128)S(1)} custom-call(f32[128,128]{1,0:T(8,128)S(1)} %slice_subtract_fusion), custom_call_target="Cholesky" | custom-call | tf_op jit(solution)/shard_map/jit(cholesky)/cholesky | solution.py:32
  90.5 1.0 copy.11
  91.6 3.9 %while.1 = (s32[]{:T(128)}, f32[256,256]{1,0:T(8,128)S(1)}, s32[2,2]{1,0:T(2,128)S(1)}, f32[2,128,128]{2,1,0:T(8,128)S(1)}, s32[]{:T(128)}) while((s32[]{:T(128)}, f32[256,256]{1,0:T(8,128)S(1)}, s32[2,2]{1,0:T(2,128)S(1)}, f32[2,128,128]{2,1,0:T(8,128)S(1)}, s32[]{:T(128)}) %tuple.29), condition=%wide.while_cond, body=%wide.while_body.sunk | while | flops 2 | bytes 131189 | solution.py:33
  92.2 1.4 %bitcast_dynamic-update-slice_fusion.2 = f32[2,128,128]{2,1,0:T(8,128)S(1)} fusion(f32[2,128,128]{2,1,0:T(8,128)S(1)} %get-tuple-element.69, s32[]{:T(128)S(6)} %copy.20, f32[256,256]{1,0:T(8,128)S(1)} %get-tuple-element.72, s32[]{:T(128)} %bitcast.43, s32[]{:T(128)} %bitcast.44), kind=kLoop, calls=%fused_computation.clone.1 | loop fusion | bytes 131084 | tf_op jit(solution)/shard_map/jit(_solve_triangular)/triangular_solve
  94.2 1.4 %bitcast_dynamic-update-slice_fusion.2 = f32[2,128,128]{2,1,0:T(8,128)S(1)} fusion(f32[2,128,128]{2,1,0:T(8,128)S(1)} %get-tuple-element.69, s32[]{:T(128)S(6)} %copy.20, f32[256,256]{1,0:T(8,128)S(1)} %get-tuple-element.72, s32[]{:T(128)} %bitcast.43, s32[]{:T(128)} %bitcast.44), kind=kLoop, calls=%fused_computation.clone.1 | loop fusion | bytes 131084 | tf_op jit(solution)/shard_map/jit(_solve_triangular)/triangular_solve
  95.6 19.7 %custom-call.16 = f32[2,128,128]{1,2,0:T(8,128)S(1)} custom-call(f32[2,128,128]{2,1,0:T(8,128)S(1)} %get-tuple-element.9), custom_call_target="InvertDiagBlocksLowerTriangular" | custom-call | tf_op jit(solution)/shard_map/jit(_solve_triangular)/triangular_solve | solution.py:33
  115.2 1.1 fusion.4
  116.3 1.8 %convolution_subtract_fusion = f32[128,2048]{0,1:T(8,128)S(1)} fusion(f32[128,2048]{1,0:T(8,128)S(1)} %fusion.4, f32[256,2048]{0,1:T(8,128)S(1)} %bitcast.46, f32[256,256]{1,0:T(8,128)S(1)} %get-tuple-element.76), kind=kOutput, calls=%fused_computation.6 | convolution fusion | flops 402915328 | bytes 3211264 | tf_op jit(solution)/shard_map/jit(_solve_triangular)/triangular_solve | solution.py:33
  118.1 1.1 fusion.14
  119.4 1.8 %copy.12 = f32[2048,256]{1,0:T(8,128)} copy(f32[2048,256]{0,1:T(8,128)S(1)} %fusion.3) | data formatting | bytes 4194304
  (31 shorter events, 4.5 us)
Async XLA Ops:
  0.6 1.1 copy-start
  11.2 3.7 %copy-start.2 = (s32[32]{0:T(128)S(1)}, s32[32]{0:T(128)}, u32[]{:S(2)}) copy-start(s32[32]{0:T(128)} %param.11) | copy-start | bytes 388
  11.2 3.7 %copy-start.1 = (f32[1,256,256]{2,1,0:T(8,128)S(1)}, f32[1,256,256]{2,1,0:T(8,128)}, u32[]{:S(2)}) copy-start(f32[1,256,256]{2,1,0:T(8,128)} %param.10) | copy-start | bytes 786436
  15.6 1.7 %collective-permute-start = (f32[256,256]{0,1:T(8,128)S(1)}, f32[256,256]{0,1:T(8,128)S(1)}, u32[]{:S(2)}, u32[]{:S(2)}) collective-permute-start(f32[256,256]{0,1:T(8,128)S(1)} %convolution_add_fusion.1), channel_id=1, source_target_pairs={{0,1},{1,0},{2,3},{3,2},{4,5},{5,4},{6,7},{7,6},{8,9},{9,8},{10,11... | collective-permute-start | bytes 786440 | tf_op jit(solution)/shard_map/ppermute | solution.py:10
  17.3 9.5 %collective-permute-start.1 = (f32[256,256]{0,1:T(8,128)S(1)}, f32[256,256]{0,1:T(8,128)S(1)}, u32[]{:S(2)}, u32[]{:S(2)}) collective-permute-start(f32[256,256]{0,1:T(8,128)S(1)} %add.58), channel_id=1, source_target_pairs={{0,2},{1,3},{2,0},{3,1},{4,6},{5,7},{6,4},{7,5},{8,10},{9,11},{10,... | collective-permute-start | bytes 786440 | tf_op jit(solution)/shard_map/ppermute | solution.py:10
  26.9 7.8 %collective-permute-start.2 = (f32[256,256]{0,1:T(8,128)S(1)}, f32[256,256]{0,1:T(8,128)S(1)}, u32[]{:S(2)}, u32[]{:S(2)}) collective-permute-start(f32[256,256]{0,1:T(8,128)S(1)} %add.59), channel_id=1, source_target_pairs={{0,4},{4,0},{8,12},{12,8},{16,20},{20,16},{24,28},{28,24},{1,5},{5... | collective-permute-start | bytes 786440 | tf_op jit(solution)/shard_map/ppermute | solution.py:10
  34.8 7.0 %collective-permute-start.3 = (f32[256,256]{0,1:T(8,128)S(1)}, f32[256,256]{0,1:T(8,128)S(1)}, u32[]{:S(2)}, u32[]{:S(2)}) collective-permute-start(f32[256,256]{0,1:T(8,128)S(1)} %add.60), channel_id=1, source_target_pairs={{0,8},{4,12},{8,0},{12,4},{16,24},{20,28},{24,16},{28,20},{1,9},{5... | collective-permute-start | bytes 786440 | tf_op jit(solution)/shard_map/ppermute | solution.py:10
  41.8 12.6 %collective-permute-start.4 = (f32[256,256]{0,1:T(8,128)S(1)}, f32[256,256]{0,1:T(8,128)S(1)}, u32[]{:S(2)}, u32[]{:S(2)}) collective-permute-start(f32[256,256]{0,1:T(8,128)S(1)} %add.61), channel_id=1, source_target_pairs={{0,16},{4,20},{8,24},{12,28},{16,0},{20,4},{24,8},{28,12},{1,17},{... | collective-permute-start | bytes 786440 | tf_op jit(solution)/shard_map/ppermute | solution.py:10

commit v2 on v1

--- a/solution.py
+++ b/solution.py
@@ -8,6 +8,26 @@
 
 def partner(array, axis, distance):
     return lax.ppermute(array, axis, [(i, i ^ 1 << distance) for i in range(lax.axis_size(axis))])
+
+
+def mm(a, b):
+    return jnp.dot(a, b, precision=lax.Precision.HIGHEST)
+
+
+def cholesky_and_inverse(gram):
+    n = gram.shape[0]
+    h = n // 2
+    eye = jnp.eye(h, dtype=gram.dtype)
+    l11 = jnp.linalg.cholesky(gram[:h, :h])
+    i11 = jax.scipy.linalg.solve_triangular(l11, eye, lower=True)
+    l21 = mm(gram[h:, :h], i11.T)
+    l22 = jnp.linalg.cholesky(gram[h:, h:] - mm(l21, l21.T))
+    i22 = jax.scipy.linalg.solve_triangular(l22, eye, lower=True)
+    i21 = -mm(i22, mm(l21, i11))
+    zero = jnp.zeros_like(l11)
+    lower = jnp.block([[l11, zero], [l21, l22]])
+    inverse = jnp.block([[i11, zero], [i21, i22]])
+    return lower, inverse
 
 
 def per_device(inputs, freqs, phases, sample_weight, stored, root):
@@ -29,9 +49,10 @@
     for bit_grp in range(lax.axis_size("grp").bit_length() - 1):
         payload = payload + partner(payload, "grp", bit_grp)
     gram = payload
-    lower = jnp.linalg.cholesky(gram)
-    solved = jax.scipy.linalg.solve_triangular(lower, features.T, lower=True)
-    basis = solved.T * math.sqrt(total_rows)
+    lower, inverse = cholesky_and_inverse(gram)
+    basis = lax.dot_general(
+        features, inverse, (((1,), (1,)), ((), ())), precision=lax.Precision.HIGHEST
+    ) * math.sqrt(total_rows)
     return (lower.T, basis)
 
 

time: 121 us -> 107 us (0.88)
  other arithmetic: 54 us -> 46.1 us
  local copies, waits for them, and re-layouts: 8.04 us -> 2.26 us
  between operations: 2.17 us -> 0.91 us
    another operation x9 -> x10, other arithmetic: 53.7 us -> 45.9 us  [the longest x3 12.5 us: cholesky_and_inverse(): l22 = jnp.linalg.cholesky(gram[h:, h:] - mm(l21, l21.T))]
    dot_general x0 -> x5, matrix products: none -> 4.22 us  [the longest x1 3.16 us: per_device(): lax.dot_general(features, inverse, (((1,), (1,)), ((), ())), precision=la...]
    another operation x9 -> x1, local copies, waits for them, and re-layouts: 3.99 us -> 0.09 us  [cholesky_and_inverse(): i22 = jax.scipy.linalg.solve_triangular(l22, eye, lower=True)]
    another operation x5 -> x2, matrix products: 4.44 us -> 0.55 us  [the longest x1 0.29 us: cholesky_and_inverse(): i11 = jax.scipy.linalg.solve_triangular(l11, eye, lower=True)]
    unnamed x8 -> x7, local copies, waits for them, and re-layouts: 3.16 us -> 1.14 us
where the time goes in v2:
time: 107 us
  other arithmetic  46.1 us (43%)
  waiting for transfers between devices  29.6 us (28%)
  matrix products  18.5 us (17%)
  starting transfers between devices  9.17 us (9%)
  local copies, waits for them, and re-layouts  2.26 us (2%)
    ppermute x5, waiting for transfers between devices, partner(): lax.ppermute(array, axis, [(i, i ^ 1 << distance) for i in range(lax.axis...  29.6 us
    another operation x3, other arithmetic, cholesky_and_inverse(): l22 = jnp.linalg.cholesky(gram[h:, h:] - mm(l21, l21.T))  12.5 us
    another operation x3, other arithmetic, cholesky_and_inverse(): l11 = jnp.linalg.cholesky(gram[:h, :h])  12.4 us
    another operation x2, other arithmetic, cholesky_and_inverse(): i11 = jax.scipy.linalg.solve_triangular(l11, eye, lower=True)  10.5 us
    another operation x2, other arithmetic, cholesky_and_inverse(): i22 = jax.scipy.linalg.solve_triangular(l22, eye, lower=True)  10.5 us
    dot_general x1, matrix products, per_device(): jnp.dot(inputs, freqs, precision=lax.Precision.HIGHEST) + phases[None, :]  9.54 us
    ppermute x5, starting transfers between devices, partner(): lax.ppermute(array, axis, [(i, i ^ 1 << distance) for i in range(lax.axis...  9.17 us
    dot_general x1, matrix products, per_device(): lax.dot_general(features, features, (((0,), (0,)), ((), ())), precision=l...  3.63 us
  transfers between devices with their start and end apart: 5, of which 5 were waited for; matrix products, arithmetic and copies ran while one was open for 0% of the time, Pallas kernels for 0%

profile of v2, /device:TPU:0, one launch (start us, length us, event | category | flops | bytes accessed | tf_op | source)
XLA Modules:
  0.0 106.5 jit_solution(9320139371288461439)
XLA Ops:
  0.6 0.8 sqrt.3
  1.7 9.5 %fusion.2 = f32[2048,256]{1,0:T(8,128)S(1)} fusion(f32[2048,64]{0,1:T(8,128)S(1)} %copy-done, f32[64,256]{1,0:T(8,128)} %param.10, f32[256]{0:T(256)} %param.11, f32[2048]{0:T(1024)S(1)} %sqrt.3), kind=kOutput, calls=%fused_computation.4 | convolution fusion | flops 404226048 | bytes 2696192 | tf_op jit(solution)/shard_map/dot_general | solution.py:36
  11.3 3.6 %fusion.28 = f32[256,256]{0,1:T(8,128)S(1)} fusion(f32[2048,256]{1,0:T(8,128)S(1)} %fusion.2), kind=kOutput, calls=%fused_computation.48 | convolution fusion | flops 1610612736 | bytes 2359296 | tf_op jit(solution)/shard_map/dot_general | solution.py:38
  15.0 0.6 convolution_add_fusion.1
  15.6 0.6 collective-permute-start
  16.1 1.2 %collective-permute-done = f32[256,256]{0,1:T(8,128)S(1)} collective-permute-done((f32[256,256]{0,1:T(8,128)S(1)}, f32[256,256]{0,1:T(8,128)S(1)}, u32[]{:S(2)}, u32[]{:S(2)}) %collective-permute-start) | collective-permute-done | bytes 262176 | tf_op jit(solution)/shard_map/ppermute | solution.py:10
  17.3 2.9 %collective-permute-start.1 = (f32[256,256]{0,1:T(8,128)S(1)}, f32[256,256]{0,1:T(8,128)S(1)}, u32[]{:S(2)}, u32[]{:S(2)}) collective-permute-start(f32[256,256]{0,1:T(8,128)S(1)} %add.46), channel_id=1, source_target_pairs={{0,2},{1,3},{2,0},{3,1},{4,6},{5,7},{6,4},{7,5},{8,10},{9,11},{10,... | collective-permute-start | bytes 786440 | tf_op jit(solution)/shard_map/ppermute | solution.py:10
  20.3 6.6 %collective-permute-done.1 = f32[256,256]{0,1:T(8,128)S(1)} collective-permute-done((f32[256,256]{0,1:T(8,128)S(1)}, f32[256,256]{0,1:T(8,128)S(1)}, u32[]{:S(2)}, u32[]{:S(2)}) %collective-permute-start.1) | collective-permute-done | bytes 262176 | tf_op jit(solution)/shard_map/ppermute | solution.py:10
  26.9 1.8 %collective-permute-start.2 = (f32[256,256]{0,1:T(8,128)S(1)}, f32[256,256]{0,1:T(8,128)S(1)}, u32[]{:S(2)}, u32[]{:S(2)}) collective-permute-start(f32[256,256]{0,1:T(8,128)S(1)} %add.47), channel_id=1, source_target_pairs={{0,4},{4,0},{8,12},{12,8},{16,20},{20,16},{24,28},{28,24},{1,5},{5... | collective-permute-start | bytes 786440 | tf_op jit(solution)/shard_map/ppermute | solution.py:10
  28.7 6.1 %collective-permute-done.2 = f32[256,256]{0,1:T(8,128)S(1)} collective-permute-done((f32[256,256]{0,1:T(8,128)S(1)}, f32[256,256]{0,1:T(8,128)S(1)}, u32[]{:S(2)}, u32[]{:S(2)}) %collective-permute-start.2) | collective-permute-done | bytes 262176 | tf_op jit(solution)/shard_map/ppermute | solution.py:10
  34.8 1.6 %collective-permute-start.3 = (f32[256,256]{0,1:T(8,128)S(1)}, f32[256,256]{0,1:T(8,128)S(1)}, u32[]{:S(2)}, u32[]{:S(2)}) collective-permute-start(f32[256,256]{0,1:T(8,128)S(1)} %add.48), channel_id=1, source_target_pairs={{0,8},{4,12},{8,0},{12,4},{16,24},{20,28},{24,16},{28,20},{1,9},{5... | collective-permute-start | bytes 786440 | tf_op jit(solution)/shard_map/ppermute | solution.py:10
  36.4 5.4 %collective-permute-done.3 = f32[256,256]{0,1:T(8,128)S(1)} collective-permute-done((f32[256,256]{0,1:T(8,128)S(1)}, f32[256,256]{0,1:T(8,128)S(1)}, u32[]{:S(2)}, u32[]{:S(2)}) %collective-permute-start.3) | collective-permute-done | bytes 262176 | tf_op jit(solution)/shard_map/ppermute | solution.py:10
  41.8 2.3 %collective-permute-start.4 = (f32[256,256]{0,1:T(8,128)S(1)}, f32[256,256]{0,1:T(8,128)S(1)}, u32[]{:S(2)}, u32[]{:S(2)}) collective-permute-start(f32[256,256]{0,1:T(8,128)S(1)} %add.49), channel_id=1, source_target_pairs={{0,16},{4,20},{8,24},{12,28},{16,0},{20,4},{24,8},{28,12},{1,17},{... | collective-permute-start | bytes 786440 | tf_op jit(solution)/shard_map/ppermute | solution.py:10
  44.1 10.3 %collective-permute-done.4 = f32[256,256]{0,1:T(8,128)S(1)} collective-permute-done((f32[256,256]{0,1:T(8,128)S(1)}, f32[256,256]{0,1:T(8,128)S(1)}, u32[]{:S(2)}, u32[]{:S(2)}) %collective-permute-start.4) | collective-permute-done | bytes 262176 | tf_op jit(solution)/shard_map/ppermute | solution.py:10
  54.6 11.7 %cholesky.44 = f32[128,128]{1,0:T(8,128)S(1)} custom-call(f32[128,128]{1,0:T(8,128)S(1)} %fusion.23), custom_call_target="Cholesky" | custom-call | tf_op jit(solution)/shard_map/jit(cholesky)/cholesky | solution.py:21
  66.4 0.6 compare_reduce_fusion.1
  67.0 0.7 select_bitcast_fusion.1
  67.7 9.8 %custom-call.6 = f32[1,128,128]{1,2,0:T(8,128)S(1)} custom-call(f32[1,128,128]{2,1,0:T(8,128)S(1)} %get-tuple-element.8), custom_call_target="InvertDiagBlocksLowerTriangular" | custom-call | tf_op jit(solution)/shard_map/jit(_solve_triangular)/triangular_solve | solution.py:22
  78.8 11.9 %cholesky.55 = f32[128,128]{1,0:T(8,128)S(1)} custom-call(f32[128,128]{1,0:T(8,128)S(1)} %fusion.21), custom_call_target="Cholesky" | custom-call | tf_op jit(solution)/shard_map/jit(cholesky)/cholesky | solution.py:24
  90.7 0.6 compare_reduce_fusion
  91.3 0.7 select_bitcast_fusion
  92.0 9.8 %custom-call.7 = f32[1,128,128]{1,2,0:T(8,128)S(1)} custom-call(f32[1,128,128]{2,1,0:T(8,128)S(1)} %get-tuple-element.6), custom_call_target="InvertDiagBlocksLowerTriangular" | custom-call | tf_op jit(solution)/shard_map/jit(_solve_triangular)/triangular_solve | solution.py:25
  102.5 0.8 copy.15
  103.4 3.2 %convolution_multiply_fusion = f32[2048,256]{1,0:T(8,128)} fusion(f32[2048,256]{1,0:T(8,128)S(1)} %fusion.2, f32[128,128]{1,0:T(8,128)S(1)} %fusion.16, f32[128,128]{1,0:T(8,128)S(1)} %copy.14, f32[128,128]{1,0:T(8,128)S(1)} %convolution_negate_fusion), kind=kOutput, calls=%fused_computation | convolution fusion | flops 1611399168 | bytes 4390912 | tf_op jit(solution)/shard_map/dot_general | solution.py:53
  (27 shorter events, 2.6 us)
Async XLA Ops:
  0.6 1.1 copy-start
  11.2 3.7 %copy-start.2 = (s32[32]{0:T(128)S(1)}, s32[32]{0:T(128)}, u32[]{:S(2)}) copy-start(s32[32]{0:T(128)} %param.14) | copy-start | bytes 388
  11.2 3.7 %copy-start.1 = (f32[1,256,256]{2,1,0:T(8,128)S(1)}, f32[1,256,256]{2,1,0:T(8,128)}, u32[]{:S(2)}) copy-start(f32[1,256,256]{2,1,0:T(8,128)} %param.13) | copy-start | bytes 786436
  15.6 1.7 %collective-permute-start = (f32[256,256]{0,1:T(8,128)S(1)}, f32[256,256]{0,1:T(8,128)S(1)}, u32[]{:S(2)}, u32[]{:S(2)}) collective-permute-start(f32[256,256]{0,1:T(8,128)S(1)} %convolution_add_fusion.1), channel_id=1, source_target_pairs={{0,1},{1,0},{2,3},{3,2},{4,5},{5,4},{6,7},{7,6},{8,9},{9,8},{10,11... | collective-permute-start | bytes 786440 | tf_op jit(solution)/shard_map/ppermute | solution.py:10
  17.3 9.5 %collective-permute-start.1 = (f32[256,256]{0,1:T(8,128)S(1)}, f32[256,256]{0,1:T(8,128)S(1)}, u32[]{:S(2)}, u32[]{:S(2)}) collective-permute-start(f32[256,256]{0,1:T(8,128)S(1)} %add.46), channel_id=1, source_target_pairs={{0,2},{1,3},{2,0},{3,1},{4,6},{5,7},{6,4},{7,5},{8,10},{9,11},{10,... | collective-permute-start | bytes 786440 | tf_op jit(solution)/shard_map/ppermute | solution.py:10
  26.9 7.8 %collective-permute-start.2 = (f32[256,256]{0,1:T(8,128)S(1)}, f32[256,256]{0,1:T(8,128)S(1)}, u32[]{:S(2)}, u32[]{:S(2)}) collective-permute-start(f32[256,256]{0,1:T(8,128)S(1)} %add.47), channel_id=1, source_target_pairs={{0,4},{4,0},{8,12},{12,8},{16,20},{20,16},{24,28},{28,24},{1,5},{5... | collective-permute-start | bytes 786440 | tf_op jit(solution)/shard_map/ppermute | solution.py:10
  34.8 7.0 %collective-permute-start.3 = (f32[256,256]{0,1:T(8,128)S(1)}, f32[256,256]{0,1:T(8,128)S(1)}, u32[]{:S(2)}, u32[]{:S(2)}) collective-permute-start(f32[256,256]{0,1:T(8,128)S(1)} %add.48), channel_id=1, source_target_pairs={{0,8},{4,12},{8,0},{12,4},{16,24},{20,28},{24,16},{28,20},{1,9},{5... | collective-permute-start | bytes 786440 | tf_op jit(solution)/shard_map/ppermute | solution.py:10
  41.8 12.6 %collective-permute-start.4 = (f32[256,256]{0,1:T(8,128)S(1)}, f32[256,256]{0,1:T(8,128)S(1)}, u32[]{:S(2)}, u32[]{:S(2)}) collective-permute-start(f32[256,256]{0,1:T(8,128)S(1)} %add.49), channel_id=1, source_target_pairs={{0,16},{4,20},{8,24},{12,28},{16,0},{20,4},{24,8},{28,12},{1,17},{... | collective-permute-start | bytes 786440 | tf_op jit(solution)/shard_map/ppermute | solution.py:10

commit v3 on v2

--- a/solution.py
+++ b/solution.py
@@ -14,20 +14,62 @@
     return jnp.dot(a, b, precision=lax.Precision.HIGHEST)
 
 
-def cholesky_and_inverse(gram):
-    n = gram.shape[0]
-    h = n // 2
-    eye = jnp.eye(h, dtype=gram.dtype)
-    l11 = jnp.linalg.cholesky(gram[:h, :h])
+def cholesky_and_inverse(g11, g21, g22):
+    h = g11.shape[0]
+    eye = jnp.eye(h, dtype=g11.dtype)
+    l11 = jnp.linalg.cholesky(g11)
     i11 = jax.scipy.linalg.solve_triangular(l11, eye, lower=True)
-    l21 = mm(gram[h:, :h], i11.T)
-    l22 = jnp.linalg.cholesky(gram[h:, h:] - mm(l21, l21.T))
+    l21 = mm(g21, i11.T)
+    l22 = jnp.linalg.cholesky(g22 - mm(l21, l21.T))
     i22 = jax.scipy.linalg.solve_triangular(l22, eye, lower=True)
     i21 = -mm(i22, mm(l21, i11))
     zero = jnp.zeros_like(l11)
     lower = jnp.block([[l11, zero], [l21, l22]])
     inverse = jnp.block([[i11, zero], [i21, i22]])
     return lower, inverse
+
+
+def pack(gram):
+    h = gram.shape[0] // 2
+    row = lax.broadcasted_iota(jnp.int32, (h, h), 0)
+    col = lax.broadcasted_iota(jnp.int32, (h, h), 1)
+    tri = jnp.where(row <= col, gram[:h, :h], gram[h:, h:])
+    diag = jnp.diagonal(gram[h:, h:])
+    pad = jnp.zeros((7, h), gram.dtype)
+    first = jnp.concatenate([tri, diag[None, :], pad], axis=0)
+    second = jnp.concatenate([gram[h:, :h], jnp.zeros((8, h), gram.dtype)], axis=0)
+    return first, second
+
+
+def unpack(first, second):
+    h = first.shape[1]
+    row = lax.broadcasted_iota(jnp.int32, (h, h), 0)
+    col = lax.broadcasted_iota(jnp.int32, (h, h), 1)
+    tri = first[:h]
+    g11 = jnp.where(row <= col, tri, tri.T)
+    g22 = jnp.where(row > col, tri, tri.T)
+    g22 = jnp.where(row == col, first[h:h + 1, :], g22)
+    g21 = second[:h]
+    return g11, g21, g22
+
+
+def all_reduce_symmetric(gram):
+    stages = [("leaf", b) for b in range(lax.axis_size("leaf").bit_length() - 1)]
+    stages += [("grp", b) for b in range(lax.axis_size("grp").bit_length() - 1)]
+    first, second = pack(gram)
+    if not stages:
+        return unpack(first, second)
+    axis0, bit0 = stages[0]
+    low = (lax.axis_index(axis0) >> bit0) % 2 == 0
+    keep = jnp.where(low, first, second)
+    send = jnp.where(low, second, first)
+    keep = keep + partner(send, axis0, bit0)
+    for axis, bit in stages[1:]:
+        keep = keep + partner(keep, axis, bit)
+    other = partner(keep, axis0, bit0)
+    first = jnp.where(low, keep, other)
+    second = jnp.where(low, other, keep)
+    return unpack(first, second)
 
 
 def per_device(inputs, freqs, phases, sample_weight, stored, root):
@@ -43,13 +85,8 @@
     gram = gram + lax.dot_general(
         running, running, (((0,), (0,)), ((), ())), precision=lax.Precision.HIGHEST
     )
-    payload = gram
-    for bit_leaf in range(lax.axis_size("leaf").bit_length() - 1):
-        payload = payload + partner(payload, "leaf", bit_leaf)
-    for bit_grp in range(lax.axis_size("grp").bit_length() - 1):
-        payload = payload + partner(payload, "grp", bit_grp)
-    gram = payload
-    lower, inverse = cholesky_and_inverse(gram)
+    gram = all_reduce_symmetric(gram)
+    lower, inverse = cholesky_and_inverse(*gram)
     basis = lax.dot_general(
         features, inverse, (((1,), (1,)), ((), ())), precision=lax.Precision.HIGHEST
     ) * math.sqrt(total_rows)

time: 107 us -> 97.1 us (0.907)
  waiting for transfers between devices: 29.6 us -> 16.9 us
  local copies, waits for them, and re-layouts: 2.26 us -> 3.89 us
  starting transfers between devices: 9.17 us -> 10.5 us
    ppermute x5 -> x6, waiting for transfers between devices: 29.6 us -> 16.9 us  [partner(): lax.ppermute(array, axis, [(i, i ^ 1 << distance) for i in range(lax.axis...]
    ppermute x5 -> x6, starting transfers between devices: 9.17 us -> 10.5 us  [partner(): lax.ppermute(array, axis, [(i, i ^ 1 << distance) for i in range(lax.axis...]
    gather x0 -> x1, local copies, waits for them, and re-layouts: none -> 1.28 us  [pack(): diag = jnp.diagonal(gram[h:, h:])]
  transfers between devices with their start and end apart: 5 -> 6, of which waited for: 5 -> 6; matrix products, arithmetic and copies ran while one was open for 0% -> 0% of each run, Pallas kernels for 0% -> 0%
where the time goes in v3:
time: 97.1 us; the launch traced here: 96.9 us
  other arithmetic  46.1 us (47%)
  matrix products  18.5 us (19%)
  waiting for transfers between devices  16.9 us (17%)
  starting transfers between devices  10.5 us (11%)
  local copies, waits for them, and re-layouts  3.89 us (4%)
  between operations  0.98 us (1%)
    ppermute x6, waiting for transfers between devices, partner(): lax.ppermute(array, axis, [(i, i ^ 1 << distance) for i in range(lax.axis...  16.9 us
    another operation x3, other arithmetic, cholesky_and_inverse(): l22 = jnp.linalg.cholesky(g22 - mm(l21, l21.T))  12.4 us
    another operation x3, other arithmetic, cholesky_and_inverse(): l11 = jnp.linalg.cholesky(g11)  12.4 us
    another operation x2, other arithmetic, cholesky_and_inverse(): i22 = jax.scipy.linalg.solve_triangular(l22, eye, lower=True)  10.6 us
    ppermute x6, starting transfers between devices, partner(): lax.ppermute(array, axis, [(i, i ^ 1 << distance) for i in range(lax.axis...  10.5 us
    another operation x2, other arithmetic, cholesky_and_inverse(): i11 = jax.scipy.linalg.solve_triangular(l11, eye, lower=True)  10.5 us
    dot_general x1, matrix products, per_device(): jnp.dot(inputs, freqs, precision=lax.Precision.HIGHEST) + phases[None, :]  9.54 us
    dot_general x1, matrix products, per_device(): lax.dot_general(features, features, (((0,), (0,)), ((), ())), precision=l...  3.63 us
  transfers between devices with their start and end apart: 6, of which 6 were waited for; matrix products, arithmetic and copies ran while one was open for 0% of the time, Pallas kernels for 0%

profile of v3, /device:TPU:0, one launch (start us, length us, event | category | flops | bytes accessed | tf_op | source)
XLA Modules:
  0.0 96.9 jit_solution(11554103775227728192)
XLA Ops:
  0.7 0.8 sqrt.3
  1.7 9.5 %fusion.2 = f32[2048,256]{1,0:T(8,128)S(1)} fusion(f32[2048,64]{0,1:T(8,128)S(1)} %copy-done, f32[64,256]{1,0:T(8,128)} %param.10, f32[256]{0:T(256)} %param.11, f32[2048]{0:T(1024)S(1)} %sqrt.3), kind=kOutput, calls=%fused_computation.5 | convolution fusion | flops 404226048 | bytes 2696192 | tf_op jit(solution)/shard_map/dot_general | solution.py:78
  11.3 3.6 %fusion.32 = f32[256,256]{0,1:T(8,128)S(1)} fusion(f32[2048,256]{1,0:T(8,128)S(1)} %fusion.2), kind=kOutput, calls=%fused_computation.65 | convolution fusion | flops 1610612736 | bytes 2359296 | tf_op jit(solution)/shard_map/dot_general | solution.py:80
  15.6 1.3 %gather_fusion = f32[128]{0:T(128)S(1)} fusion(f32[128,128]{0,1:T(8,128)S(1)} %get-tuple-element.14, s32[128]{0:T(128)S(1)} %or_bitcast_fusion), kind=kCustom, calls=%fused_computation | custom fusion | bytes 2048 | tf_op jit(solution)/shard_map/jit(diagonal)/cond/branch_0_fun/gather | solution.py:37
  17.7 1.0 %collective-permute-done = f32[136,128]{0,1:T(8,128)S(1)} collective-permute-done((f32[136,128]{0,1:T(8,128)S(1)}, f32[136,128]{0,1:T(8,128)S(1)}, u32[]{:S(2)}, u32[]{:S(2)}) %collective-permute-start) | collective-permute-done | bytes 69664 | tf_op jit(solution)/shard_map/ppermute | solution.py:10
  18.7 2.9 %collective-permute-start.1 = (f32[136,128]{0,1:T(8,128)S(1)}, f32[136,128]{0,1:T(8,128)S(1)}, u32[]{:S(2)}, u32[]{:S(2)}) collective-permute-start(f32[136,128]{0,1:T(8,128)S(1)} %fusion.10), channel_id=1, source_target_pairs={{0,2},{1,3},{2,0},{3,1},{4,6},{5,7},{6,4},{7,5},{8,10},{9,11},{10,... | collective-permute-start | bytes 208904 | tf_op jit(solution)/shard_map/ppermute | solution.py:10
  21.6 3.8 %collective-permute-done.1 = f32[136,128]{0,1:T(8,128)S(1)} collective-permute-done((f32[136,128]{0,1:T(8,128)S(1)}, f32[136,128]{0,1:T(8,128)S(1)}, u32[]{:S(2)}, u32[]{:S(2)}) %collective-permute-start.1) | collective-permute-done | bytes 69664 | tf_op jit(solution)/shard_map/ppermute | solution.py:10
  25.4 1.8 %collective-permute-start.2 = (f32[136,128]{0,1:T(8,128)S(1)}, f32[136,128]{0,1:T(8,128)S(1)}, u32[]{:S(2)}, u32[]{:S(2)}) collective-permute-start(f32[136,128]{0,1:T(8,128)S(1)} %add.58), channel_id=1, source_target_pairs={{0,4},{4,0},{8,12},{12,8},{16,20},{20,16},{24,28},{28,24},{1,5},{5... | collective-permute-start | bytes 208904 | tf_op jit(solution)/shard_map/ppermute | solution.py:10
  27.2 3.3 %collective-permute-done.2 = f32[136,128]{0,1:T(8,128)S(1)} collective-permute-done((f32[136,128]{0,1:T(8,128)S(1)}, f32[136,128]{0,1:T(8,128)S(1)}, u32[]{:S(2)}, u32[]{:S(2)}) %collective-permute-start.2) | collective-permute-done | bytes 69664 | tf_op jit(solution)/shard_map/ppermute | solution.py:10
  30.5 1.9 %collective-permute-start.3 = (f32[136,128]{0,1:T(8,128)S(1)}, f32[136,128]{0,1:T(8,128)S(1)}, u32[]{:S(2)}, u32[]{:S(2)}) collective-permute-start(f32[136,128]{0,1:T(8,128)S(1)} %add.59), channel_id=1, source_target_pairs={{0,8},{4,12},{8,0},{12,4},{16,24},{20,28},{24,16},{28,20},{1,9},{5... | collective-permute-start | bytes 208904 | tf_op jit(solution)/shard_map/ppermute | solution.py:10
  32.4 3.2 %collective-permute-done.3 = f32[136,128]{0,1:T(8,128)S(1)} collective-permute-done((f32[136,128]{0,1:T(8,128)S(1)}, f32[136,128]{0,1:T(8,128)S(1)}, u32[]{:S(2)}, u32[]{:S(2)}) %collective-permute-start.3) | collective-permute-done | bytes 69664 | tf_op jit(solution)/shard_map/ppermute | solution.py:10
  35.5 3.3 %collective-permute-start.4 = (f32[136,128]{0,1:T(8,128)S(1)}, f32[136,128]{0,1:T(8,128)S(1)}, u32[]{:S(2)}, u32[]{:S(2)}) collective-permute-start(f32[136,128]{0,1:T(8,128)S(1)} %add.60), channel_id=1, source_target_pairs={{0,16},{4,20},{8,24},{12,28},{16,0},{20,4},{24,8},{28,12},{1,17},{... | collective-permute-start | bytes 208904 | tf_op jit(solution)/shard_map/ppermute | solution.py:10
  38.9 4.4 %collective-permute-done.4 = f32[136,128]{0,1:T(8,128)S(1)} collective-permute-done((f32[136,128]{0,1:T(8,128)S(1)}, f32[136,128]{0,1:T(8,128)S(1)}, u32[]{:S(2)}, u32[]{:S(2)}) %collective-permute-start.4) | collective-permute-done | bytes 69664 | tf_op jit(solution)/shard_map/ppermute | solution.py:10
  43.3 1.3 %collective-permute-done.5 = f32[136,128]{0,1:T(8,128)S(1)} collective-permute-done((f32[136,128]{0,1:T(8,128)S(1)}, f32[136,128]{0,1:T(8,128)S(1)}, u32[]{:S(2)}, u32[]{:S(2)}) %collective-permute-start.5) | collective-permute-done | bytes 69664 | tf_op jit(solution)/shard_map/ppermute | solution.py:10
  45.0 11.7 %cholesky.44 = f32[128,128]{1,0:T(8,128)S(1)} custom-call(f32[128,128]{1,0:T(8,128)S(1)} %fusion.24), custom_call_target="Cholesky" | custom-call | tf_op jit(solution)/shard_map/jit(cholesky)/cholesky | solution.py:20
  56.8 0.6 compare_reduce_fusion.1
  57.4 0.7 select_bitcast_fusion.1
  58.1 9.8 %custom-call.8 = f32[1,128,128]{1,2,0:T(8,128)S(1)} custom-call(f32[1,128,128]{2,1,0:T(8,128)S(1)} %get-tuple-element.10), custom_call_target="InvertDiagBlocksLowerTriangular" | custom-call | tf_op jit(solution)/shard_map/jit(_solve_triangular)/triangular_solve | solution.py:21
  69.2 11.7 %cholesky.55 = f32[128,128]{1,0:T(8,128)S(1)} custom-call(f32[128,128]{1,0:T(8,128)S(1)} %fusion.22), custom_call_target="Cholesky" | custom-call | tf_op jit(solution)/shard_map/jit(cholesky)/cholesky | solution.py:23
  80.9 0.6 compare_reduce_fusion
  81.6 0.7 select_bitcast_fusion
  82.3 10.0 %custom-call.9 = f32[1,128,128]{1,2,0:T(8,128)S(1)} custom-call(f32[1,128,128]{2,1,0:T(8,128)S(1)} %get-tuple-element.8), custom_call_target="InvertDiagBlocksLowerTriangular" | custom-call | tf_op jit(solution)/shard_map/jit(_solve_triangular)/triangular_solve | solution.py:24
  92.9 0.8 copy.27
  93.7 3.2 %convolution_multiply_fusion = f32[2048,256]{1,0:T(8,128)} fusion(f32[2048,256]{1,0:T(8,128)S(1)} %fusion.2, f32[128,128]{1,0:T(8,128)S(1)} %fusion.17, f32[128,128]{1,0:T(8,128)S(1)} %copy.26, f32[128,128]{1,0:T(8,128)S(1)} %convolution_negate_fusion), kind=kOutput, calls=%fused_computation.1 | convolution fusion | flops 1611399168 | bytes 4390912 | tf_op jit(solution)/shard_map/dot_general | solution.py:90
  (40 shorter events, 4.1 us)
Async XLA Ops:
  0.6 1.1 %copy-start = (f32[2048,64]{0,1:T(8,128)S(1)}, f32[2048,64]{0,1:T(8,128)}, u32[]{:S(2)}) copy-start(f32[2048,64]{0,1:T(8,128)} %param.9) | copy-start | bytes 1572868
  11.2 3.7 %copy-start.2 = (s32[32]{0:T(128)S(1)}, s32[32]{0:T(128)}, u32[]{:S(2)}) copy-start(s32[32]{0:T(128)} %param.14) | copy-start | bytes 388
  11.2 3.7 %copy-start.1 = (f32[1,256,256]{2,1,0:T(8,128)S(1)}, f32[1,256,256]{2,1,0:T(8,128)}, u32[]{:S(2)}) copy-start(f32[1,256,256]{2,1,0:T(8,128)} %param.13) | copy-start | bytes 786436
  17.1 1.5 %collective-permute-start = (f32[136,128]{0,1:T(8,128)S(1)}, f32[136,128]{0,1:T(8,128)S(1)}, u32[]{:S(2)}, u32[]{:S(2)}) collective-permute-start(f32[136,128]{0,1:T(8,128)S(1)} %pad_select_fusion), channel_id=1, source_target_pairs={{0,1},{1,0},{2,3},{3,2},{4,5},{5,4},{6,7},{7,6},{8,9},{9,8},{10,11... | collective-permute-start | bytes 208904 | tf_op jit(solution)/shard_map/ppermute | solution.py:10
  18.7 6.7 %collective-permute-start.1 = (f32[136,128]{0,1:T(8,128)S(1)}, f32[136,128]{0,1:T(8,128)S(1)}, u32[]{:S(2)}, u32[]{:S(2)}) collective-permute-start(f32[136,128]{0,1:T(8,128)S(1)} %fusion.10), channel_id=1, source_target_pairs={{0,2},{1,3},{2,0},{3,1},{4,6},{5,7},{6,4},{7,5},{8,10},{9,11},{10,... | collective-permute-start | bytes 208904 | tf_op jit(solution)/shard_map/ppermute | solution.py:10
  25.4 5.0 %collective-permute-start.2 = (f32[136,128]{0,1:T(8,128)S(1)}, f32[136,128]{0,1:T(8,128)S(1)}, u32[]{:S(2)}, u32[]{:S(2)}) collective-permute-start(f32[136,128]{0,1:T(8,128)S(1)} %add.58), channel_id=1, source_target_pairs={{0,4},{4,0},{8,12},{12,8},{16,20},{20,16},{24,28},{28,24},{1,5},{5... | collective-permute-start | bytes 208904 | tf_op jit(solution)/shard_map/ppermute | solution.py:10
  30.5 5.0 %collective-permute-start.3 = (f32[136,128]{0,1:T(8,128)S(1)}, f32[136,128]{0,1:T(8,128)S(1)}, u32[]{:S(2)}, u32[]{:S(2)}) collective-permute-start(f32[136,128]{0,1:T(8,128)S(1)} %add.59), channel_id=1, source_target_pairs={{0,8},{4,12},{8,0},{12,4},{16,24},{20,28},{24,16},{28,20},{1,9},{5... | collective-permute-start | bytes 208904 | tf_op jit(solution)/shard_map/ppermute | solution.py:10
  35.5 7.7 %collective-permute-start.4 = (f32[136,128]{0,1:T(8,128)S(1)}, f32[136,128]{0,1:T(8,128)S(1)}, u32[]{:S(2)}, u32[]{:S(2)}) collective-permute-start(f32[136,128]{0,1:T(8,128)S(1)} %add.60), channel_id=1, source_target_pairs={{0,16},{4,20},{8,24},{12,28},{16,0},{20,4},{24,8},{28,12},{1,17},{... | collective-permute-start | bytes 208904 | tf_op jit(solution)/shard_map/ppermute | solution.py:10
  43.2 1.4 %collective-permute-start.5 = (f32[136,128]{0,1:T(8,128)S(1)}, f32[136,128]{0,1:T(8,128)S(1)}, u32[]{:S(2)}, u32[]{:S(2)}) collective-permute-start(f32[136,128]{0,1:T(8,128)S(1)} %add.61), channel_id=1, source_target_pairs={{0,1},{1,0},{2,3},{3,2},{4,5},{5,4},{6,7},{7,6},{8,9},{9,8},{10,11... | collective-permute-start | bytes 208904 | tf_op jit(solution)/shard_map/ppermute | solution.py:10

commit v4 on v3

--- a/solution.py
+++ b/solution.py
@@ -3,6 +3,8 @@
 import jax
 import jax.numpy as jnp
 from jax import lax
+from jax.experimental import pallas as pl
+from jax.experimental.pallas import tpu as pltpu
 from jax.sharding import PartitionSpec as P
 
 
@@ -14,19 +16,52 @@
     return jnp.dot(a, b, precision=lax.Precision.HIGHEST)
 
 
-def cholesky_and_inverse(g11, g21, g22):
-    h = g11.shape[0]
-    eye = jnp.eye(h, dtype=g11.dtype)
-    l11 = jnp.linalg.cholesky(g11)
-    i11 = jax.scipy.linalg.solve_triangular(l11, eye, lower=True)
-    l21 = mm(g21, i11.T)
-    l22 = jnp.linalg.cholesky(g22 - mm(l21, l21.T))
-    i22 = jax.scipy.linalg.solve_triangular(l22, eye, lower=True)
-    i21 = -mm(i22, mm(l21, i11))
-    zero = jnp.zeros_like(l11)
-    lower = jnp.block([[l11, zero], [l21, l22]])
-    inverse = jnp.block([[i11, zero], [i21, i22]])
-    return lower, inverse
+def _chol_kernel(g_ref, r_ref, li_ref, a_ref, z_ref):
+    n = g_ref.shape[0]
+    h = n // 2
+    a_ref[...] = g_ref[...]
+    row = lax.broadcasted_iota(jnp.int32, (n, n), 0)
+    col = lax.broadcasted_iota(jnp.int32, (n, n), 1)
+    z_ref[...] = jnp.where(row == col, 1.0, 0.0).astype(jnp.float32)
+    lane = lax.broadcasted_iota(jnp.int32, (1, n), 1)
+
+    def step(j, lo):
+        a_row = a_ref[pl.ds(j, 1), :]
+        d = jnp.sum(jnp.where(lane == j, a_row, 0.0), axis=1, keepdims=True)
+        s = 1.0 / jnp.sqrt(d)
+        r = jnp.where(lane >= j, a_row * s, 0.0)
+        z = z_ref[pl.ds(j, 1), :] * s
+        r_ref[pl.ds(j, 1), :] = r
+        li_ref[pl.ds(j, 1), :] = z
+        c = jnp.broadcast_to(r, (8, n)).T[:, 0:1]
+        if lo:
+            a_ref[...] = a_ref[...] - c * r
+            z_ref[:, :h] = z_ref[:, :h] - c * z[:, :h]
+        else:
+            a_ref[h:, h:] = a_ref[h:, h:] - c[h:] * r[:, h:]
+            z_ref[h:, :] = z_ref[h:, :] - c[h:] * z
+
+    def body_lo(j, carry):
+        step(j, True)
+        return carry
+
+    def body_hi(j, carry):
+        step(j, False)
+        return carry
+
+    lax.fori_loop(0, h, body_lo, 0)
+    lax.fori_loop(h, n, body_hi, 0)
+
+
+def cholesky_kernel(gram):
+    n = gram.shape[0]
+    return pl.pallas_call(
+        _chol_kernel,
+        out_shape=(jax.ShapeDtypeStruct((n, n), jnp.float32),) * 2,
+        in_specs=[pl.BlockSpec(memory_space=pltpu.VMEM)],
+        out_specs=(pl.BlockSpec(memory_space=pltpu.VMEM),) * 2,
+        scratch_shapes=[pltpu.VMEM((n, n), jnp.float32)] * 2,
+    )(gram)
 
 
 def pack(gram):
@@ -86,11 +121,15 @@
         running, running, (((0,), (0,)), ((), ())), precision=lax.Precision.HIGHEST
     )
     gram = all_reduce_symmetric(gram)
-    lower, inverse = cholesky_and_inverse(*gram)
+    g11, g21, g22 = gram
+    full = jnp.concatenate(
+        [jnp.concatenate([g11, g21.T], axis=1), jnp.concatenate([g21, g22], axis=1)], axis=0
+    )
+    upper, inverse = cholesky_kernel(full)
     basis = lax.dot_general(
         features, inverse, (((1,), (1,)), ((), ())), precision=lax.Precision.HIGHEST
     ) * math.sqrt(total_rows)
-    return (lower.T, basis)
+    return (upper, basis)
 
 
 def solution(mesh):

time: 97.1 us -> 122 us (1.26)
  Pallas kernels: 0 us -> 71.9 us
  other arithmetic: 46.1 us -> 0.93 us
    pallas_call x0 -> x1, Pallas kernels: none -> 71.9 us  [cholesky_kernel(): pl.pallas_call(_chol_kernel, out_shape=(jax.ShapeDtypeStruct((n, n), jnp....]
    another operation x10 -> x0, other arithmetic: 45.9 us -> none  [the longest x3 12.4 us: cholesky_and_inverse(): l22 = jnp.linalg.cholesky(g22 - mm(l21, l21.T))]
where the time goes in v4:
time: 122 us
  Pallas kernels  71.9 us (59%)
  matrix products  17.9 us (15%)
  waiting for transfers between devices  16.8 us (14%)
  starting transfers between devices  10.5 us (9%)
  local copies, waits for them, and re-layouts  2.9 us (2%)
    pallas_call x1, Pallas kernels, cholesky_kernel(): pl.pallas_call(_chol_kernel, out_shape=(jax.ShapeDtypeStruct((n, n), jnp....  71.9 us
    ppermute x6, waiting for transfers between devices, partner(): lax.ppermute(array, axis, [(i, i ^ 1 << distance) for i in range(lax.axis...  16.8 us
    ppermute x6, starting transfers between devices, partner(): lax.ppermute(array, axis, [(i, i ^ 1 << distance) for i in range(lax.axis...  10.5 us
    dot_general x1, matrix products, per_device(): jnp.dot(inputs, freqs, precision=lax.Precision.HIGHEST) + phases[None, :]  9.54 us
    dot_general x1, matrix products, per_device(): lax.dot_general(features, inverse, (((1,), (1,)), ((), ())), precision=la...  4.1 us
    dot_general x1, matrix products, per_device(): lax.dot_general(features, features, (((0,), (0,)), ((), ())), precision=l...  3.63 us
  transfers between devices with their start and end apart: 6, of which 6 were waited for; matrix products, arithmetic and copies ran while one was open for 0% of the time, Pallas kernels for 0%

profile of v4, /device:TPU:0, one launch (start us, length us, event | category | flops | bytes accessed | tf_op | source)
XLA Modules:
  0.0 121.8 jit_solution(7024464035698016986)
XLA Ops:
  0.7 0.8 sqrt.3
  1.4 0.3 copy-done
  1.7 9.5 %fusion.2 = f32[2048,256]{1,0:T(8,128)S(1)} fusion(f32[2048,64]{0,1:T(8,128)S(1)} %copy-done, f32[64,256]{1,0:T(8,128)} %param.7, f32[256]{0:T(256)} %param.8, f32[2048]{0:T(1024)S(1)} %sqrt.3), kind=kOutput, calls=%fused_computation.5 | convolution fusion | flops 404226048 | bytes 2696192 | tf_op jit(solution)/shard_map/dot_general | solution.py:113
  11.3 3.6 %fusion.10 = f32[256,256]{0,1:T(8,128)S(1)} fusion(f32[2048,256]{1,0:T(8,128)S(1)} %fusion.2), kind=kOutput, calls=%fused_computation.28 | convolution fusion | flops 1610612736 | bytes 2359296 | tf_op jit(solution)/shard_map/dot_general | solution.py:115
  15.0 0.6 convolution_add_fusion.1
  15.6 1.3 %gather_fusion = f32[128]{0:T(128)S(1)} fusion(f32[128,128]{0,1:T(8,128)S(1)} %get-tuple-element.8, s32[128]{0:T(128)S(1)} %or_bitcast_fusion), kind=kCustom, calls=%fused_computation | custom fusion | bytes 2048 | tf_op jit(solution)/shard_map/jit(diagonal)/cond/branch_0_fun/gather | solution.py:72
  16.9 0.1 copy.17
  17.1 0.6 collective-permute-start
  17.7 1.0 collective-permute-done
  18.7 2.9 %collective-permute-start.1 = (f32[136,128]{0,1:T(8,128)S(1)}, f32[136,128]{0,1:T(8,128)S(1)}, u32[]{:S(2)}, u32[]{:S(2)}) collective-permute-start(f32[136,128]{0,1:T(8,128)S(1)} %fusion.5), channel_id=1, source_target_pairs={{0,2},{1,3},{2,0},{3,1},{4,6},{5,7},{6,4},{7,5},{8,10},{9,11},{10,... | collective-permute-start | bytes 208904 | tf_op jit(solution)/shard_map/ppermute | solution.py:12
  21.6 3.8 %collective-permute-done.1 = f32[136,128]{0,1:T(8,128)S(1)} collective-permute-done((f32[136,128]{0,1:T(8,128)S(1)}, f32[136,128]{0,1:T(8,128)S(1)}, u32[]{:S(2)}, u32[]{:S(2)}) %collective-permute-start.1) | collective-permute-done | bytes 69664 | tf_op jit(solution)/shard_map/ppermute | solution.py:12
  25.4 1.8 %collective-permute-start.2 = (f32[136,128]{0,1:T(8,128)S(1)}, f32[136,128]{0,1:T(8,128)S(1)}, u32[]{:S(2)}, u32[]{:S(2)}) collective-permute-start(f32[136,128]{0,1:T(8,128)S(1)} %add.45), channel_id=1, source_target_pairs={{0,4},{4,0},{8,12},{12,8},{16,20},{20,16},{24,28},{28,24},{1,5},{5... | collective-permute-start | bytes 208904 | tf_op jit(solution)/shard_map/ppermute | solution.py:12
  27.2 3.3 %collective-permute-done.2 = f32[136,128]{0,1:T(8,128)S(1)} collective-permute-done((f32[136,128]{0,1:T(8,128)S(1)}, f32[136,128]{0,1:T(8,128)S(1)}, u32[]{:S(2)}, u32[]{:S(2)}) %collective-permute-start.2) | collective-permute-done | bytes 69664 | tf_op jit(solution)/shard_map/ppermute | solution.py:12
  30.5 1.9 %collective-permute-start.3 = (f32[136,128]{0,1:T(8,128)S(1)}, f32[136,128]{0,1:T(8,128)S(1)}, u32[]{:S(2)}, u32[]{:S(2)}) collective-permute-start(f32[136,128]{0,1:T(8,128)S(1)} %add.46), channel_id=1, source_target_pairs={{0,8},{4,12},{8,0},{12,4},{16,24},{20,28},{24,16},{28,20},{1,9},{5... | collective-permute-start | bytes 208904 | tf_op jit(solution)/shard_map/ppermute | solution.py:12
  32.4 3.2 %collective-permute-done.3 = f32[136,128]{0,1:T(8,128)S(1)} collective-permute-done((f32[136,128]{0,1:T(8,128)S(1)}, f32[136,128]{0,1:T(8,128)S(1)}, u32[]{:S(2)}, u32[]{:S(2)}) %collective-permute-start.3) | collective-permute-done | bytes 69664 | tf_op jit(solution)/shard_map/ppermute | solution.py:12
  35.5 3.3 %collective-permute-start.4 = (f32[136,128]{0,1:T(8,128)S(1)}, f32[136,128]{0,1:T(8,128)S(1)}, u32[]{:S(2)}, u32[]{:S(2)}) collective-permute-start(f32[136,128]{0,1:T(8,128)S(1)} %add.47), channel_id=1, source_target_pairs={{0,16},{4,20},{8,24},{12,28},{16,0},{20,4},{24,8},{28,12},{1,17},{... | collective-permute-start | bytes 208904 | tf_op jit(solution)/shard_map/ppermute | solution.py:12
  38.9 4.4 %collective-permute-done.4 = f32[136,128]{0,1:T(8,128)S(1)} collective-permute-done((f32[136,128]{0,1:T(8,128)S(1)}, f32[136,128]{0,1:T(8,128)S(1)}, u32[]{:S(2)}, u32[]{:S(2)}) %collective-permute-start.4) | collective-permute-done | bytes 69664 | tf_op jit(solution)/shard_map/ppermute | solution.py:12
  43.3 0.1 copy.18
  43.5 1.2 collective-permute-done.5
  44.7 0.1 slice_reduce_fusion
  44.8 0.1 copy.19
  45.0 0.7 maximum_maximum_fusion.g_ref
  45.8 71.9 %shard_map.77 = (f32[256,256]{1,0:T(8,128)}, f32[256,256]{1,0:T(8,128)}) custom-call(f32[256,256]{1,0:T(8,128)} %maximum_maximum_fusion.g_ref), custom_call_target="tpu_custom_call" | custom-call | tf_op jit(solution)/shard_map/pallas_call | solution.py:58
  117.7 4.1 %convolution_multiply_fusion = f32[2048,256]{1,0:T(8,128)} fusion(f32[2048,256]{1,0:T(8,128)S(1)} %fusion.2, f32[256,256]{1,0:T(8,128)} %get-tuple-element.5), kind=kOutput, calls=%fused_computation.1 | convolution fusion | flops 1611137024 | bytes 4456448 | tf_op jit(solution)/shard_map/dot_general | solution.py:129
  (22 shorter events, 0.5 us)
Async XLA Ops:
  0.6 1.1 copy-start
  11.2 3.7 %copy-start.2 = (s32[32]{0:T(128)S(1)}, s32[32]{0:T(128)}, u32[]{:S(2)}) copy-start(s32[32]{0:T(128)} %param.11) | copy-start | bytes 388
  11.2 3.7 %copy-start.1 = (f32[1,256,256]{2,1,0:T(8,128)S(1)}, f32[1,256,256]{2,1,0:T(8,128)}, u32[]{:S(2)}) copy-start(f32[1,256,256]{2,1,0:T(8,128)} %param.10) | copy-start | bytes 786436
  17.1 1.5 %collective-permute-start = (f32[136,128]{0,1:T(8,128)S(1)}, f32[136,128]{0,1:T(8,128)S(1)}, u32[]{:S(2)}, u32[]{:S(2)}) collective-permute-start(f32[136,128]{0,1:T(8,128)S(1)} %pad_select_fusion), channel_id=1, source_target_pairs={{0,1},{1,0},{2,3},{3,2},{4,5},{5,4},{6,7},{7,6},{8,9},{9,8},{10,11... | collective-permute-start | bytes 208904 | tf_op jit(solution)/shard_map/ppermute | solution.py:12
  18.7 6.7 %collective-permute-start.1 = (f32[136,128]{0,1:T(8,128)S(1)}, f32[136,128]{0,1:T(8,128)S(1)}, u32[]{:S(2)}, u32[]{:S(2)}) collective-permute-start(f32[136,128]{0,1:T(8,128)S(1)} %fusion.5), channel_id=1, source_target_pairs={{0,2},{1,3},{2,0},{3,1},{4,6},{5,7},{6,4},{7,5},{8,10},{9,11},{10,... | collective-permute-start | bytes 208904 | tf_op jit(solution)/shard_map/ppermute | solution.py:12
  25.4 5.0 %collective-permute-start.2 = (f32[136,128]{0,1:T(8,128)S(1)}, f32[136,128]{0,1:T(8,128)S(1)}, u32[]{:S(2)}, u32[]{:S(2)}) collective-permute-start(f32[136,128]{0,1:T(8,128)S(1)} %add.45), channel_id=1, source_target_pairs={{0,4},{4,0},{8,12},{12,8},{16,20},{20,16},{24,28},{28,24},{1,5},{5... | collective-permute-start | bytes 208904 | tf_op jit(solution)/shard_map/ppermute | solution.py:12
  30.5 5.0 %collective-permute-start.3 = (f32[136,128]{0,1:T(8,128)S(1)}, f32[136,128]{0,1:T(8,128)S(1)}, u32[]{:S(2)}, u32[]{:S(2)}) collective-permute-start(f32[136,128]{0,1:T(8,128)S(1)} %add.46), channel_id=1, source_target_pairs={{0,8},{4,12},{8,0},{12,4},{16,24},{20,28},{24,16},{28,20},{1,9},{5... | collective-permute-start | bytes 208904 | tf_op jit(solution)/shard_map/ppermute | solution.py:12
  35.5 7.7 %collective-permute-start.4 = (f32[136,128]{0,1:T(8,128)S(1)}, f32[136,128]{0,1:T(8,128)S(1)}, u32[]{:S(2)}, u32[]{:S(2)}) collective-permute-start(f32[136,128]{0,1:T(8,128)S(1)} %add.47), channel_id=1, source_target_pairs={{0,16},{4,20},{8,24},{12,28},{16,0},{20,4},{24,8},{28,12},{1,17},{... | collective-permute-start | bytes 208904 | tf_op jit(solution)/shard_map/ppermute | solution.py:12
  43.2 1.4 %collective-permute-start.5 = (f32[136,128]{0,1:T(8,128)S(1)}, f32[136,128]{0,1:T(8,128)S(1)}, u32[]{:S(2)}, u32[]{:S(2)}) collective-permute-start(f32[136,128]{0,1:T(8,128)S(1)} %add.48), channel_id=1, source_target_pairs={{0,1},{1,0},{2,3},{3,2},{4,5},{5,4},{6,7},{7,6},{8,9},{9,8},{10,11... | collective-permute-start | bytes 208904 | tf_op jit(solution)/shard_map/ppermute | solution.py:12

commit v5 on v3

--- a/solution.py
+++ b/solution.py
@@ -72,11 +72,27 @@
     return unpack(first, second)
 
 
+def bounded_cos(x):
+    k = jnp.round(x * (1.0 / math.pi))
+    r = x - k * 3.140625
+    r = r - k * 0.0009675025939941406
+    r = r - k * 1.5099580252808664e-07
+    r2 = r * r
+    poly = -1.0 / 479001600.0 * r2 + 1.0 / 3628800.0
+    poly = poly * r2 - 1.0 / 40320.0
+    poly = poly * r2 + 1.0 / 720.0
+    poly = poly * r2 - 1.0 / 24.0
+    poly = poly * r2 + 0.5
+    value = 1.0 - poly * r2
+    half = k * 0.5
+    return jnp.where(jnp.floor(half) == half, value, -value)
+
+
 def per_device(inputs, freqs, phases, sample_weight, stored, root):
     total_rows = inputs.shape[0] * lax.axis_size("grp") * lax.axis_size("leaf")
     norm_scale = 1.0 / math.sqrt(total_rows)
     proj = jnp.dot(inputs, freqs, precision=lax.Precision.HIGHEST) + phases[None, :]
-    features = jnp.sqrt(sample_weight)[:, None] * jnp.cos(proj) * norm_scale
+    features = jnp.sqrt(sample_weight)[:, None] * bounded_cos(proj) * norm_scale
     gram = lax.dot_general(
         features, features, (((0,), (0,)), ((), ())), precision=lax.Precision.HIGHEST
     )

time: 97.1 us -> 92.1 us (0.949)
  matrix products: 18.5 us -> 13.4 us
    dot_general x1, matrix products: 9.54 us -> 4.58 us  [per_device(): jnp.dot(inputs, freqs, precision=lax.Precision.HIGHEST) + phases[None, :]]
where the time goes in v5:
time: 92.1 us; the launch traced here: 91.9 us
  other arithmetic  46.1 us (50%)
  waiting for transfers between devices  16.9 us (18%)
  matrix products  13.4 us (15%)
  starting transfers between devices  10.5 us (11%)
  local copies, waits for them, and re-layouts  4.07 us (4%)
  between operations  0.98 us (1%)
    ppermute x6, waiting for transfers between devices, partner(): lax.ppermute(array, axis, [(i, i ^ 1 << distance) for i in range(lax.axis...  16.9 us
    another operation x3, other arithmetic, cholesky_and_inverse(): l22 = jnp.linalg.cholesky(g22 - mm(l21, l21.T))  12.4 us
    another operation x3, other arithmetic, cholesky_and_inverse(): l11 = jnp.linalg.cholesky(g11)  12.4 us
    another operation x2, other arithmetic, cholesky_and_inverse(): i22 = jax.scipy.linalg.solve_triangular(l22, eye, lower=True)  10.6 us
    ppermute x6, starting transfers between devices, partner(): lax.ppermute(array, axis, [(i, i ^ 1 << distance) for i in range(lax.axis...  10.5 us
    another operation x2, other arithmetic, cholesky_and_inverse(): i11 = jax.scipy.linalg.solve_triangular(l11, eye, lower=True)  10.5 us
    dot_general x1, matrix products, per_device(): jnp.dot(inputs, freqs, precision=lax.Precision.HIGHEST) + phases[None, :]  4.58 us
    dot_general x1, matrix products, per_device(): lax.dot_general(features, features, (((0,), (0,)), ((), ())), precision=l...  3.45 us
  transfers between devices with their start and end apart: 6, of which 6 were waited for; matrix products, arithmetic and copies ran while one was open for 0% of the time, Pallas kernels for 0%

profile of v5, /device:TPU:0, one launch (start us, length us, event | category | flops | bytes accessed | tf_op | source)
XLA Modules:
  0.0 91.9 jit_solution(10116650731250822874)
XLA Ops:
  0.7 0.8 sqrt.3
  1.7 4.6 %fusion.1 = f32[2048,256]{1,0:T(8,128)S(1)} fusion(f32[2048,64]{0,1:T(8,128)S(1)} %copy-done, f32[64,256]{1,0:T(8,128)} %param.10, f32[256]{0:T(256)} %param.11, f32[2048]{0:T(1024)S(1)} %sqrt.3), kind=kOutput, calls=%fused_computation.6 | convolution fusion | flops 417857536 | bytes 2696192 | tf_op jit(solution)/shard_map/dot_general | solution.py:94
  6.3 3.5 %fusion.31 = f32[256,256]{0,1:T(8,128)S(1)} fusion(f32[2048,256]{1,0:T(8,128)S(1)} %fusion.1), kind=kOutput, calls=%fused_computation.66 | convolution fusion | flops 1610612736 | bytes 2359296 | tf_op jit(solution)/shard_map/dot_general | solution.py:96
  10.5 1.5 %gather_fusion = f32[128]{0:T(128)S(1)} fusion(f32[128,128]{0,1:T(8,128)S(1)} %get-tuple-element.14, s32[128]{0:T(128)S(1)} %or_bitcast_fusion), kind=kCustom, calls=%fused_computation | custom fusion | bytes 2048 | tf_op jit(solution)/shard_map/jit(diagonal)/cond/branch_0_fun/gather | solution.py:37
  12.7 1.0 %collective-permute-done = f32[136,128]{0,1:T(8,128)S(1)} collective-permute-done((f32[136,128]{0,1:T(8,128)S(1)}, f32[136,128]{0,1:T(8,128)S(1)}, u32[]{:S(2)}, u32[]{:S(2)}) %collective-permute-start) | collective-permute-done | bytes 69664 | tf_op jit(solution)/shard_map/ppermute | solution.py:10
  13.7 2.9 %collective-permute-start.1 = (f32[136,128]{0,1:T(8,128)S(1)}, f32[136,128]{0,1:T(8,128)S(1)}, u32[]{:S(2)}, u32[]{:S(2)}) collective-permute-start(f32[136,128]{0,1:T(8,128)S(1)} %fusion.9), channel_id=1, source_target_pairs={{0,2},{1,3},{2,0},{3,1},{4,6},{5,7},{6,4},{7,5},{8,10},{9,11},{10,... | collective-permute-start | bytes 208904 | tf_op jit(solution)/shard_map/ppermute | solution.py:10
  16.7 3.8 %collective-permute-done.1 = f32[136,128]{0,1:T(8,128)S(1)} collective-permute-done((f32[136,128]{0,1:T(8,128)S(1)}, f32[136,128]{0,1:T(8,128)S(1)}, u32[]{:S(2)}, u32[]{:S(2)}) %collective-permute-start.1) | collective-permute-done | bytes 69664 | tf_op jit(solution)/shard_map/ppermute | solution.py:10
  20.5 1.8 %collective-permute-start.2 = (f32[136,128]{0,1:T(8,128)S(1)}, f32[136,128]{0,1:T(8,128)S(1)}, u32[]{:S(2)}, u32[]{:S(2)}) collective-permute-start(f32[136,128]{0,1:T(8,128)S(1)} %add.80), channel_id=1, source_target_pairs={{0,4},{4,0},{8,12},{12,8},{16,20},{20,16},{24,28},{28,24},{1,5},{5... | collective-permute-start | bytes 208904 | tf_op jit(solution)/shard_map/ppermute | solution.py:10
  22.3 3.3 %collective-permute-done.2 = f32[136,128]{0,1:T(8,128)S(1)} collective-permute-done((f32[136,128]{0,1:T(8,128)S(1)}, f32[136,128]{0,1:T(8,128)S(1)}, u32[]{:S(2)}, u32[]{:S(2)}) %collective-permute-start.2) | collective-permute-done | bytes 69664 | tf_op jit(solution)/shard_map/ppermute | solution.py:10
  25.5 1.9 %collective-permute-start.3 = (f32[136,128]{0,1:T(8,128)S(1)}, f32[136,128]{0,1:T(8,128)S(1)}, u32[]{:S(2)}, u32[]{:S(2)}) collective-permute-start(f32[136,128]{0,1:T(8,128)S(1)} %add.81), channel_id=1, source_target_pairs={{0,8},{4,12},{8,0},{12,4},{16,24},{20,28},{24,16},{28,20},{1,9},{5... | collective-permute-start | bytes 208904 | tf_op jit(solution)/shard_map/ppermute | solution.py:10
  27.4 3.2 %collective-permute-done.3 = f32[136,128]{0,1:T(8,128)S(1)} collective-permute-done((f32[136,128]{0,1:T(8,128)S(1)}, f32[136,128]{0,1:T(8,128)S(1)}, u32[]{:S(2)}, u32[]{:S(2)}) %collective-permute-start.3) | collective-permute-done | bytes 69664 | tf_op jit(solution)/shard_map/ppermute | solution.py:10
  30.6 3.3 %collective-permute-start.4 = (f32[136,128]{0,1:T(8,128)S(1)}, f32[136,128]{0,1:T(8,128)S(1)}, u32[]{:S(2)}, u32[]{:S(2)}) collective-permute-start(f32[136,128]{0,1:T(8,128)S(1)} %add.82), channel_id=1, source_target_pairs={{0,16},{4,20},{8,24},{12,28},{16,0},{20,4},{24,8},{28,12},{1,17},{... | collective-permute-start | bytes 208904 | tf_op jit(solution)/shard_map/ppermute | solution.py:10
  33.9 4.4 %collective-permute-done.4 = f32[136,128]{0,1:T(8,128)S(1)} collective-permute-done((f32[136,128]{0,1:T(8,128)S(1)}, f32[136,128]{0,1:T(8,128)S(1)}, u32[]{:S(2)}, u32[]{:S(2)}) %collective-permute-start.4) | collective-permute-done | bytes 69664 | tf_op jit(solution)/shard_map/ppermute | solution.py:10
  38.4 1.3 %collective-permute-done.5 = f32[136,128]{0,1:T(8,128)S(1)} collective-permute-done((f32[136,128]{0,1:T(8,128)S(1)}, f32[136,128]{0,1:T(8,128)S(1)}, u32[]{:S(2)}, u32[]{:S(2)}) %collective-permute-start.5) | collective-permute-done | bytes 69664 | tf_op jit(solution)/shard_map/ppermute | solution.py:10
  40.1 11.7 %cholesky.44 = f32[128,128]{1,0:T(8,128)S(1)} custom-call(f32[128,128]{1,0:T(8,128)S(1)} %fusion.23), custom_call_target="Cholesky" | custom-call | tf_op jit(solution)/shard_map/jit(cholesky)/cholesky | solution.py:20
  51.8 0.6 compare_reduce_fusion.1
  52.5 0.7 select_bitcast_fusion.1
  53.1 9.8 %custom-call.8 = f32[1,128,128]{1,2,0:T(8,128)S(1)} custom-call(f32[1,128,128]{2,1,0:T(8,128)S(1)} %get-tuple-element.10), custom_call_target="InvertDiagBlocksLowerTriangular" | custom-call | tf_op jit(solution)/shard_map/jit(_solve_triangular)/triangular_solve | solution.py:21
  64.2 11.7 %cholesky.55 = f32[128,128]{1,0:T(8,128)S(1)} custom-call(f32[128,128]{1,0:T(8,128)S(1)} %fusion.21), custom_call_target="Cholesky" | custom-call | tf_op jit(solution)/shard_map/jit(cholesky)/cholesky | solution.py:23
  76.0 0.6 compare_reduce_fusion
  76.6 0.7 select_bitcast_fusion
  77.3 10.0 %custom-call.9 = f32[1,128,128]{1,2,0:T(8,128)S(1)} custom-call(f32[1,128,128]{2,1,0:T(8,128)S(1)} %get-tuple-element.8), custom_call_target="InvertDiagBlocksLowerTriangular" | custom-call | tf_op jit(solution)/shard_map/jit(_solve_triangular)/triangular_solve | solution.py:24
  87.9 0.8 copy.27
  88.8 3.2 %convolution_multiply_fusion = f32[2048,256]{1,0:T(8,128)} fusion(f32[2048,256]{1,0:T(8,128)S(1)} %fusion.1, f32[128,128]{1,0:T(8,128)S(1)} %fusion.16, f32[128,128]{1,0:T(8,128)S(1)} %copy.26, f32[128,128]{1,0:T(8,128)S(1)} %convolution_negate_fusion), kind=kOutput, calls=%fused_computation.3 | convolution fusion | flops 1611399168 | bytes 4390912 | tf_op jit(solution)/shard_map/dot_general | solution.py:106
  (40 shorter events, 4.1 us)
Async XLA Ops:
  0.6 1.1 %copy-start = (f32[2048,64]{0,1:T(8,128)S(1)}, f32[2048,64]{0,1:T(8,128)}, u32[]{:S(2)}) copy-start(f32[2048,64]{0,1:T(8,128)} %param.9) | copy-start | bytes 1572868
  6.3 3.5 %copy-start.2 = (s32[32]{0:T(128)S(1)}, s32[32]{0:T(128)}, u32[]{:S(2)}) copy-start(s32[32]{0:T(128)} %param.14) | copy-start | bytes 388
  6.3 3.5 %copy-start.1 = (f32[1,256,256]{2,1,0:T(8,128)S(1)}, f32[1,256,256]{2,1,0:T(8,128)}, u32[]{:S(2)}) copy-start(f32[1,256,256]{2,1,0:T(8,128)} %param.13) | copy-start | bytes 786436
  12.1 1.5 %collective-permute-start = (f32[136,128]{0,1:T(8,128)S(1)}, f32[136,128]{0,1:T(8,128)S(1)}, u32[]{:S(2)}, u32[]{:S(2)}) collective-permute-start(f32[136,128]{0,1:T(8,128)S(1)} %pad_select_fusion), channel_id=1, source_target_pairs={{0,1},{1,0},{2,3},{3,2},{4,5},{5,4},{6,7},{7,6},{8,9},{9,8},{10,11... | collective-permute-start | bytes 208904 | tf_op jit(solution)/shard_map/ppermute | solution.py:10
  13.7 6.7 %collective-permute-start.1 = (f32[136,128]{0,1:T(8,128)S(1)}, f32[136,128]{0,1:T(8,128)S(1)}, u32[]{:S(2)}, u32[]{:S(2)}) collective-permute-start(f32[136,128]{0,1:T(8,128)S(1)} %fusion.9), channel_id=1, source_target_pairs={{0,2},{1,3},{2,0},{3,1},{4,6},{5,7},{6,4},{7,5},{8,10},{9,11},{10,... | collective-permute-start | bytes 208904 | tf_op jit(solution)/shard_map/ppermute | solution.py:10
  20.5 5.0 %collective-permute-start.2 = (f32[136,128]{0,1:T(8,128)S(1)}, f32[136,128]{0,1:T(8,128)S(1)}, u32[]{:S(2)}, u32[]{:S(2)}) collective-permute-start(f32[136,128]{0,1:T(8,128)S(1)} %add.80), channel_id=1, source_target_pairs={{0,4},{4,0},{8,12},{12,8},{16,20},{20,16},{24,28},{28,24},{1,5},{5... | collective-permute-start | bytes 208904 | tf_op jit(solution)/shard_map/ppermute | solution.py:10
  25.5 5.0 %collective-permute-start.3 = (f32[136,128]{0,1:T(8,128)S(1)}, f32[136,128]{0,1:T(8,128)S(1)}, u32[]{:S(2)}, u32[]{:S(2)}) collective-permute-start(f32[136,128]{0,1:T(8,128)S(1)} %add.81), channel_id=1, source_target_pairs={{0,8},{4,12},{8,0},{12,4},{16,24},{20,28},{24,16},{28,20},{1,9},{5... | collective-permute-start | bytes 208904 | tf_op jit(solution)/shard_map/ppermute | solution.py:10
  30.6 7.7 %collective-permute-start.4 = (f32[136,128]{0,1:T(8,128)S(1)}, f32[136,128]{0,1:T(8,128)S(1)}, u32[]{:S(2)}, u32[]{:S(2)}) collective-permute-start(f32[136,128]{0,1:T(8,128)S(1)} %add.82), channel_id=1, source_target_pairs={{0,16},{4,20},{8,24},{12,28},{16,0},{20,4},{24,8},{28,12},{1,17},{... | collective-permute-start | bytes 208904 | tf_op jit(solution)/shard_map/ppermute | solution.py:10
  38.3 1.4 %collective-permute-start.5 = (f32[136,128]{0,1:T(8,128)S(1)}, f32[136,128]{0,1:T(8,128)S(1)}, u32[]{:S(2)}, u32[]{:S(2)}) collective-permute-start(f32[136,128]{0,1:T(8,128)S(1)} %add.83), channel_id=1, source_target_pairs={{0,1},{1,0},{2,3},{3,2},{4,5},{5,4},{6,7},{7,6},{8,9},{9,8},{10,11... | collective-permute-start | bytes 208904 | tf_op jit(solution)/shard_map/ppermute | solution.py:10

commit v6 on v5

--- a/solution.py
+++ b/solution.py
@@ -34,7 +34,7 @@
     row = lax.broadcasted_iota(jnp.int32, (h, h), 0)
     col = lax.broadcasted_iota(jnp.int32, (h, h), 1)
     tri = jnp.where(row <= col, gram[:h, :h], gram[h:, h:])
-    diag = jnp.diagonal(gram[h:, h:])
+    diag = jnp.sum(jnp.where(row == col, gram[h:, h:], 0.0), axis=0)
     pad = jnp.zeros((7, h), gram.dtype)
     first = jnp.concatenate([tri, diag[None, :], pad], axis=0)
     second = jnp.concatenate([gram[h:, :h], jnp.zeros((8, h), gram.dtype)], axis=0)
@@ -53,20 +53,34 @@
     return g11, g21, g22
 
 
+def flip(array, mask):
+    axes = ("grp", "leaf")
+    count = lax.axis_size("grp") * lax.axis_size("leaf")
+    return lax.ppermute(array, axes, [(i, i ^ mask) for i in range(count)])
+
+
 def all_reduce_symmetric(gram):
-    stages = [("leaf", b) for b in range(lax.axis_size("leaf").bit_length() - 1)]
-    stages += [("grp", b) for b in range(lax.axis_size("grp").bit_length() - 1)]
+    bits = (lax.axis_size("grp") * lax.axis_size("leaf")).bit_length() - 1
     first, second = pack(gram)
-    if not stages:
+    if bits == 0:
         return unpack(first, second)
-    axis0, bit0 = stages[0]
-    low = (lax.axis_index(axis0) >> bit0) % 2 == 0
+    me = lax.axis_index("grp") * lax.axis_size("leaf") + lax.axis_index("leaf")
+    low = me % 2 == 0
     keep = jnp.where(low, first, second)
     send = jnp.where(low, second, first)
-    keep = keep + partner(send, axis0, bit0)
-    for axis, bit in stages[1:]:
-        keep = keep + partner(keep, axis, bit)
-    other = partner(keep, axis0, bit0)
+    keep = keep + flip(send, 1)
+    rest = list(range(1, bits))
+    while rest:
+        if len(rest) == 1:
+            keep = keep + flip(keep, 1 << rest[0])
+            rest = []
+        else:
+            ma, mb = 1 << rest[0], 1 << rest[1]
+            near = keep + flip(keep, ma)
+            far = flip(keep, mb) + flip(keep, ma | mb)
+            keep = near + far
+            rest = rest[2:]
+    other = flip(keep, 1)
     first = jnp.where(low, keep, other)
     second = jnp.where(low, other, keep)
     return unpack(first, second)

time: 92.1 us -> 91.9 us (level)
  local copies, waits for them, and re-layouts: 4.07 us -> 2.3 us
  waiting for transfers between devices: 16.9 us -> 18.6 us
    ppermute x6 -> x8, waiting for transfers between devices: 16.9 us -> 18.6 us  [flip(): return lax.ppermute(array, axes, [(i, i ^ mask) for i in range(count)])]
    gather x1 -> x0, local copies, waits for them, and re-layouts: 1.46 us -> none  [pack(): diag = jnp.diagonal(gram[h:, h:])]
    ppermute x6 -> x8, starting transfers between devices: 10.5 us -> 9.58 us  [flip(): return lax.ppermute(array, axes, [(i, i ^ mask) for i in range(count)])]
  transfers between devices with their start and end apart: 6 -> 8, of which waited for: 6 -> 6; matrix products, arithmetic and copies ran while one was open for 0% -> 0% of each run, Pallas kernels for 0% -> 0%
where the time goes in v6:
time: 91.9 us; the launch traced here: 91.6 us
  other arithmetic  46.2 us (50%)
  waiting for transfers between devices  18.6 us (20%)
  matrix products  13.4 us (15%)
  starting transfers between devices  9.58 us (10%)
  local copies, waits for them, and re-layouts  2.3 us (3%)
  between operations  1.61 us (2%)
    ppermute x8, waiting for transfers between devices, flip(): return lax.ppermute(array, axes, [(i, i ^ mask) for i in range(count)])  18.6 us
    another operation x3, other arithmetic, cholesky_and_inverse(): l11 = jnp.linalg.cholesky(g11)  12.5 us
    another operation x3, other arithmetic, cholesky_and_inverse(): l22 = jnp.linalg.cholesky(g22 - mm(l21, l21.T))  12.4 us
    another operation x2, other arithmetic, cholesky_and_inverse(): i11 = jax.scipy.linalg.solve_triangular(l11, eye, lower=True)  10.5 us
    another operation x2, other arithmetic, cholesky_and_inverse(): i22 = jax.scipy.linalg.solve_triangular(l22, eye, lower=True)  10.5 us
    ppermute x8, starting transfers between devices, flip(): return lax.ppermute(array, axes, [(i, i ^ mask) for i in range(count)])  9.58 us
    dot_general x1, matrix products, per_device(): jnp.dot(inputs, freqs, precision=lax.Precision.HIGHEST) + phases[None, :]  4.59 us
    dot_general x1, matrix products, per_device(): lax.dot_general(features, features, (((0,), (0,)), ((), ())), precision=l...  3.45 us
  transfers between devices with their start and end apart: 8, of which 6 were waited for; matrix products, arithmetic and copies ran while one was open for 0% of the time, Pallas kernels for 0%

profile of v6, /device:TPU:0, one launch (start us, length us, event | category | flops | bytes accessed | tf_op | source)
XLA Modules:
  0.0 91.6 jit_solution(8242554988407242513)
XLA Ops:
  1.4 0.7 sqrt.3
  2.1 4.6 %fusion.1 = f32[2048,256]{1,0:T(8,128)S(1)} fusion(f32[2048,64]{0,1:T(8,128)S(1)} %copy-done, f32[64,256]{1,0:T(8,128)} %param.10, f32[256]{0:T(256)} %param.11, f32[2048]{0:T(1024)S(1)} %sqrt.3), kind=kOutput, calls=%fused_computation.5 | convolution fusion | flops 417857536 | bytes 2696192 | tf_op jit(solution)/shard_map/dot_general | solution.py:108
  6.7 3.5 %fusion.31 = f32[256,256]{0,1:T(8,128)S(1)} fusion(f32[2048,256]{1,0:T(8,128)S(1)} %fusion.1), kind=kOutput, calls=%fused_computation.67 | convolution fusion | flops 1610612736 | bytes 2359296 | tf_op jit(solution)/shard_map/dot_general | solution.py:110
  10.1 0.6 convolution_add_fusion.1
  11.1 0.6 collective-permute-start
  11.7 1.0 %collective-permute-done = f32[136,128]{0,1:T(8,128)S(1)} collective-permute-done((f32[136,128]{0,1:T(8,128)S(1)}, f32[136,128]{0,1:T(8,128)S(1)}, u32[]{:S(2)}, u32[]{:S(2)}) %collective-permute-start) | collective-permute-done | bytes 69664 | tf_op jit(solution)/shard_map/ppermute | solution.py:59
  12.7 3.9 %collective-permute-start.3 = (f32[136,128]{0,1:T(8,128)S(1)}, f32[136,128]{0,1:T(8,128)S(1)}, u32[]{:S(2)}, u32[]{:S(2)}) collective-permute-start(f32[136,128]{0,1:T(8,128)S(1)} %fusion.9), channel_id=1, source_target_pairs={{0,6},{1,7},{2,4},{3,5},{4,2},{5,3},{6,0},{7,1},{8,14},{9,15},{10,... | collective-permute-start | bytes 208904 | tf_op jit(solution)/shard_map/ppermute | solution.py:59
  17.2 3.7 %collective-permute-done.3 = f32[136,128]{0,1:T(8,128)S(1)} collective-permute-done((f32[136,128]{0,1:T(8,128)S(1)}, f32[136,128]{0,1:T(8,128)S(1)}, u32[]{:S(2)}, u32[]{:S(2)}) %collective-permute-start.3) | collective-permute-done | bytes 69664 | tf_op jit(solution)/shard_map/ppermute | solution.py:59
  20.9 2.5 %collective-permute-done.2 = f32[136,128]{0,1:T(8,128)S(1)} collective-permute-done((f32[136,128]{0,1:T(8,128)S(1)}, f32[136,128]{0,1:T(8,128)S(1)}, u32[]{:S(2)}, u32[]{:S(2)}) %collective-permute-start.2) | collective-permute-done | bytes 69664 | tf_op jit(solution)/shard_map/ppermute | solution.py:59
  23.4 3.7 %collective-permute-start.6 = (f32[136,128]{0,1:T(8,128)S(1)}, f32[136,128]{0,1:T(8,128)S(1)}, u32[]{:S(2)}, u32[]{:S(2)}) collective-permute-start(f32[136,128]{0,1:T(8,128)S(1)} %add_add_fusion.1), channel_id=1, source_target_pairs={{0,24},{1,25},{2,26},{3,27},{4,28},{5,29},{6,30},{7,31},{8,16},{9,... | collective-permute-start | bytes 208904 | tf_op jit(solution)/shard_map/ppermute | solution.py:59
  27.1 0.8 collective-permute-start.4
  27.9 3.8 %collective-permute-done.6 = f32[136,128]{0,1:T(8,128)S(1)} collective-permute-done((f32[136,128]{0,1:T(8,128)S(1)}, f32[136,128]{0,1:T(8,128)S(1)}, u32[]{:S(2)}, u32[]{:S(2)}) %collective-permute-start.6) | collective-permute-done | bytes 69664 | tf_op jit(solution)/shard_map/ppermute | solution.py:59
  31.7 6.2 %collective-permute-done.5 = f32[136,128]{0,1:T(8,128)S(1)} collective-permute-done((f32[136,128]{0,1:T(8,128)S(1)}, f32[136,128]{0,1:T(8,128)S(1)}, u32[]{:S(2)}, u32[]{:S(2)}) %collective-permute-start.5) | collective-permute-done | bytes 69664 | tf_op jit(solution)/shard_map/ppermute | solution.py:59
  38.1 1.3 %collective-permute-done.7 = f32[136,128]{0,1:T(8,128)S(1)} collective-permute-done((f32[136,128]{0,1:T(8,128)S(1)}, f32[136,128]{0,1:T(8,128)S(1)}, u32[]{:S(2)}, u32[]{:S(2)}) %collective-permute-start.7) | collective-permute-done | bytes 69664 | tf_op jit(solution)/shard_map/ppermute | solution.py:59
  39.8 11.9 %cholesky.44 = f32[128,128]{1,0:T(8,128)S(1)} custom-call(f32[128,128]{1,0:T(8,128)S(1)} %fusion.23), custom_call_target="Cholesky" | custom-call | tf_op jit(solution)/shard_map/jit(cholesky)/cholesky | solution.py:20
  51.7 0.6 compare_reduce_fusion.1
  52.3 0.7 select_bitcast_fusion.1
  53.0 9.8 %custom-call.6 = f32[1,128,128]{1,2,0:T(8,128)S(1)} custom-call(f32[1,128,128]{2,1,0:T(8,128)S(1)} %get-tuple-element.10), custom_call_target="InvertDiagBlocksLowerTriangular" | custom-call | tf_op jit(solution)/shard_map/jit(_solve_triangular)/triangular_solve | solution.py:21
  64.1 11.7 %cholesky.55 = f32[128,128]{1,0:T(8,128)S(1)} custom-call(f32[128,128]{1,0:T(8,128)S(1)} %fusion.21), custom_call_target="Cholesky" | custom-call | tf_op jit(solution)/shard_map/jit(cholesky)/cholesky | solution.py:23
  75.9 0.6 compare_reduce_fusion
  76.5 0.7 select_bitcast_fusion
  77.2 9.8 %custom-call.7 = f32[1,128,128]{1,2,0:T(8,128)S(1)} custom-call(f32[1,128,128]{2,1,0:T(8,128)S(1)} %get-tuple-element.8), custom_call_target="InvertDiagBlocksLowerTriangular" | custom-call | tf_op jit(solution)/shard_map/jit(_solve_triangular)/triangular_solve | solution.py:24
  87.6 0.8 copy.27
  88.5 3.2 %convolution_multiply_fusion = f32[2048,256]{1,0:T(8,128)} fusion(f32[2048,256]{1,0:T(8,128)S(1)} %fusion.1, f32[128,128]{1,0:T(8,128)S(1)} %fusion.16, f32[128,128]{1,0:T(8,128)S(1)} %copy.26, f32[128,128]{1,0:T(8,128)S(1)} %convolution_negate_fusion), kind=kOutput, calls=%fused_computation.2 | convolution fusion | flops 1611399168 | bytes 4390912 | tf_op jit(solution)/shard_map/dot_general | solution.py:120
  (38 shorter events, 3.4 us)
Async XLA Ops:
  0.6 1.4 %copy-start = (f32[2048,64]{0,1:T(8,128)S(1)}, f32[2048,64]{0,1:T(8,128)}, u32[]{:S(2)}) copy-start(f32[2048,64]{0,1:T(8,128)} %param.9) | copy-start | bytes 1572868
  6.7 3.5 %copy-start.1 = (f32[1,256,256]{2,1,0:T(8,128)S(1)}, f32[1,256,256]{2,1,0:T(8,128)}, u32[]{:S(2)}) copy-start(f32[1,256,256]{2,1,0:T(8,128)} %param.13) | copy-start | bytes 786436
  11.1 1.5 %collective-permute-start = (f32[136,128]{0,1:T(8,128)S(1)}, f32[136,128]{0,1:T(8,128)S(1)}, u32[]{:S(2)}, u32[]{:S(2)}) collective-permute-start(f32[136,128]{0,1:T(8,128)S(1)} %pad_select_fusion), channel_id=1, source_target_pairs={{0,1},{1,0},{2,3},{3,2},{4,5},{5,4},{6,7},{7,6},{8,9},{9,8},{10,11... | collective-permute-start | bytes 208904 | tf_op jit(solution)/shard_map/ppermute | solution.py:59
  12.7 8.2 %collective-permute-start.3 = (f32[136,128]{0,1:T(8,128)S(1)}, f32[136,128]{0,1:T(8,128)S(1)}, u32[]{:S(2)}, u32[]{:S(2)}) collective-permute-start(f32[136,128]{0,1:T(8,128)S(1)} %fusion.9), channel_id=1, source_target_pairs={{0,6},{1,7},{2,4},{3,5},{4,2},{5,3},{6,0},{7,1},{8,14},{9,15},{10,... | collective-permute-start | bytes 208904 | tf_op jit(solution)/shard_map/ppermute | solution.py:59
  16.5 6.9 %collective-permute-start.2 = (f32[136,128]{0,1:T(8,128)S(1)}, f32[136,128]{0,1:T(8,128)S(1)}, u32[]{:S(2)}, u32[]{:S(2)}) collective-permute-start(f32[136,128]{0,1:T(8,128)S(1)} %fusion.9), channel_id=1, source_target_pairs={{0,4},{1,5},{2,6},{3,7},{4,0},{5,1},{6,2},{7,3},{8,12},{9,13},{10,... | collective-permute-start | bytes 208904 | tf_op jit(solution)/shard_map/ppermute | solution.py:59
  17.1 6.3 %collective-permute-start.1 = (f32[136,128]{0,1:T(8,128)S(1)}, f32[136,128]{0,1:T(8,128)S(1)}, u32[]{:S(2)}, u32[]{:S(2)}) collective-permute-start(f32[136,128]{0,1:T(8,128)S(1)} %fusion.9), channel_id=1, source_target_pairs={{0,2},{1,3},{2,0},{3,1},{4,6},{5,7},{6,4},{7,5},{8,10},{9,11},{10,... | collective-permute-start | bytes 208904 | tf_op jit(solution)/shard_map/ppermute | solution.py:59
  23.4 8.3 %collective-permute-start.6 = (f32[136,128]{0,1:T(8,128)S(1)}, f32[136,128]{0,1:T(8,128)S(1)}, u32[]{:S(2)}, u32[]{:S(2)}) collective-permute-start(f32[136,128]{0,1:T(8,128)S(1)} %add_add_fusion.1), channel_id=1, source_target_pairs={{0,24},{1,25},{2,26},{3,27},{4,28},{5,29},{6,30},{7,31},{8,16},{9,... | collective-permute-start | bytes 208904 | tf_op jit(solution)/shard_map/ppermute | solution.py:59
  27.1 10.8 %collective-permute-start.5 = (f32[136,128]{0,1:T(8,128)S(1)}, f32[136,128]{0,1:T(8,128)S(1)}, u32[]{:S(2)}, u32[]{:S(2)}) collective-permute-start(f32[136,128]{0,1:T(8,128)S(1)} %add_add_fusion.1), channel_id=1, source_target_pairs={{0,16},{1,17},{2,18},{3,19},{4,20},{5,21},{6,22},{7,23},{8,24},{9,... | collective-permute-start | bytes 208904 | tf_op jit(solution)/shard_map/ppermute | solution.py:59
  27.1 10.8 %collective-permute-start.4 = (f32[136,128]{0,1:T(8,128)S(1)}, f32[136,128]{0,1:T(8,128)S(1)}, u32[]{:S(2)}, u32[]{:S(2)}) collective-permute-start(f32[136,128]{0,1:T(8,128)S(1)} %add_add_fusion.1), channel_id=1, source_target_pairs={{0,8},{1,9},{2,10},{3,11},{4,12},{5,13},{6,14},{7,15},{8,0},{9,1},... | collective-permute-start | bytes 208904 | tf_op jit(solution)/shard_map/ppermute | solution.py:59
  38.0 1.4 %collective-permute-start.7 = (f32[136,128]{0,1:T(8,128)S(1)}, f32[136,128]{0,1:T(8,128)S(1)}, u32[]{:S(2)}, u32[]{:S(2)}) collective-permute-start(f32[136,128]{0,1:T(8,128)S(1)} %add_add_fusion), channel_id=1, source_target_pairs={{0,1},{1,0},{2,3},{3,2},{4,5},{5,4},{6,7},{7,6},{8,9},{9,8},{10,11... | collective-permute-start | bytes 208904 | tf_op jit(solution)/shard_map/ppermute | solution.py:59

commit v7 on v6

--- a/solution.py
+++ b/solution.py
@@ -53,6 +53,9 @@
     return g11, g21, g22
 
 
+ROUND_BITS = 4
+
+
 def flip(array, mask):
     axes = ("grp", "leaf")
     count = lax.axis_size("grp") * lax.axis_size("leaf")
@@ -71,15 +74,14 @@
     keep = keep + flip(send, 1)
     rest = list(range(1, bits))
     while rest:
-        if len(rest) == 1:
-            keep = keep + flip(keep, 1 << rest[0])
-            rest = []
-        else:
-            ma, mb = 1 << rest[0], 1 << rest[1]
-            near = keep + flip(keep, ma)
-            far = flip(keep, mb) + flip(keep, ma | mb)
-            keep = near + far
-            rest = rest[2:]
+        group, rest = rest[:ROUND_BITS], rest[ROUND_BITS:]
+        copies = [keep]
+        for m in range(1, 1 << len(group)):
+            mask = sum(1 << b for k, b in enumerate(group) if m >> k & 1)
+            copies.append(flip(keep, mask))
+        while len(copies) > 1:
+            copies = [copies[i] + copies[i + 1] for i in range(0, len(copies), 2)]
+        keep = copies[0]
     other = flip(keep, 1)
     first = jnp.where(low, keep, other)
     second = jnp.where(low, other, keep)

time: 91.9 us -> 131 us (1.43)
  starting transfers between devices: 9.58 us -> 44.3 us
  waiting for transfers between devices: 18.6 us -> 23 us
    ppermute x8 -> x17, starting transfers between devices: 9.58 us -> 44.3 us  [flip(): return lax.ppermute(array, axes, [(i, i ^ mask) for i in range(count)])]
    ppermute x8 -> x17, waiting for transfers between devices: 18.6 us -> 23 us  [flip(): return lax.ppermute(array, axes, [(i, i ^ mask) for i in range(count)])]
  transfers between devices with their start and end apart: 8 -> 17, of which waited for: 6 -> 12; matrix products, arithmetic and copies ran while one was open for 0% -> 0% of each run, Pallas kernels for 0% -> 0%
where the time goes in v7:
time: 131 us
  other arithmetic  46.2 us (35%)
  starting transfers between devices  44.3 us (34%)
  waiting for transfers between devices  23 us (18%)
  matrix products  13.4 us (10%)
  local copies, waits for them, and re-layouts  2.3 us (2%)
  between operations  1.61 us (1%)
    ppermute x17, starting transfers between devices, flip(): return lax.ppermute(array, axes, [(i, i ^ mask) for i in range(count)])  44.3 us
    ppermute x17, waiting for transfers between devices, flip(): return lax.ppermute(array, axes, [(i, i ^ mask) for i in range(count)])  23 us
    another operation x3, other arithmetic, cholesky_and_inverse(): l11 = jnp.linalg.cholesky(g11)  12.5 us
    another operation x3, other arithmetic, cholesky_and_inverse(): l22 = jnp.linalg.cholesky(g22 - mm(l21, l21.T))  12.4 us
    another operation x2, other arithmetic, cholesky_and_inverse(): i11 = jax.scipy.linalg.solve_triangular(l11, eye, lower=True)  10.5 us
    another operation x2, other arithmetic, cholesky_and_inverse(): i22 = jax.scipy.linalg.solve_triangular(l22, eye, lower=True)  10.5 us
    dot_general x1, matrix products, per_device(): jnp.dot(inputs, freqs, precision=lax.Precision.HIGHEST) + phases[None, :]  4.59 us
    dot_general x1, matrix products, per_device(): lax.dot_general(features, features, (((0,), (0,)), ((), ())), precision=l...  3.45 us
  transfers between devices with their start and end apart: 17, of which 12 were waited for; matrix products, arithmetic and copies ran while one was open for 0% of the time, Pallas kernels for 0%

profile of v7, /device:TPU:0, one launch (start us, length us, event | category | flops | bytes accessed | tf_op | source)
XLA Modules:
  0.0 130.8 jit_solution(13128384490443853641)
XLA Ops:
  2.1 4.6 %fusion.1 = f32[2048,256]{1,0:T(8,128)S(1)} fusion(f32[2048,64]{0,1:T(8,128)S(1)} %copy-done, f32[64,256]{1,0:T(8,128)} %param.10, f32[256]{0:T(256)} %param.11, f32[2048]{0:T(1024)S(1)} %sqrt.3), kind=kOutput, calls=%fused_computation.5 | convolution fusion | flops 417857536 | bytes 2696192 | tf_op jit(solution)/shard_map/dot_general | solution.py:110
  6.7 3.5 %fusion.31 = f32[256,256]{0,1:T(8,128)S(1)} fusion(f32[2048,256]{1,0:T(8,128)S(1)} %fusion.1), kind=kOutput, calls=%fused_computation.66 | convolution fusion | flops 1610612736 | bytes 2359296 | tf_op jit(solution)/shard_map/dot_general | solution.py:112
  11.7 1.0 collective-permute-done
  12.7 6.9 %collective-permute-start.15 = (f32[136,128]{0,1:T(8,128)S(1)}, f32[136,128]{0,1:T(8,128)S(1)}, u32[]{:S(2)}, u32[]{:S(2)}) collective-permute-start(f32[136,128]{0,1:T(8,128)S(1)} %fusion.9), channel_id=1, source_target_pairs={{0,30},{1,31},{2,28},{3,29},{4,26},{5,27},{6,24},{7,25},{8,22},{9,... | collective-permute-start | bytes 208904 | tf_op jit(solution)/shard_map/ppermute | solution.py:62
  19.8 3.5 %collective-permute-start.13 = (f32[136,128]{0,1:T(8,128)S(1)}, f32[136,128]{0,1:T(8,128)S(1)}, u32[]{:S(2)}, u32[]{:S(2)}) collective-permute-start(f32[136,128]{0,1:T(8,128)S(1)} %fusion.9), channel_id=1, source_target_pairs={{0,26},{1,27},{2,24},{3,25},{4,30},{5,31},{6,28},{7,29},{8,18},{9,... | collective-permute-start | bytes 208904 | tf_op jit(solution)/shard_map/ppermute | solution.py:62
  24.4 16.8 %collective-permute-start.10 = (f32[136,128]{0,1:T(8,128)S(1)}, f32[136,128]{0,1:T(8,128)S(1)}, u32[]{:S(2)}, u32[]{:S(2)}) collective-permute-start(f32[136,128]{0,1:T(8,128)S(1)} %fusion.9), channel_id=1, source_target_pairs={{0,20},{1,21},{2,22},{3,23},{4,16},{5,17},{6,18},{7,19},{8,28},{9,... | collective-permute-start | bytes 208904 | tf_op jit(solution)/shard_map/ppermute | solution.py:62
  41.2 1.9 %collective-permute-start.9 = (f32[136,128]{0,1:T(8,128)S(1)}, f32[136,128]{0,1:T(8,128)S(1)}, u32[]{:S(2)}, u32[]{:S(2)}) collective-permute-start(f32[136,128]{0,1:T(8,128)S(1)} %fusion.9), channel_id=1, source_target_pairs={{0,18},{1,19},{2,16},{3,17},{4,22},{5,23},{6,20},{7,21},{8,26},{9,... | collective-permute-start | bytes 208904 | tf_op jit(solution)/shard_map/ppermute | solution.py:62
  43.1 6.5 %collective-permute-start.8 = (f32[136,128]{0,1:T(8,128)S(1)}, f32[136,128]{0,1:T(8,128)S(1)}, u32[]{:S(2)}, u32[]{:S(2)}) collective-permute-start(f32[136,128]{0,1:T(8,128)S(1)} %fusion.9), channel_id=1, source_target_pairs={{0,16},{1,17},{2,18},{3,19},{4,20},{5,21},{6,22},{7,23},{8,24},{9,... | collective-permute-start | bytes 208904 | tf_op jit(solution)/shard_map/ppermute | solution.py:62
  49.6 3.8 %collective-permute-start.7 = (f32[136,128]{0,1:T(8,128)S(1)}, f32[136,128]{0,1:T(8,128)S(1)}, u32[]{:S(2)}, u32[]{:S(2)}) collective-permute-start(f32[136,128]{0,1:T(8,128)S(1)} %fusion.9), channel_id=1, source_target_pairs={{0,14},{1,15},{2,12},{3,13},{4,10},{5,11},{6,8},{7,9},{8,6},{9,7},... | collective-permute-start | bytes 208904 | tf_op jit(solution)/shard_map/ppermute | solution.py:62
  53.3 3.8 %collective-permute-done.11 = f32[136,128]{0,1:T(8,128)S(1)} collective-permute-done((f32[136,128]{0,1:T(8,128)S(1)}, f32[136,128]{0,1:T(8,128)S(1)}, u32[]{:S(2)}, u32[]{:S(2)}) %collective-permute-start.11) | collective-permute-done | bytes 69664 | tf_op jit(solution)/shard_map/ppermute | solution.py:62
  57.1 2.9 %collective-permute-done.10 = f32[136,128]{0,1:T(8,128)S(1)} collective-permute-done((f32[136,128]{0,1:T(8,128)S(1)}, f32[136,128]{0,1:T(8,128)S(1)}, u32[]{:S(2)}, u32[]{:S(2)}) %collective-permute-start.10) | collective-permute-done | bytes 69664 | tf_op jit(solution)/shard_map/ppermute | solution.py:62
  60.0 1.0 collective-permute-start.5
  61.0 1.7 %collective-permute-done.9 = f32[136,128]{0,1:T(8,128)S(1)} collective-permute-done((f32[136,128]{0,1:T(8,128)S(1)}, f32[136,128]{0,1:T(8,128)S(1)}, u32[]{:S(2)}, u32[]{:S(2)}) %collective-permute-start.9) | collective-permute-done | bytes 69664 | tf_op jit(solution)/shard_map/ppermute | solution.py:62
  62.8 2.1 %collective-permute-done.8 = f32[136,128]{0,1:T(8,128)S(1)} collective-permute-done((f32[136,128]{0,1:T(8,128)S(1)}, f32[136,128]{0,1:T(8,128)S(1)}, u32[]{:S(2)}, u32[]{:S(2)}) %collective-permute-start.8) | collective-permute-done | bytes 69664 | tf_op jit(solution)/shard_map/ppermute | solution.py:62
  66.1 1.5 %collective-permute-start.2 = (f32[136,128]{0,1:T(8,128)S(1)}, f32[136,128]{0,1:T(8,128)S(1)}, u32[]{:S(2)}, u32[]{:S(2)}) collective-permute-start(f32[136,128]{0,1:T(8,128)S(1)} %fusion.9), channel_id=1, source_target_pairs={{0,4},{1,5},{2,6},{3,7},{4,0},{5,1},{6,2},{7,3},{8,12},{9,13},{10,... | collective-permute-start | bytes 208904 | tf_op jit(solution)/shard_map/ppermute | solution.py:62
  67.6 2.7 %collective-permute-done.6 = f32[136,128]{0,1:T(8,128)S(1)} collective-permute-done((f32[136,128]{0,1:T(8,128)S(1)}, f32[136,128]{0,1:T(8,128)S(1)}, u32[]{:S(2)}, u32[]{:S(2)}) %collective-permute-start.6) | collective-permute-done | bytes 69664 | tf_op jit(solution)/shard_map/ppermute | solution.py:62
  70.2 4.1 %collective-permute-done.5 = f32[136,128]{0,1:T(8,128)S(1)} collective-permute-done((f32[136,128]{0,1:T(8,128)S(1)}, f32[136,128]{0,1:T(8,128)S(1)}, u32[]{:S(2)}, u32[]{:S(2)}) %collective-permute-start.5) | collective-permute-done | bytes 69664 | tf_op jit(solution)/shard_map/ppermute | solution.py:62
  74.8 2.3 %collective-permute-done.1 = f32[136,128]{0,1:T(8,128)S(1)} collective-permute-done((f32[136,128]{0,1:T(8,128)S(1)}, f32[136,128]{0,1:T(8,128)S(1)}, u32[]{:S(2)}, u32[]{:S(2)}) %collective-permute-start.1) | collective-permute-done | bytes 69664 | tf_op jit(solution)/shard_map/ppermute | solution.py:62
  77.3 1.3 %collective-permute-done.16 = f32[136,128]{0,1:T(8,128)S(1)} collective-permute-done((f32[136,128]{0,1:T(8,128)S(1)}, f32[136,128]{0,1:T(8,128)S(1)}, u32[]{:S(2)}, u32[]{:S(2)}) %collective-permute-start.16) | collective-permute-done | bytes 69664 | tf_op jit(solution)/shard_map/ppermute | solution.py:62
  79.0 11.8 %cholesky.44 = f32[128,128]{1,0:T(8,128)S(1)} custom-call(f32[128,128]{1,0:T(8,128)S(1)} %fusion.23), custom_call_target="Cholesky" | custom-call | tf_op jit(solution)/shard_map/jit(cholesky)/cholesky | solution.py:20
  92.2 9.8 %custom-call.6 = f32[1,128,128]{1,2,0:T(8,128)S(1)} custom-call(f32[1,128,128]{2,1,0:T(8,128)S(1)} %get-tuple-element.10), custom_call_target="InvertDiagBlocksLowerTriangular" | custom-call | tf_op jit(solution)/shard_map/jit(_solve_triangular)/triangular_solve | solution.py:21
  103.3 11.7 %cholesky.55 = f32[128,128]{1,0:T(8,128)S(1)} custom-call(f32[128,128]{1,0:T(8,128)S(1)} %fusion.21), custom_call_target="Cholesky" | custom-call | tf_op jit(solution)/shard_map/jit(cholesky)/cholesky | solution.py:23
  116.3 9.8 %custom-call.7 = f32[1,128,128]{1,2,0:T(8,128)S(1)} custom-call(f32[1,128,128]{2,1,0:T(8,128)S(1)} %get-tuple-element.8), custom_call_target="InvertDiagBlocksLowerTriangular" | custom-call | tf_op jit(solution)/shard_map/jit(_solve_triangular)/triangular_solve | solution.py:24
  127.6 3.2 %convolution_multiply_fusion = f32[2048,256]{1,0:T(8,128)} fusion(f32[2048,256]{1,0:T(8,128)S(1)} %fusion.1, f32[128,128]{1,0:T(8,128)S(1)} %fusion.16, f32[128,128]{1,0:T(8,128)S(1)} %copy.26, f32[128,128]{1,0:T(8,128)S(1)} %convolution_negate_fusion), kind=kOutput, calls=%fused_computation.2 | convolution fusion | flops 1611399168 | bytes 4390912 | tf_op jit(solution)/shard_map/dot_general | solution.py:122
  (55 shorter events, 11.2 us)
Async XLA Ops:
  0.6 1.4 %copy-start = (f32[2048,64]{0,1:T(8,128)S(1)}, f32[2048,64]{0,1:T(8,128)}, u32[]{:S(2)}) copy-start(f32[2048,64]{0,1:T(8,128)} %param.9) | copy-start | bytes 1572868
  6.7 3.5 %copy-start.1 = (f32[1,256,256]{2,1,0:T(8,128)S(1)}, f32[1,256,256]{2,1,0:T(8,128)}, u32[]{:S(2)}) copy-start(f32[1,256,256]{2,1,0:T(8,128)} %param.13) | copy-start | bytes 786436
  11.1 1.5 %collective-permute-start = (f32[136,128]{0,1:T(8,128)S(1)}, f32[136,128]{0,1:T(8,128)S(1)}, u32[]{:S(2)}, u32[]{:S(2)}) collective-permute-start(f32[136,128]{0,1:T(8,128)S(1)} %pad_select_fusion), channel_id=1, source_target_pairs={{0,1},{1,0},{2,3},{3,2},{4,5},{5,4},{6,7},{7,6},{8,9},{9,8},{10,11... | collective-permute-start | bytes 208904 | tf_op jit(solution)/shard_map/ppermute | solution.py:62
  12.7 11.7 %collective-permute-start.15 = (f32[136,128]{0,1:T(8,128)S(1)}, f32[136,128]{0,1:T(8,128)S(1)}, u32[]{:S(2)}, u32[]{:S(2)}) collective-permute-start(f32[136,128]{0,1:T(8,128)S(1)} %fusion.9), channel_id=1, source_target_pairs={{0,30},{1,31},{2,28},{3,29},{4,26},{5,27},{6,24},{7,25},{8,22},{9,... | collective-permute-start | bytes 208904 | tf_op jit(solution)/shard_map/ppermute | solution.py:62
  19.6 21.6 %collective-permute-start.14 = (f32[136,128]{0,1:T(8,128)S(1)}, f32[136,128]{0,1:T(8,128)S(1)}, u32[]{:S(2)}, u32[]{:S(2)}) collective-permute-start(f32[136,128]{0,1:T(8,128)S(1)} %fusion.9), channel_id=1, source_target_pairs={{0,28},{1,29},{2,30},{3,31},{4,24},{5,25},{6,26},{7,27},{8,20},{9,... | collective-permute-start | bytes 208904 | tf_op jit(solution)/shard_map/ppermute | solution.py:62
  19.8 23.3 %collective-permute-start.13 = (f32[136,128]{0,1:T(8,128)S(1)}, f32[136,128]{0,1:T(8,128)S(1)}, u32[]{:S(2)}, u32[]{:S(2)}) collective-permute-start(f32[136,128]{0,1:T(8,128)S(1)} %fusion.9), channel_id=1, source_target_pairs={{0,26},{1,27},{2,24},{3,25},{4,30},{5,31},{6,28},{7,29},{8,18},{9,... | collective-permute-start | bytes 208904 | tf_op jit(solution)/shard_map/ppermute | solution.py:62
  23.3 26.3 %collective-permute-start.12 = (f32[136,128]{0,1:T(8,128)S(1)}, f32[136,128]{0,1:T(8,128)S(1)}, u32[]{:S(2)}, u32[]{:S(2)}) collective-permute-start(f32[136,128]{0,1:T(8,128)S(1)} %fusion.9), channel_id=1, source_target_pairs={{0,24},{1,25},{2,26},{3,27},{4,28},{5,29},{6,30},{7,31},{8,16},{9,... | collective-permute-start | bytes 208904 | tf_op jit(solution)/shard_map/ppermute | solution.py:62
  23.5 33.6 %collective-permute-start.11 = (f32[136,128]{0,1:T(8,128)S(1)}, f32[136,128]{0,1:T(8,128)S(1)}, u32[]{:S(2)}, u32[]{:S(2)}) collective-permute-start(f32[136,128]{0,1:T(8,128)S(1)} %fusion.9), channel_id=1, source_target_pairs={{0,22},{1,23},{2,20},{3,21},{4,18},{5,19},{6,16},{7,17},{8,30},{9,... | collective-permute-start | bytes 208904 | tf_op jit(solution)/shard_map/ppermute | solution.py:62
  24.4 35.6 %collective-permute-start.10 = (f32[136,128]{0,1:T(8,128)S(1)}, f32[136,128]{0,1:T(8,128)S(1)}, u32[]{:S(2)}, u32[]{:S(2)}) collective-permute-start(f32[136,128]{0,1:T(8,128)S(1)} %fusion.9), channel_id=1, source_target_pairs={{0,20},{1,21},{2,22},{3,23},{4,16},{5,17},{6,18},{7,19},{8,28},{9,... | collective-permute-start | bytes 208904 | tf_op jit(solution)/shard_map/ppermute | solution.py:62
  41.2 21.5 %collective-permute-start.9 = (f32[136,128]{0,1:T(8,128)S(1)}, f32[136,128]{0,1:T(8,128)S(1)}, u32[]{:S(2)}, u32[]{:S(2)}) collective-permute-start(f32[136,128]{0,1:T(8,128)S(1)} %fusion.9), channel_id=1, source_target_pairs={{0,18},{1,19},{2,16},{3,17},{4,22},{5,23},{6,20},{7,21},{8,26},{9,... | collective-permute-start | bytes 208904 | tf_op jit(solution)/shard_map/ppermute | solution.py:62
  43.1 21.7 %collective-permute-start.8 = (f32[136,128]{0,1:T(8,128)S(1)}, f32[136,128]{0,1:T(8,128)S(1)}, u32[]{:S(2)}, u32[]{:S(2)}) collective-permute-start(f32[136,128]{0,1:T(8,128)S(1)} %fusion.9), channel_id=1, source_target_pairs={{0,16},{1,17},{2,18},{3,19},{4,20},{5,21},{6,22},{7,23},{8,24},{9,... | collective-permute-start | bytes 208904 | tf_op jit(solution)/shard_map/ppermute | solution.py:62
  49.6 16.5 %collective-permute-start.7 = (f32[136,128]{0,1:T(8,128)S(1)}, f32[136,128]{0,1:T(8,128)S(1)}, u32[]{:S(2)}, u32[]{:S(2)}) collective-permute-start(f32[136,128]{0,1:T(8,128)S(1)} %fusion.9), channel_id=1, source_target_pairs={{0,14},{1,15},{2,12},{3,13},{4,10},{5,11},{6,8},{7,9},{8,6},{9,7},... | collective-permute-start | bytes 208904 | tf_op jit(solution)/shard_map/ppermute | solution.py:62
  57.1 13.1 %collective-permute-start.6 = (f32[136,128]{0,1:T(8,128)S(1)}, f32[136,128]{0,1:T(8,128)S(1)}, u32[]{:S(2)}, u32[]{:S(2)}) collective-permute-start(f32[136,128]{0,1:T(8,128)S(1)} %fusion.9), channel_id=1, source_target_pairs={{0,12},{1,13},{2,14},{3,15},{4,8},{5,9},{6,10},{7,11},{8,4},{9,5},... | collective-permute-start | bytes 208904 | tf_op jit(solution)/shard_map/ppermute | solution.py:62
  60.0 14.4 %collective-permute-start.5 = (f32[136,128]{0,1:T(8,128)S(1)}, f32[136,128]{0,1:T(8,128)S(1)}, u32[]{:S(2)}, u32[]{:S(2)}) collective-permute-start(f32[136,128]{0,1:T(8,128)S(1)} %fusion.9), channel_id=1, source_target_pairs={{0,10},{1,11},{2,8},{3,9},{4,14},{5,15},{6,12},{7,13},{8,2},{9,3},... | collective-permute-start | bytes 208904 | tf_op jit(solution)/shard_map/ppermute | solution.py:62
  62.7 11.7 %collective-permute-start.4 = (f32[136,128]{0,1:T(8,128)S(1)}, f32[136,128]{0,1:T(8,128)S(1)}, u32[]{:S(2)}, u32[]{:S(2)}) collective-permute-start(f32[136,128]{0,1:T(8,128)S(1)} %fusion.9), channel_id=1, source_target_pairs={{0,8},{1,9},{2,10},{3,11},{4,12},{5,13},{6,14},{7,15},{8,0},{9,1},... | collective-permute-start | bytes 208904 | tf_op jit(solution)/shard_map/ppermute | solution.py:62
  64.8 9.7 %collective-permute-start.3 = (f32[136,128]{0,1:T(8,128)S(1)}, f32[136,128]{0,1:T(8,128)S(1)}, u32[]{:S(2)}, u32[]{:S(2)}) collective-permute-start(f32[136,128]{0,1:T(8,128)S(1)} %fusion.9), channel_id=1, source_target_pairs={{0,6},{1,7},{2,4},{3,5},{4,2},{5,3},{6,0},{7,1},{8,14},{9,15},{10,... | collective-permute-start | bytes 208904 | tf_op jit(solution)/shard_map/ppermute | solution.py:62
  66.1 8.7 %collective-permute-start.2 = (f32[136,128]{0,1:T(8,128)S(1)}, f32[136,128]{0,1:T(8,128)S(1)}, u32[]{:S(2)}, u32[]{:S(2)}) collective-permute-start(f32[136,128]{0,1:T(8,128)S(1)} %fusion.9), channel_id=1, source_target_pairs={{0,4},{1,5},{2,6},{3,7},{4,0},{5,1},{6,2},{7,3},{8,12},{9,13},{10,... | collective-permute-start | bytes 208904 | tf_op jit(solution)/shard_map/ppermute | solution.py:62
  70.2 6.8 %collective-permute-start.1 = (f32[136,128]{0,1:T(8,128)S(1)}, f32[136,128]{0,1:T(8,128)S(1)}, u32[]{:S(2)}, u32[]{:S(2)}) collective-permute-start(f32[136,128]{0,1:T(8,128)S(1)} %fusion.9), channel_id=1, source_target_pairs={{0,2},{1,3},{2,0},{3,1},{4,6},{5,7},{6,4},{7,5},{8,10},{9,11},{10,... | collective-permute-start | bytes 208904 | tf_op jit(solution)/shard_map/ppermute | solution.py:62
  77.2 1.4 %collective-permute-start.16 = (f32[136,128]{0,1:T(8,128)S(1)}, f32[136,128]{0,1:T(8,128)S(1)}, u32[]{:S(2)}, u32[]{:S(2)}) collective-permute-start(f32[136,128]{0,1:T(8,128)S(1)} %add_add_fusion), channel_id=1, source_target_pairs={{0,1},{1,0},{2,3},{3,2},{4,5},{5,4},{6,7},{7,6},{8,9},{9,8},{10,11... | collective-permute-start | bytes 208904 | tf_op jit(solution)/shard_map/ppermute | solution.py:62

commit v8 on v6

--- a/solution.py
+++ b/solution.py
@@ -17,11 +17,11 @@
 def cholesky_and_inverse(g11, g21, g22):
     h = g11.shape[0]
     eye = jnp.eye(h, dtype=g11.dtype)
-    l11 = jnp.linalg.cholesky(g11)
-    i11 = jax.scipy.linalg.solve_triangular(l11, eye, lower=True)
+    l11 = lax.linalg.cholesky(g11, symmetrize_input=False)
+    i11 = lax.linalg.triangular_solve(l11, eye, left_side=True, lower=True)
     l21 = mm(g21, i11.T)
-    l22 = jnp.linalg.cholesky(g22 - mm(l21, l21.T))
-    i22 = jax.scipy.linalg.solve_triangular(l22, eye, lower=True)
+    l22 = lax.linalg.cholesky(g22 - mm(l21, l21.T), symmetrize_input=False)
+    i22 = lax.linalg.triangular_solve(l22, eye, left_side=True, lower=True)
     i21 = -mm(i22, mm(l21, i11))
     zero = jnp.zeros_like(l11)
     lower = jnp.block([[l11, zero], [l21, l22]])

time: 91.9 us -> 84 us (0.914)
  waiting for transfers between devices: 18.6 us -> 11 us
    ppermute x8, waiting for transfers between devices: 18.6 us -> 11 us  [flip(): return lax.ppermute(array, axes, [(i, i ^ mask) for i in range(count)])]
  transfers between devices with their start and end apart: 8 -> 8, of which waited for: 6 -> 7; matrix products, arithmetic and copies ran while one was open for 0% -> 0% of each run, Pallas kernels for 0% -> 0%
where the time goes in v8:
time: 84 us; the launch traced here: 83.7 us
  other arithmetic  46.2 us (55%)
  matrix products  13.5 us (16%)
  waiting for transfers between devices  11 us (13%)
  starting transfers between devices  9.57 us (11%)
  local copies, waits for them, and re-layouts  1.91 us (2%)
  between operations  1.56 us (2%)
    another operation x3, other arithmetic, cholesky_and_inverse(): l11 = lax.linalg.cholesky(g11, symmetrize_input=False)  12.6 us
    another operation x3, other arithmetic, cholesky_and_inverse(): l22 = lax.linalg.cholesky(g22 - mm(l21, l21.T), symmetrize_input=False)  12.4 us
    ppermute x8, waiting for transfers between devices, flip(): return lax.ppermute(array, axes, [(i, i ^ mask) for i in range(count)])  11 us
    another operation x2, other arithmetic, cholesky_and_inverse(): i22 = lax.linalg.triangular_solve(l22, eye, left_side=True, lower=True)  10.5 us
    another operation x2, other arithmetic, cholesky_and_inverse(): i11 = lax.linalg.triangular_solve(l11, eye, left_side=True, lower=True)  10.5 us
    ppermute x8, starting transfers between devices, flip(): return lax.ppermute(array, axes, [(i, i ^ mask) for i in range(count)])  9.57 us
    dot_general x1, matrix products, per_device(): jnp.dot(inputs, freqs, precision=lax.Precision.HIGHEST) + phases[None, :]  4.59 us
    dot_general x1, matrix products, per_device(): lax.dot_general(features, features, (((0,), (0,)), ((), ())), precision=l...  3.48 us
  transfers between devices with their start and end apart: 8, of which 7 were waited for; matrix products, arithmetic and copies ran while one was open for 0% of the time, Pallas kernels for 0%

profile of v8, /device:TPU:0, one launch (start us, length us, event | category | flops | bytes accessed | tf_op | source)
XLA Modules:
  0.0 83.7 jit_solution(3173187591952398106)
XLA Ops:
  1.4 0.7 sqrt.3
  2.1 4.6 %fusion.1 = f32[2048,256]{1,0:T(8,128)S(1)} fusion(f32[2048,64]{0,1:T(8,128)S(1)} %copy-done, f32[64,256]{1,0:T(8,128)} %param.10, f32[256]{0:T(256)} %param.11, f32[2048]{0:T(1024)S(1)} %sqrt.3), kind=kOutput, calls=%fused_computation.5 | convolution fusion | flops 417857536 | bytes 2696192 | tf_op jit(solution)/shard_map/dot_general | solution.py:108
  6.7 3.5 %fusion.30 = f32[256,256]{1,0:T(8,128)S(1)} fusion(f32[2048,256]{1,0:T(8,128)S(1)} %fusion.1), kind=kOutput, calls=%fused_computation.62 | convolution fusion | flops 1610612736 | bytes 2359296 | tf_op jit(solution)/shard_map/dot_general | solution.py:110
  10.2 0.6 convolution_add_fusion.1
  11.0 0.6 collective-permute-start
  11.6 0.9 %collective-permute-done = f32[136,128]{1,0:T(8,128)S(1)} collective-permute-done((f32[136,128]{1,0:T(8,128)S(1)}, f32[136,128]{1,0:T(8,128)S(1)}, u32[]{:S(2)}, u32[]{:S(2)}) %collective-permute-start) | collective-permute-done | bytes 69664 | tf_op jit(solution)/shard_map/ppermute | solution.py:59
  12.6 3.8 %collective-permute-start.3 = (f32[136,128]{1,0:T(8,128)S(1)}, f32[136,128]{1,0:T(8,128)S(1)}, u32[]{:S(2)}, u32[]{:S(2)}) collective-permute-start(f32[136,128]{1,0:T(8,128)S(1)} %select_add_fusion), channel_id=1, source_target_pairs={{0,6},{1,7},{2,4},{3,5},{4,2},{5,3},{6,0},{7,1},{8,14},{9,15},{10,... | collective-permute-start | bytes 208904 | tf_op jit(solution)/shard_map/ppermute | solution.py:59
  17.0 1.9 %collective-permute-done.3 = f32[136,128]{1,0:T(8,128)S(1)} collective-permute-done((f32[136,128]{1,0:T(8,128)S(1)}, f32[136,128]{1,0:T(8,128)S(1)}, u32[]{:S(2)}, u32[]{:S(2)}) %collective-permute-start.3) | collective-permute-done | bytes 69664 | tf_op jit(solution)/shard_map/ppermute | solution.py:59
  19.0 1.7 %collective-permute-done.2 = f32[136,128]{1,0:T(8,128)S(1)} collective-permute-done((f32[136,128]{1,0:T(8,128)S(1)}, f32[136,128]{1,0:T(8,128)S(1)}, u32[]{:S(2)}, u32[]{:S(2)}) %collective-permute-start.2) | collective-permute-done | bytes 69664 | tf_op jit(solution)/shard_map/ppermute | solution.py:59
  21.3 3.7 %collective-permute-start.6 = (f32[136,128]{1,0:T(8,128)S(1)}, f32[136,128]{1,0:T(8,128)S(1)}, u32[]{:S(2)}, u32[]{:S(2)}) collective-permute-start(f32[136,128]{1,0:T(8,128)S(1)} %add_add_fusion.1), channel_id=1, source_target_pairs={{0,24},{1,25},{2,26},{3,27},{4,28},{5,29},{6,30},{7,31},{8,16},{9,... | collective-permute-start | bytes 208904 | tf_op jit(solution)/shard_map/ppermute | solution.py:59
  24.9 0.8 collective-permute-start.4
  25.7 2.0 %collective-permute-done.6 = f32[136,128]{1,0:T(8,128)S(1)} collective-permute-done((f32[136,128]{1,0:T(8,128)S(1)}, f32[136,128]{1,0:T(8,128)S(1)}, u32[]{:S(2)}, u32[]{:S(2)}) %collective-permute-start.6) | collective-permute-done | bytes 69664 | tf_op jit(solution)/shard_map/ppermute | solution.py:59
  27.7 2.7 %collective-permute-done.5 = f32[136,128]{1,0:T(8,128)S(1)} collective-permute-done((f32[136,128]{1,0:T(8,128)S(1)}, f32[136,128]{1,0:T(8,128)S(1)}, u32[]{:S(2)}, u32[]{:S(2)}) %collective-permute-start.5) | collective-permute-done | bytes 69664 | tf_op jit(solution)/shard_map/ppermute | solution.py:59
  30.5 1.2 %collective-permute-done.7 = f32[136,128]{1,0:T(8,128)S(1)} collective-permute-done((f32[136,128]{1,0:T(8,128)S(1)}, f32[136,128]{1,0:T(8,128)S(1)}, u32[]{:S(2)}, u32[]{:S(2)}) %collective-permute-start.7) | collective-permute-done | bytes 69664 | tf_op jit(solution)/shard_map/ppermute | solution.py:59
  31.9 11.9 %custom-call.8 = f32[128,128]{1,0:T(8,128)S(1)} custom-call(f32[128,128]{1,0:T(8,128)S(1)} %bitcast_select_fusion.1), custom_call_target="Cholesky" | custom-call | tf_op jit(solution)/shard_map/cholesky/custom-call.1 | solution.py:20
  43.8 0.6 compare_reduce_fusion.1
  44.5 0.7 select_bitcast_fusion.1
  45.1 9.8 %custom-call.9 = f32[1,128,128]{1,2,0:T(8,128)S(1)} custom-call(f32[1,128,128]{2,1,0:T(8,128)S(1)} %get-tuple-element.8), custom_call_target="InvertDiagBlocksLowerTriangular" | custom-call | tf_op jit(solution)/shard_map/triangular_solve/custom-call.0 | solution.py:21
  56.2 11.7 %custom-call.10 = f32[128,128]{1,0:T(8,128)S(1)} custom-call(f32[128,128]{1,0:T(8,128)S(1)} %fusion.22), custom_call_target="Cholesky" | custom-call | tf_op jit(solution)/shard_map/cholesky/custom-call.1 | solution.py:23
  67.9 0.6 compare_reduce_fusion
  68.6 0.7 select_bitcast_fusion
  69.2 9.8 %custom-call.11 = f32[1,128,128]{1,2,0:T(8,128)S(1)} custom-call(f32[1,128,128]{2,1,0:T(8,128)S(1)} %get-tuple-element.6), custom_call_target="InvertDiagBlocksLowerTriangular" | custom-call | tf_op jit(solution)/shard_map/triangular_solve/custom-call.0 | solution.py:24
  79.7 0.8 copy.11
  80.6 3.2 %convolution_multiply_fusion = f32[2048,256]{1,0:T(8,128)} fusion(f32[2048,256]{1,0:T(8,128)S(1)} %fusion.1, f32[128,128]{1,0:T(8,128)S(1)} %fusion.15, f32[128,128]{1,0:T(8,128)S(1)} %copy.10, f32[128,128]{1,0:T(8,128)S(1)} %convolution_negate_fusion), kind=kOutput, calls=%fused_computation.2 | convolution fusion | flops 1611399168 | bytes 4390912 | tf_op jit(solution)/shard_map/dot_general | solution.py:120
  (33 shorter events, 3.7 us)
Async XLA Ops:
  0.6 1.4 %copy-start = (f32[2048,64]{0,1:T(8,128)S(1)}, f32[2048,64]{0,1:T(8,128)}, u32[]{:S(2)}) copy-start(f32[2048,64]{0,1:T(8,128)} %param.9) | copy-start | bytes 1572868
  6.7 3.5 %copy-start.1 = (f32[1,256,256]{2,1,0:T(8,128)S(1)}, f32[1,256,256]{2,1,0:T(8,128)}, u32[]{:S(2)}) copy-start(f32[1,256,256]{2,1,0:T(8,128)} %param.13) | copy-start | bytes 786436
  11.0 1.5 %collective-permute-start = (f32[136,128]{1,0:T(8,128)S(1)}, f32[136,128]{1,0:T(8,128)S(1)}, u32[]{:S(2)}, u32[]{:S(2)}) collective-permute-start(f32[136,128]{1,0:T(8,128)S(1)} %pad_select_fusion), channel_id=1, source_target_pairs={{0,1},{1,0},{2,3},{3,2},{4,5},{5,4},{6,7},{7,6},{8,9},{9,8},{10,11... | collective-permute-start | bytes 208904 | tf_op jit(solution)/shard_map/ppermute | solution.py:59
  12.6 6.4 %collective-permute-start.3 = (f32[136,128]{1,0:T(8,128)S(1)}, f32[136,128]{1,0:T(8,128)S(1)}, u32[]{:S(2)}, u32[]{:S(2)}) collective-permute-start(f32[136,128]{1,0:T(8,128)S(1)} %select_add_fusion), channel_id=1, source_target_pairs={{0,6},{1,7},{2,4},{3,5},{4,2},{5,3},{6,0},{7,1},{8,14},{9,15},{10,... | collective-permute-start | bytes 208904 | tf_op jit(solution)/shard_map/ppermute | solution.py:59
  16.4 4.3 %collective-permute-start.2 = (f32[136,128]{1,0:T(8,128)S(1)}, f32[136,128]{1,0:T(8,128)S(1)}, u32[]{:S(2)}, u32[]{:S(2)}) collective-permute-start(f32[136,128]{1,0:T(8,128)S(1)} %select_add_fusion), channel_id=1, source_target_pairs={{0,4},{1,5},{2,6},{3,7},{4,0},{5,1},{6,2},{7,3},{8,12},{9,13},{10,... | collective-permute-start | bytes 208904 | tf_op jit(solution)/shard_map/ppermute | solution.py:59
  16.9 4.3 %collective-permute-start.1 = (f32[136,128]{1,0:T(8,128)S(1)}, f32[136,128]{1,0:T(8,128)S(1)}, u32[]{:S(2)}, u32[]{:S(2)}) collective-permute-start(f32[136,128]{1,0:T(8,128)S(1)} %select_add_fusion), channel_id=1, source_target_pairs={{0,2},{1,3},{2,0},{3,1},{4,6},{5,7},{6,4},{7,5},{8,10},{9,11},{10,... | collective-permute-start | bytes 208904 | tf_op jit(solution)/shard_map/ppermute | solution.py:59
  21.3 6.4 %collective-permute-start.6 = (f32[136,128]{1,0:T(8,128)S(1)}, f32[136,128]{1,0:T(8,128)S(1)}, u32[]{:S(2)}, u32[]{:S(2)}) collective-permute-start(f32[136,128]{1,0:T(8,128)S(1)} %add_add_fusion.1), channel_id=1, source_target_pairs={{0,24},{1,25},{2,26},{3,27},{4,28},{5,29},{6,30},{7,31},{8,16},{9,... | collective-permute-start | bytes 208904 | tf_op jit(solution)/shard_map/ppermute | solution.py:59
  24.9 5.5 %collective-permute-start.5 = (f32[136,128]{1,0:T(8,128)S(1)}, f32[136,128]{1,0:T(8,128)S(1)}, u32[]{:S(2)}, u32[]{:S(2)}) collective-permute-start(f32[136,128]{1,0:T(8,128)S(1)} %add_add_fusion.1), channel_id=1, source_target_pairs={{0,16},{1,17},{2,18},{3,19},{4,20},{5,21},{6,22},{7,23},{8,24},{9,... | collective-permute-start | bytes 208904 | tf_op jit(solution)/shard_map/ppermute | solution.py:59
  24.9 5.5 %collective-permute-start.4 = (f32[136,128]{1,0:T(8,128)S(1)}, f32[136,128]{1,0:T(8,128)S(1)}, u32[]{:S(2)}, u32[]{:S(2)}) collective-permute-start(f32[136,128]{1,0:T(8,128)S(1)} %add_add_fusion.1), channel_id=1, source_target_pairs={{0,8},{1,9},{2,10},{3,11},{4,12},{5,13},{6,14},{7,15},{8,0},{9,1},... | collective-permute-start | bytes 208904 | tf_op jit(solution)/shard_map/ppermute | solution.py:59
  30.4 1.3 %collective-permute-start.7 = (f32[136,128]{1,0:T(8,128)S(1)}, f32[136,128]{1,0:T(8,128)S(1)}, u32[]{:S(2)}, u32[]{:S(2)}) collective-permute-start(f32[136,128]{1,0:T(8,128)S(1)} %add_add_fusion), channel_id=1, source_target_pairs={{0,1},{1,0},{2,3},{3,2},{4,5},{5,4},{6,7},{7,6},{8,9},{9,8},{10,11... | collective-permute-start | bytes 208904 | tf_op jit(solution)/shard_map/ppermute | solution.py:59

commit v9 on v8

--- a/solution.py
+++ b/solution.py
@@ -12,6 +12,14 @@
 
 def mm(a, b):
     return jnp.dot(a, b, precision=lax.Precision.HIGHEST)
+
+
+def tmm(a, b):
+    return lax.dot_general(a, b, (((0,), (0,)), ((), ())), precision=lax.Precision.HIGHEST)
+
+
+def rmm(a, b):
+    return lax.dot_general(a, b, (((1,), (1,)), ((), ())), precision=lax.Precision.HIGHEST)
 
 
 def cholesky_and_inverse(g11, g21, g22):
@@ -29,15 +37,15 @@
     return lower, inverse
 
 
-def pack(gram):
-    h = gram.shape[0] // 2
+def pack(g11, g12, g22):
+    h = g11.shape[0]
     row = lax.broadcasted_iota(jnp.int32, (h, h), 0)
     col = lax.broadcasted_iota(jnp.int32, (h, h), 1)
-    tri = jnp.where(row <= col, gram[:h, :h], gram[h:, h:])
-    diag = jnp.sum(jnp.where(row == col, gram[h:, h:], 0.0), axis=0)
-    pad = jnp.zeros((7, h), gram.dtype)
+    tri = jnp.where(row <= col, g11, g22)
+    diag = jnp.sum(jnp.where(row == col, g22, 0.0), axis=0)
+    pad = jnp.zeros((7, h), g11.dtype)
     first = jnp.concatenate([tri, diag[None, :], pad], axis=0)
-    second = jnp.concatenate([gram[h:, :h], jnp.zeros((8, h), gram.dtype)], axis=0)
+    second = jnp.concatenate([g12.T, jnp.zeros((8, h), g11.dtype)], axis=0)
     return first, second
 
 
@@ -59,9 +67,9 @@
     return lax.ppermute(array, axes, [(i, i ^ mask) for i in range(count)])
 
 
-def all_reduce_symmetric(gram):
+def all_reduce_symmetric(g11, g12, g22):
     bits = (lax.axis_size("grp") * lax.axis_size("leaf")).bit_length() - 1
-    first, second = pack(gram)
+    first, second = pack(g11, g12, g22)
     if bits == 0:
         return unpack(first, second)
     me = lax.axis_index("grp") * lax.axis_size("leaf") + lax.axis_index("leaf")
@@ -107,19 +115,14 @@
     norm_scale = 1.0 / math.sqrt(total_rows)
     proj = jnp.dot(inputs, freqs, precision=lax.Precision.HIGHEST) + phases[None, :]
     features = jnp.sqrt(sample_weight)[:, None] * bounded_cos(proj) * norm_scale
-    gram = lax.dot_general(
-        features, features, (((0,), (0,)), ((), ())), precision=lax.Precision.HIGHEST
-    )
     slot = lax.axis_index("grp") * lax.axis_size("leaf") + lax.axis_index("leaf")
     running = jnp.where(slot == root[0], stored[0], jnp.zeros_like(stored[0]))
-    gram = gram + lax.dot_general(
-        running, running, (((0,), (0,)), ((), ())), precision=lax.Precision.HIGHEST
-    )
-    gram = all_reduce_symmetric(gram)
+    h = features.shape[1] // 2
+    g_top = tmm(features[:, :h], features) + tmm(running[:, :h], running)
+    g22 = tmm(features[:, h:], features[:, h:]) + tmm(running[:, h:], running[:, h:])
+    gram = all_reduce_symmetric(g_top[:, :h], g_top[:, h:], g22)
     lower, inverse = cholesky_and_inverse(*gram)
-    basis = lax.dot_general(
-        features, inverse, (((1,), (1,)), ((), ())), precision=lax.Precision.HIGHEST
-    ) * math.sqrt(total_rows)
+    basis = rmm(features, inverse) * math.sqrt(total_rows)
     return (lower.T, basis)
 
 

time: 84 us -> 85.9 us (1.023)
  matrix products: 13.5 us -> 15.7 us
    dot_general x3 -> x5, matrix products: 7.24 us -> 9.39 us  [the longest x4 6.24 us: tmm(): lax.dot_general(a, b, (((0,), (0,)), ((), ())), precision=lax.Precision.H...]
where the time goes in v9:
time: 85.9 us; the launch traced here: 85.7 us
  other arithmetic  46.1 us (54%)
  matrix products  15.7 us (18%)
  waiting for transfers between devices  11 us (13%)
  starting transfers between devices  9.57 us (11%)
  local copies, waits for them, and re-layouts  2.35 us (3%)
  between operations  0.94 us (1%)
    another operation x3, other arithmetic, cholesky_and_inverse(): l11 = lax.linalg.cholesky(g11, symmetrize_input=False)  12.5 us
    another operation x3, other arithmetic, cholesky_and_inverse(): l22 = lax.linalg.cholesky(g22 - mm(l21, l21.T), symmetrize_input=False)  12.4 us
    ppermute x8, waiting for transfers between devices, flip(): return lax.ppermute(array, axes, [(i, i ^ mask) for i in range(count)])  11 us
    another operation x2, other arithmetic, cholesky_and_inverse(): i22 = lax.linalg.triangular_solve(l22, eye, left_side=True, lower=True)  10.5 us
    another operation x2, other arithmetic, cholesky_and_inverse(): i11 = lax.linalg.triangular_solve(l11, eye, left_side=True, lower=True)  10.5 us
    ppermute x8, starting transfers between devices, flip(): return lax.ppermute(array, axes, [(i, i ^ mask) for i in range(count)])  9.57 us
    dot_general x4, matrix products, tmm(): lax.dot_general(a, b, (((0,), (0,)), ((), ())), precision=lax.Precision.H...  6.24 us
    dot_general x1, matrix products, per_device(): jnp.dot(inputs, freqs, precision=lax.Precision.HIGHEST) + phases[None, :]  4.58 us
  transfers between devices with their start and end apart: 8, of which 7 were waited for; matrix products, arithmetic and copies ran while one was open for 0% of the time, Pallas kernels for 0%

profile of v9, /device:TPU:0, one launch (start us, length us, event | category | flops | bytes accessed | tf_op | source)
XLA Modules:
  0.0 85.7 jit_solution(8111593913383543821)
XLA Ops:
  0.7 0.8 sqrt.3
  1.7 4.6 %fusion.1 = f32[2048,256]{1,0:T(8,128)S(1)} fusion(f32[2048,64]{0,1:T(8,128)S(1)} %copy-done, f32[64,256]{1,0:T(8,128)} %param.10, f32[256]{0:T(256)} %param.11, f32[2048]{0:T(1024)S(1)} %sqrt.3), kind=kOutput, calls=%fused_computation.5 | convolution fusion | flops 417857536 | bytes 2696192 | tf_op jit(solution)/shard_map/dot_general | solution.py:116
  6.3 1.8 %fusion.2 = f32[128,128]{1,0:T(8,128)S(1)} fusion(f32[2048,256]{1,0:T(8,128)S(1)} %fusion.1), kind=kOutput, calls=%fused_computation.9 | convolution fusion | flops 402653184 | bytes 1114112 | tf_op jit(solution)/shard_map/dot_general | solution.py:18
  8.1 3.4 %fusion.4 = f32[128,256]{0,1:T(8,128)S(1)} fusion(f32[2048,256]{1,0:T(8,128)S(1)} %fusion.1), kind=kOutput, calls=%fused_computation.11 | convolution fusion | flops 805306368 | bytes 3276800 | tf_op jit(solution)/shard_map/dot_general | solution.py:18
  11.7 0.6 convolution_add_fusion.1
  13.5 0.9 %collective-permute-done = f32[136,128]{1,0:T(8,128)S(1)} collective-permute-done((f32[136,128]{1,0:T(8,128)S(1)}, f32[136,128]{1,0:T(8,128)S(1)}, u32[]{:S(2)}, u32[]{:S(2)}) %collective-permute-start) | collective-permute-done | bytes 69664 | tf_op jit(solution)/shard_map/ppermute | solution.py:67
  14.5 3.8 %collective-permute-start.3 = (f32[136,128]{1,0:T(8,128)S(1)}, f32[136,128]{1,0:T(8,128)S(1)}, u32[]{:S(2)}, u32[]{:S(2)}) collective-permute-start(f32[136,128]{1,0:T(8,128)S(1)} %select_add_fusion), channel_id=1, source_target_pairs={{0,6},{1,7},{2,4},{3,5},{4,2},{5,3},{6,0},{7,1},{8,14},{9,15},{10,... | collective-permute-start | bytes 208904 | tf_op jit(solution)/shard_map/ppermute | solution.py:67
  19.0 1.9 %collective-permute-done.3 = f32[136,128]{1,0:T(8,128)S(1)} collective-permute-done((f32[136,128]{1,0:T(8,128)S(1)}, f32[136,128]{1,0:T(8,128)S(1)}, u32[]{:S(2)}, u32[]{:S(2)}) %collective-permute-start.3) | collective-permute-done | bytes 69664 | tf_op jit(solution)/shard_map/ppermute | solution.py:67
  20.9 1.7 %collective-permute-done.2 = f32[136,128]{1,0:T(8,128)S(1)} collective-permute-done((f32[136,128]{1,0:T(8,128)S(1)}, f32[136,128]{1,0:T(8,128)S(1)}, u32[]{:S(2)}, u32[]{:S(2)}) %collective-permute-start.2) | collective-permute-done | bytes 69664 | tf_op jit(solution)/shard_map/ppermute | solution.py:67
  23.2 3.7 %collective-permute-start.6 = (f32[136,128]{1,0:T(8,128)S(1)}, f32[136,128]{1,0:T(8,128)S(1)}, u32[]{:S(2)}, u32[]{:S(2)}) collective-permute-start(f32[136,128]{1,0:T(8,128)S(1)} %add_add_fusion.1), channel_id=1, source_target_pairs={{0,24},{1,25},{2,26},{3,27},{4,28},{5,29},{6,30},{7,31},{8,16},{9,... | collective-permute-start | bytes 208904 | tf_op jit(solution)/shard_map/ppermute | solution.py:67
  26.9 0.8 collective-permute-start.4
  27.7 2.0 %collective-permute-done.6 = f32[136,128]{1,0:T(8,128)S(1)} collective-permute-done((f32[136,128]{1,0:T(8,128)S(1)}, f32[136,128]{1,0:T(8,128)S(1)}, u32[]{:S(2)}, u32[]{:S(2)}) %collective-permute-start.6) | collective-permute-done | bytes 69664 | tf_op jit(solution)/shard_map/ppermute | solution.py:67
  29.6 2.7 %collective-permute-done.5 = f32[136,128]{1,0:T(8,128)S(1)} collective-permute-done((f32[136,128]{1,0:T(8,128)S(1)}, f32[136,128]{1,0:T(8,128)S(1)}, u32[]{:S(2)}, u32[]{:S(2)}) %collective-permute-start.5) | collective-permute-done | bytes 69664 | tf_op jit(solution)/shard_map/ppermute | solution.py:67
  32.4 1.2 %collective-permute-done.7 = f32[136,128]{1,0:T(8,128)S(1)} collective-permute-done((f32[136,128]{1,0:T(8,128)S(1)}, f32[136,128]{1,0:T(8,128)S(1)}, u32[]{:S(2)}, u32[]{:S(2)}) %collective-permute-start.7) | collective-permute-done | bytes 69664 | tf_op jit(solution)/shard_map/ppermute | solution.py:67
  33.8 11.9 %custom-call.8 = f32[128,128]{1,0:T(8,128)S(1)} custom-call(f32[128,128]{1,0:T(8,128)S(1)} %bitcast_select_fusion.1), custom_call_target="Cholesky" | custom-call | tf_op jit(solution)/shard_map/cholesky/custom-call.1 | solution.py:28
  45.7 0.6 compare_reduce_fusion.1
  46.4 0.7 select_bitcast_fusion.2
  47.0 9.8 %custom-call.9 = f32[1,128,128]{1,2,0:T(8,128)S(1)} custom-call(f32[1,128,128]{2,1,0:T(8,128)S(1)} %get-tuple-element.8), custom_call_target="InvertDiagBlocksLowerTriangular" | custom-call | tf_op jit(solution)/shard_map/triangular_solve/custom-call.0 | solution.py:29
  58.1 11.7 %custom-call.10 = f32[128,128]{1,0:T(8,128)S(1)} custom-call(f32[128,128]{1,0:T(8,128)S(1)} %fusion.24), custom_call_target="Cholesky" | custom-call | tf_op jit(solution)/shard_map/cholesky/custom-call.1 | solution.py:31
  69.9 0.6 compare_reduce_fusion
  70.5 0.7 select_bitcast_fusion.1
  71.2 9.8 %custom-call.11 = f32[1,128,128]{1,2,0:T(8,128)S(1)} custom-call(f32[1,128,128]{2,1,0:T(8,128)S(1)} %get-tuple-element.6), custom_call_target="InvertDiagBlocksLowerTriangular" | custom-call | tf_op jit(solution)/shard_map/triangular_solve/custom-call.0 | solution.py:32
  81.7 0.8 copy.14
  82.5 3.2 %convolution_multiply_fusion = f32[2048,256]{1,0:T(8,128)} fusion(f32[2048,256]{1,0:T(8,128)S(1)} %fusion.1, f32[128,128]{1,0:T(8,128)S(1)} %fusion.17, f32[128,128]{1,0:T(8,128)S(1)} %copy.13, f32[128,128]{1,0:T(8,128)S(1)} %convolution_negate_fusion), kind=kOutput, calls=%fused_computation.2 | convolution fusion | flops 1611399168 | bytes 4390912 | tf_op jit(solution)/shard_map/dot_general | solution.py:22
  (39 shorter events, 5.0 us)
Async XLA Ops:
  0.6 1.1 %copy-start = (f32[2048,64]{0,1:T(8,128)S(1)}, f32[2048,64]{0,1:T(8,128)}, u32[]{:S(2)}) copy-start(f32[2048,64]{0,1:T(8,128)} %param.9) | copy-start | bytes 1572868
  6.3 5.3 %copy-start.2 = (s32[32]{0:T(128)S(1)}, s32[32]{0:T(128)}, u32[]{:S(2)}) copy-start(s32[32]{0:T(128)} %param.14) | copy-start | bytes 388
  6.3 5.3 %copy-start.1 = (f32[1,256,256]{2,1,0:T(8,128)S(1)}, f32[1,256,256]{2,1,0:T(8,128)}, u32[]{:S(2)}) copy-start(f32[1,256,256]{2,1,0:T(8,128)} %param.13) | copy-start | bytes 786436
  12.9 1.5 %collective-permute-start = (f32[136,128]{1,0:T(8,128)S(1)}, f32[136,128]{1,0:T(8,128)S(1)}, u32[]{:S(2)}, u32[]{:S(2)}) collective-permute-start(f32[136,128]{1,0:T(8,128)S(1)} %pad_select_fusion), channel_id=1, source_target_pairs={{0,1},{1,0},{2,3},{3,2},{4,5},{5,4},{6,7},{7,6},{8,9},{9,8},{10,11... | collective-permute-start | bytes 208904 | tf_op jit(solution)/shard_map/ppermute | solution.py:67
  14.5 6.4 %collective-permute-start.3 = (f32[136,128]{1,0:T(8,128)S(1)}, f32[136,128]{1,0:T(8,128)S(1)}, u32[]{:S(2)}, u32[]{:S(2)}) collective-permute-start(f32[136,128]{1,0:T(8,128)S(1)} %select_add_fusion), channel_id=1, source_target_pairs={{0,6},{1,7},{2,4},{3,5},{4,2},{5,3},{6,0},{7,1},{8,14},{9,15},{10,... | collective-permute-start | bytes 208904 | tf_op jit(solution)/shard_map/ppermute | solution.py:67
  18.4 4.3 %collective-permute-start.2 = (f32[136,128]{1,0:T(8,128)S(1)}, f32[136,128]{1,0:T(8,128)S(1)}, u32[]{:S(2)}, u32[]{:S(2)}) collective-permute-start(f32[136,128]{1,0:T(8,128)S(1)} %select_add_fusion), channel_id=1, source_target_pairs={{0,4},{1,5},{2,6},{3,7},{4,0},{5,1},{6,2},{7,3},{8,12},{9,13},{10,... | collective-permute-start | bytes 208904 | tf_op jit(solution)/shard_map/ppermute | solution.py:67
  18.9 4.3 %collective-permute-start.1 = (f32[136,128]{1,0:T(8,128)S(1)}, f32[136,128]{1,0:T(8,128)S(1)}, u32[]{:S(2)}, u32[]{:S(2)}) collective-permute-start(f32[136,128]{1,0:T(8,128)S(1)} %select_add_fusion), channel_id=1, source_target_pairs={{0,2},{1,3},{2,0},{3,1},{4,6},{5,7},{6,4},{7,5},{8,10},{9,11},{10,... | collective-permute-start | bytes 208904 | tf_op jit(solution)/shard_map/ppermute | solution.py:67
  23.2 6.4 %collective-permute-start.6 = (f32[136,128]{1,0:T(8,128)S(1)}, f32[136,128]{1,0:T(8,128)S(1)}, u32[]{:S(2)}, u32[]{:S(2)}) collective-permute-start(f32[136,128]{1,0:T(8,128)S(1)} %add_add_fusion.1), channel_id=1, source_target_pairs={{0,24},{1,25},{2,26},{3,27},{4,28},{5,29},{6,30},{7,31},{8,16},{9,... | collective-permute-start | bytes 208904 | tf_op jit(solution)/shard_map/ppermute | solution.py:67
  26.9 5.4 %collective-permute-start.5 = (f32[136,128]{1,0:T(8,128)S(1)}, f32[136,128]{1,0:T(8,128)S(1)}, u32[]{:S(2)}, u32[]{:S(2)}) collective-permute-start(f32[136,128]{1,0:T(8,128)S(1)} %add_add_fusion.1), channel_id=1, source_target_pairs={{0,16},{1,17},{2,18},{3,19},{4,20},{5,21},{6,22},{7,23},{8,24},{9,... | collective-permute-start | bytes 208904 | tf_op jit(solution)/shard_map/ppermute | solution.py:67
  26.9 5.4 %collective-permute-start.4 = (f32[136,128]{1,0:T(8,128)S(1)}, f32[136,128]{1,0:T(8,128)S(1)}, u32[]{:S(2)}, u32[]{:S(2)}) collective-permute-start(f32[136,128]{1,0:T(8,128)S(1)} %add_add_fusion.1), channel_id=1, source_target_pairs={{0,8},{1,9},{2,10},{3,11},{4,12},{5,13},{6,14},{7,15},{8,0},{9,1},... | collective-permute-start | bytes 208904 | tf_op jit(solution)/shard_map/ppermute | solution.py:67
  32.4 1.3 %collective-permute-start.7 = (f32[136,128]{1,0:T(8,128)S(1)}, f32[136,128]{1,0:T(8,128)S(1)}, u32[]{:S(2)}, u32[]{:S(2)}) collective-permute-start(f32[136,128]{1,0:T(8,128)S(1)} %add_add_fusion), channel_id=1, source_target_pairs={{0,1},{1,0},{2,3},{3,2},{4,5},{5,4},{6,7},{7,6},{8,9},{9,8},{10,11... | collective-permute-start | bytes 208904 | tf_op jit(solution)/shard_map/ppermute | solution.py:67

commit v10 on v8

--- a/solution.py
+++ b/solution.py
@@ -14,14 +14,27 @@
     return jnp.dot(a, b, precision=lax.Precision.HIGHEST)
 
 
+def shared_inverse(lower):
+    q = lower.shape[0] // 2
+    low = (lax.axis_index("grp") * lax.axis_size("leaf") + lax.axis_index("leaf")) % 2 == 0
+    block = jnp.where(low, lower[:q, :q], lower[q:, q:])
+    mine = lax.linalg.triangular_solve(
+        block, jnp.eye(q, dtype=lower.dtype), left_side=True, lower=True
+    )
+    other = flip(mine, 1)
+    top = jnp.where(low, mine, other)
+    bottom = jnp.where(low, other, mine)
+    corner = -mm(bottom, mm(lower[q:, :q], top))
+    zero = jnp.zeros_like(top)
+    return jnp.block([[top, zero], [corner, bottom]])
+
+
 def cholesky_and_inverse(g11, g21, g22):
-    h = g11.shape[0]
-    eye = jnp.eye(h, dtype=g11.dtype)
     l11 = lax.linalg.cholesky(g11, symmetrize_input=False)
-    i11 = lax.linalg.triangular_solve(l11, eye, left_side=True, lower=True)
+    i11 = shared_inverse(l11)
     l21 = mm(g21, i11.T)
     l22 = lax.linalg.cholesky(g22 - mm(l21, l21.T), symmetrize_input=False)
-    i22 = lax.linalg.triangular_solve(l22, eye, left_side=True, lower=True)
+    i22 = shared_inverse(l22)
     i21 = -mm(i22, mm(l21, i11))
     zero = jnp.zeros_like(l11)
     lower = jnp.block([[l11, zero], [l21, l22]])

time: 84 us -> 76.6 us (0.912)
  other arithmetic: 46.2 us -> 36.5 us
  waiting for transfers between devices: 11 us -> 12.3 us
    another operation x4, other arithmetic: 20.9 us -> 9.95 us  [shared_inverse(): lax.linalg.triangular_solve(block, jnp.eye(q, dtype=lower.dtype), left_si...]
    select_n x0 -> x4, other arithmetic: none -> 1.33 us  [the longest x1 0.66 us: cholesky_and_inverse(): l11 = lax.linalg.cholesky(g11, symmetrize_input=False)]
    ppermute x8 -> x10, waiting for transfers between devices: 11 us -> 12.3 us  [flip(): return lax.ppermute(array, axes, [(i, i ^ mask) for i in range(count)])]
    dot_general x4 -> x8, matrix products: 1.13 us -> 1.74 us  [mm(): return jnp.dot(a, b, precision=lax.Precision.HIGHEST)]
    ppermute x8 -> x10, starting transfers between devices: 9.57 us -> 10 us  [flip(): return lax.ppermute(array, axes, [(i, i ^ mask) for i in range(count)])]
  transfers between devices with their start and end apart: 8 -> 10, of which waited for: 7 -> 9; matrix products, arithmetic and copies ran while one was open for 0% -> 1% of each run, Pallas kernels for 0% -> 0%
where the time goes in v10:
time: 76.6 us; the launch traced here: 76.3 us
  other arithmetic  36.5 us (48%)
  matrix products  14.1 us (18%)
  waiting for transfers between devices  12.3 us (16%)
  starting transfers between devices  10 us (13%)
  local copies, waits for them, and re-layouts  1.82 us (2%)
  between operations  1.58 us (2%)
    another operation x3, other arithmetic, cholesky_and_inverse(): l11 = lax.linalg.cholesky(g11, symmetrize_input=False)  12.5 us
    another operation x3, other arithmetic, cholesky_and_inverse(): l22 = lax.linalg.cholesky(g22 - mm(l21, l21.T), symmetrize_input=False)  12.4 us
    ppermute x10, waiting for transfers between devices, flip(): return lax.ppermute(array, axes, [(i, i ^ mask) for i in range(count)])  12.3 us
    ppermute x10, starting transfers between devices, flip(): return lax.ppermute(array, axes, [(i, i ^ mask) for i in range(count)])  10 us
    another operation x4, other arithmetic, shared_inverse(): lax.linalg.triangular_solve(block, jnp.eye(q, dtype=lower.dtype), left_si...  9.95 us
    dot_general x1, matrix products, per_device(): jnp.dot(inputs, freqs, precision=lax.Precision.HIGHEST) + phases[None, :]  4.59 us
    dot_general x1, matrix products, per_device(): lax.dot_general(features, features, (((0,), (0,)), ((), ())), precision=l...  3.48 us
    dot_general x1, matrix products, per_device(): lax.dot_general(features, inverse, (((1,), (1,)), ((), ())), precision=la...  3.18 us
  transfers between devices with their start and end apart: 10, of which 9 were waited for; matrix products, arithmetic and copies ran while one was open for 1% of the time, Pallas kernels for 0%

profile of v10, /device:TPU:0, one launch (start us, length us, event | category | flops | bytes accessed | tf_op | source)
XLA Modules:
  0.0 76.3 jit_solution(543809150399423407)
XLA Ops:
  1.4 0.7 sqrt.3
  2.1 4.6 %fusion.1 = f32[2048,256]{1,0:T(8,128)S(1)} fusion(f32[2048,64]{0,1:T(8,128)S(1)} %copy-done, f32[64,256]{1,0:T(8,128)} %param.10, f32[256]{0:T(256)} %param.11, f32[2048]{0:T(1024)S(1)} %sqrt.3), kind=kOutput, calls=%fused_computation.5 | convolution fusion | flops 417857536 | bytes 2696192 | tf_op jit(solution)/shard_map/dot_general | solution.py:121
  6.7 3.5 %fusion.48 = f32[256,256]{1,0:T(8,128)S(1)} fusion(f32[2048,256]{1,0:T(8,128)S(1)} %fusion.1), kind=kOutput, calls=%fused_computation.90 | convolution fusion | flops 1610612736 | bytes 2359296 | tf_op jit(solution)/shard_map/dot_general | solution.py:123
  10.2 0.6 convolution_add_fusion.1
  11.6 0.9 %collective-permute-done = f32[136,128]{1,0:T(8,128)S(1)} collective-permute-done((f32[136,128]{1,0:T(8,128)S(1)}, f32[136,128]{1,0:T(8,128)S(1)}, u32[]{:S(2)}, u32[]{:S(2)}) %collective-permute-start) | collective-permute-done | bytes 69664 | tf_op jit(solution)/shard_map/ppermute | solution.py:72
  12.6 3.8 %collective-permute-start.3 = (f32[136,128]{1,0:T(8,128)S(1)}, f32[136,128]{1,0:T(8,128)S(1)}, u32[]{:S(2)}, u32[]{:S(2)}) collective-permute-start(f32[136,128]{1,0:T(8,128)S(1)} %select_add_fusion), channel_id=1, source_target_pairs={{0,6},{1,7},{2,4},{3,5},{4,2},{5,3},{6,0},{7,1},{8,14},{9,15},{10,... | collective-permute-start | bytes 208904 | tf_op jit(solution)/shard_map/ppermute | solution.py:72
  17.0 1.9 %collective-permute-done.3 = f32[136,128]{1,0:T(8,128)S(1)} collective-permute-done((f32[136,128]{1,0:T(8,128)S(1)}, f32[136,128]{1,0:T(8,128)S(1)}, u32[]{:S(2)}, u32[]{:S(2)}) %collective-permute-start.3) | collective-permute-done | bytes 69664 | tf_op jit(solution)/shard_map/ppermute | solution.py:72
  19.0 1.7 %collective-permute-done.2 = f32[136,128]{1,0:T(8,128)S(1)} collective-permute-done((f32[136,128]{1,0:T(8,128)S(1)}, f32[136,128]{1,0:T(8,128)S(1)}, u32[]{:S(2)}, u32[]{:S(2)}) %collective-permute-start.2) | collective-permute-done | bytes 69664 | tf_op jit(solution)/shard_map/ppermute | solution.py:72
  21.3 3.7 %collective-permute-start.6 = (f32[136,128]{1,0:T(8,128)S(1)}, f32[136,128]{1,0:T(8,128)S(1)}, u32[]{:S(2)}, u32[]{:S(2)}) collective-permute-start(f32[136,128]{1,0:T(8,128)S(1)} %add_add_fusion.1), channel_id=1, source_target_pairs={{0,24},{1,25},{2,26},{3,27},{4,28},{5,29},{6,30},{7,31},{8,16},{9,... | collective-permute-start | bytes 208904 | tf_op jit(solution)/shard_map/ppermute | solution.py:72
  24.9 0.8 %collective-permute-start.4 = (f32[136,128]{1,0:T(8,128)S(1)}, f32[136,128]{1,0:T(8,128)S(1)}, u32[]{:S(2)}, u32[]{:S(2)}) collective-permute-start(f32[136,128]{1,0:T(8,128)S(1)} %add_add_fusion.1), channel_id=1, source_target_pairs={{0,8},{1,9},{2,10},{3,11},{4,12},{5,13},{6,14},{7,15},{8,0},{9,1},... | collective-permute-start | bytes 208904 | tf_op jit(solution)/shard_map/ppermute | solution.py:72
  25.7 2.0 %collective-permute-done.6 = f32[136,128]{1,0:T(8,128)S(1)} collective-permute-done((f32[136,128]{1,0:T(8,128)S(1)}, f32[136,128]{1,0:T(8,128)S(1)}, u32[]{:S(2)}, u32[]{:S(2)}) %collective-permute-start.6) | collective-permute-done | bytes 69664 | tf_op jit(solution)/shard_map/ppermute | solution.py:72
  27.7 2.7 %collective-permute-done.5 = f32[136,128]{1,0:T(8,128)S(1)} collective-permute-done((f32[136,128]{1,0:T(8,128)S(1)}, f32[136,128]{1,0:T(8,128)S(1)}, u32[]{:S(2)}, u32[]{:S(2)}) %collective-permute-start.5) | collective-permute-done | bytes 69664 | tf_op jit(solution)/shard_map/ppermute | solution.py:72
  30.5 1.2 %collective-permute-done.7 = f32[136,128]{1,0:T(8,128)S(1)} collective-permute-done((f32[136,128]{1,0:T(8,128)S(1)}, f32[136,128]{1,0:T(8,128)S(1)}, u32[]{:S(2)}, u32[]{:S(2)}) %collective-permute-start.7) | collective-permute-done | bytes 69664 | tf_op jit(solution)/shard_map/ppermute | solution.py:72
  31.9 11.8 %custom-call.8 = f32[128,128]{1,0:T(8,128)S(1)} custom-call(f32[128,128]{1,0:T(8,128)S(1)} %bitcast_select_fusion.1), custom_call_target="Cholesky" | custom-call | tf_op jit(solution)/shard_map/cholesky/custom-call.1 | solution.py:33
  43.7 0.6 compare_reduce_fusion.1
  44.4 0.7 select_select_fusion.1
  45.1 4.9 %custom-call.9 = f32[1,64,64]{1,2,0:T(8,128)S(1)} custom-call(f32[1,64,64]{2,1,0:T(8,128)S(1)} %fusion.39), custom_call_target="InvertDiagBlocksLowerTriangular" | custom-call | tf_op jit(solution)/shard_map/triangular_solve/custom-call.0 | solution.py:21
  50.5 1.0 %collective-permute-done.8 = f32[64,64]{1,0:T(8,128)S(1)} collective-permute-done((f32[64,64]{1,0:T(8,128)S(1)}, f32[64,64]{1,0:T(8,128)S(1)}, u32[]{:S(2)}, u32[]{:S(2)}) %collective-permute-start.8) | collective-permute-done | bytes 16416 | tf_op jit(solution)/shard_map/ppermute | solution.py:72
  52.9 11.7 %custom-call.10 = f32[128,128]{1,0:T(8,128)S(1)} custom-call(f32[128,128]{1,0:T(8,128)S(1)} %fusion.25), custom_call_target="Cholesky" | custom-call | tf_op jit(solution)/shard_map/cholesky/custom-call.1 | solution.py:36
  64.7 0.6 compare_reduce_fusion
  65.3 0.7 select_select_fusion
  66.1 4.9 %custom-call.11 = f32[1,64,64]{1,2,0:T(8,128)S(1)} custom-call(f32[1,64,64]{2,1,0:T(8,128)S(1)} %fusion.35), custom_call_target="InvertDiagBlocksLowerTriangular" | custom-call | tf_op jit(solution)/shard_map/triangular_solve/custom-call.0 | solution.py:21
  71.5 0.8 %copy.10 = f32[256,256]{1,0:T(8,128)} copy(f32[256,256]{0,1:T(8,128)S(1)} %fusion.3) | data formatting | bytes 524288
  73.1 3.2 %convolution_multiply_fusion = f32[2048,256]{1,0:T(8,128)} fusion(f32[2048,256]{1,0:T(8,128)S(1)} %fusion.1, f32[128,128]{1,0:T(8,128)S(1)} %select_maximum_fusion.3, f32[64,64]{1,0:T(8,128)S(1)} %get-tuple-element.10, f32[64,64]{1,0:T(8,128)S(1)} %convolution_negate_fusion.1, f32[64,128]{1,0:T(8,128)S(1)} %concatenate.57, ...), kind=kOutput, calls=%fused_computation.2 | convolution fusion | flops 1611530240 | bytes 4390912 | tf_op jit(solution)/shard_map/dot_general | solution.py:133
  (46 shorter events, 5.6 us)
Async XLA Ops:
  0.6 1.4 %copy-start = (f32[2048,64]{0,1:T(8,128)S(1)}, f32[2048,64]{0,1:T(8,128)}, u32[]{:S(2)}) copy-start(f32[2048,64]{0,1:T(8,128)} %param.9) | copy-start | bytes 1572868
  6.7 3.5 %copy-start.1 = (f32[1,256,256]{2,1,0:T(8,128)S(1)}, f32[1,256,256]{2,1,0:T(8,128)}, u32[]{:S(2)}) copy-start(f32[1,256,256]{2,1,0:T(8,128)} %param.13) | copy-start | bytes 786436
  11.0 1.5 %collective-permute-start = (f32[136,128]{1,0:T(8,128)S(1)}, f32[136,128]{1,0:T(8,128)S(1)}, u32[]{:S(2)}, u32[]{:S(2)}) collective-permute-start(f32[136,128]{1,0:T(8,128)S(1)} %pad_select_fusion), channel_id=1, source_target_pairs={{0,1},{1,0},{2,3},{3,2},{4,5},{5,4},{6,7},{7,6},{8,9},{9,8},{10,11... | collective-permute-start | bytes 208904 | tf_op jit(solution)/shard_map/ppermute | solution.py:72
  12.6 6.4 %collective-permute-start.3 = (f32[136,128]{1,0:T(8,128)S(1)}, f32[136,128]{1,0:T(8,128)S(1)}, u32[]{:S(2)}, u32[]{:S(2)}) collective-permute-start(f32[136,128]{1,0:T(8,128)S(1)} %select_add_fusion), channel_id=1, source_target_pairs={{0,6},{1,7},{2,4},{3,5},{4,2},{5,3},{6,0},{7,1},{8,14},{9,15},{10,... | collective-permute-start | bytes 208904 | tf_op jit(solution)/shard_map/ppermute | solution.py:72
  16.4 4.3 %collective-permute-start.2 = (f32[136,128]{1,0:T(8,128)S(1)}, f32[136,128]{1,0:T(8,128)S(1)}, u32[]{:S(2)}, u32[]{:S(2)}) collective-permute-start(f32[136,128]{1,0:T(8,128)S(1)} %select_add_fusion), channel_id=1, source_target_pairs={{0,4},{1,5},{2,6},{3,7},{4,0},{5,1},{6,2},{7,3},{8,12},{9,13},{10,... | collective-permute-start | bytes 208904 | tf_op jit(solution)/shard_map/ppermute | solution.py:72
  16.9 4.3 %collective-permute-start.1 = (f32[136,128]{1,0:T(8,128)S(1)}, f32[136,128]{1,0:T(8,128)S(1)}, u32[]{:S(2)}, u32[]{:S(2)}) collective-permute-start(f32[136,128]{1,0:T(8,128)S(1)} %select_add_fusion), channel_id=1, source_target_pairs={{0,2},{1,3},{2,0},{3,1},{4,6},{5,7},{6,4},{7,5},{8,10},{9,11},{10,... | collective-permute-start | bytes 208904 | tf_op jit(solution)/shard_map/ppermute | solution.py:72
  21.3 6.4 %collective-permute-start.6 = (f32[136,128]{1,0:T(8,128)S(1)}, f32[136,128]{1,0:T(8,128)S(1)}, u32[]{:S(2)}, u32[]{:S(2)}) collective-permute-start(f32[136,128]{1,0:T(8,128)S(1)} %add_add_fusion.1), channel_id=1, source_target_pairs={{0,24},{1,25},{2,26},{3,27},{4,28},{5,29},{6,30},{7,31},{8,16},{9,... | collective-permute-start | bytes 208904 | tf_op jit(solution)/shard_map/ppermute | solution.py:72
  24.9 5.5 %collective-permute-start.5 = (f32[136,128]{1,0:T(8,128)S(1)}, f32[136,128]{1,0:T(8,128)S(1)}, u32[]{:S(2)}, u32[]{:S(2)}) collective-permute-start(f32[136,128]{1,0:T(8,128)S(1)} %add_add_fusion.1), channel_id=1, source_target_pairs={{0,16},{1,17},{2,18},{3,19},{4,20},{5,21},{6,22},{7,23},{8,24},{9,... | collective-permute-start | bytes 208904 | tf_op jit(solution)/shard_map/ppermute | solution.py:72
  24.9 5.5 %collective-permute-start.4 = (f32[136,128]{1,0:T(8,128)S(1)}, f32[136,128]{1,0:T(8,128)S(1)}, u32[]{:S(2)}, u32[]{:S(2)}) collective-permute-start(f32[136,128]{1,0:T(8,128)S(1)} %add_add_fusion.1), channel_id=1, source_target_pairs={{0,8},{1,9},{2,10},{3,11},{4,12},{5,13},{6,14},{7,15},{8,0},{9,1},... | collective-permute-start | bytes 208904 | tf_op jit(solution)/shard_map/ppermute | solution.py:72
  30.4 1.3 %collective-permute-start.7 = (f32[136,128]{1,0:T(8,128)S(1)}, f32[136,128]{1,0:T(8,128)S(1)}, u32[]{:S(2)}, u32[]{:S(2)}) collective-permute-start(f32[136,128]{1,0:T(8,128)S(1)} %add_add_fusion), channel_id=1, source_target_pairs={{0,1},{1,0},{2,3},{3,2},{4,5},{5,4},{6,7},{7,6},{8,9},{9,8},{10,11... | collective-permute-start | bytes 208904 | tf_op jit(solution)/shard_map/ppermute | solution.py:72
  50.3 1.3 %collective-permute-start.8 = (f32[64,64]{1,0:T(8,128)S(1)}, f32[64,64]{1,0:T(8,128)S(1)}, u32[]{:S(2)}, u32[]{:S(2)}) collective-permute-start(f32[64,64]{1,0:T(8,128)S(1)} %fusion.30), channel_id=1, source_target_pairs={{0,1},{1,0},{2,3},{3,2},{4,5},{5,4},{6,7},{7,6},{8,9},{9,8},{10,11... | collective-permute-start | bytes 49160 | tf_op jit(solution)/shard_map/ppermute | solution.py:72
  71.2 1.3 %collective-permute-start.9 = (f32[64,64]{1,0:T(8,128)S(1)}, f32[64,64]{1,0:T(8,128)S(1)}, u32[]{:S(2)}, u32[]{:S(2)}) collective-permute-start(f32[64,64]{1,0:T(8,128)S(1)} %fusion.28), channel_id=1, source_target_pairs={{0,1},{1,0},{2,3},{3,2},{4,5},{5,4},{6,7},{7,6},{8,9},{9,8},{10,11... | collective-permute-start | bytes 49160 | tf_op jit(solution)/shard_map/ppermute | solution.py:72

commit v11 on v10

--- a/solution.py
+++ b/solution.py
@@ -115,14 +115,24 @@
     return jnp.where(jnp.floor(half) == half, value, -value)
 
 
+def split_gram(f):
+    def tdot(a, b):
+        return lax.dot_general(a, b, (((0,), (0,)), ((), ())), preferred_element_type=jnp.float32)
+
+    high = f.astype(jnp.bfloat16)
+    rest = f - high.astype(jnp.float32)
+    mid = rest.astype(jnp.bfloat16)
+    low = (rest - mid.astype(jnp.float32)).astype(jnp.bfloat16)
+    cross = tdot(high, mid) + tdot(high, low)
+    return tdot(high, high) + (cross + cross.T) + tdot(mid, mid)
+
+
 def per_device(inputs, freqs, phases, sample_weight, stored, root):
     total_rows = inputs.shape[0] * lax.axis_size("grp") * lax.axis_size("leaf")
     norm_scale = 1.0 / math.sqrt(total_rows)
     proj = jnp.dot(inputs, freqs, precision=lax.Precision.HIGHEST) + phases[None, :]
     features = jnp.sqrt(sample_weight)[:, None] * bounded_cos(proj) * norm_scale
-    gram = lax.dot_general(
-        features, features, (((0,), (0,)), ((), ())), precision=lax.Precision.HIGHEST
-    )
+    gram = split_gram(features)
     slot = lax.axis_index("grp") * lax.axis_size("leaf") + lax.axis_index("leaf")
     running = jnp.where(slot == root[0], stored[0], jnp.zeros_like(stored[0]))
     gram = gram + lax.dot_general(

time: 76.6 us -> 75.3 us (0.983)
  matrix products: 14.1 us -> 12.8 us
    dot_general x1 -> x4, matrix products: 3.48 us -> 2 us  [tdot(): lax.dot_general(a, b, (((0,), (0,)), ((), ())), preferred_element_type=jn...]
where the time goes in v11:
time: 75.3 us; the launch traced here: 75.1 us
  other arithmetic  36.4 us (48%)
  matrix products  12.8 us (17%)
  waiting for transfers between devices  12.3 us (16%)
  starting transfers between devices  10 us (13%)
  local copies, waits for them, and re-layouts  1.95 us (3%)
  between operations  1.62 us (2%)
    another operation x3, other arithmetic, cholesky_and_inverse(): l22 = lax.linalg.cholesky(g22 - mm(l21, l21.T), symmetrize_input=False)  12.4 us
    another operation x3, other arithmetic, cholesky_and_inverse(): l11 = lax.linalg.cholesky(g11, symmetrize_input=False)  12.4 us
    ppermute x10, waiting for transfers between devices, flip(): return lax.ppermute(array, axes, [(i, i ^ mask) for i in range(count)])  12.3 us
    ppermute x10, starting transfers between devices, flip(): return lax.ppermute(array, axes, [(i, i ^ mask) for i in range(count)])  10 us
    another operation x4, other arithmetic, shared_inverse(): lax.linalg.triangular_solve(block, jnp.eye(q, dtype=lower.dtype), left_si...  9.95 us
    dot_general x1, matrix products, per_device(): jnp.dot(inputs, freqs, precision=lax.Precision.HIGHEST) + phases[None, :]  4.59 us
    dot_general x1, matrix products, per_device(): lax.dot_general(features, inverse, (((1,), (1,)), ((), ())), precision=la...  3.18 us
    dot_general x4, matrix products, tdot(): lax.dot_general(a, b, (((0,), (0,)), ((), ())), preferred_element_type=jn...  2 us
  transfers between devices with their start and end apart: 10, of which 9 were waited for; matrix products, arithmetic and copies ran while one was open for 1% of the time, Pallas kernels for 0%

profile of v11, /device:TPU:0, one launch (start us, length us, event | category | flops | bytes accessed | tf_op | source)
XLA Modules:
  0.0 75.1 jit_solution(2937093763684266460)
XLA Ops:
  1.4 0.7 sqrt.3
  2.1 4.6 %fusion.1 = f32[2048,256]{1,0:T(8,128)S(1)} fusion(f32[2048,64]{0,1:T(8,128)S(1)} %copy-done, f32[64,256]{1,0:T(8,128)} %param.10, f32[256]{0:T(256)} %param.11, f32[2048]{0:T(1024)S(1)} %sqrt.3), kind=kOutput, calls=%fused_computation.5 | convolution fusion | flops 417857536 | bytes 2696192 | tf_op jit(solution)/shard_map/dot_general | solution.py:133
  8.9 0.6 convolution_add_fusion.1
  9.7 0.6 collective-permute-start
  10.2 0.9 %collective-permute-done = f32[136,128]{1,0:T(8,128)S(1)} collective-permute-done((f32[136,128]{1,0:T(8,128)S(1)}, f32[136,128]{1,0:T(8,128)S(1)}, u32[]{:S(2)}, u32[]{:S(2)}) %collective-permute-start) | collective-permute-done | bytes 69664 | tf_op jit(solution)/shard_map/ppermute | solution.py:72
  11.2 3.9 %collective-permute-start.3 = (f32[136,128]{1,0:T(8,128)S(1)}, f32[136,128]{1,0:T(8,128)S(1)}, u32[]{:S(2)}, u32[]{:S(2)}) collective-permute-start(f32[136,128]{1,0:T(8,128)S(1)} %select_add_fusion), channel_id=1, source_target_pairs={{0,6},{1,7},{2,4},{3,5},{4,2},{5,3},{6,0},{7,1},{8,14},{9,15},{10,... | collective-permute-start | bytes 208904 | tf_op jit(solution)/shard_map/ppermute | solution.py:72
  15.7 1.9 %collective-permute-done.3 = f32[136,128]{1,0:T(8,128)S(1)} collective-permute-done((f32[136,128]{1,0:T(8,128)S(1)}, f32[136,128]{1,0:T(8,128)S(1)}, u32[]{:S(2)}, u32[]{:S(2)}) %collective-permute-start.3) | collective-permute-done | bytes 69664 | tf_op jit(solution)/shard_map/ppermute | solution.py:72
  17.7 1.7 %collective-permute-done.2 = f32[136,128]{1,0:T(8,128)S(1)} collective-permute-done((f32[136,128]{1,0:T(8,128)S(1)}, f32[136,128]{1,0:T(8,128)S(1)}, u32[]{:S(2)}, u32[]{:S(2)}) %collective-permute-start.2) | collective-permute-done | bytes 69664 | tf_op jit(solution)/shard_map/ppermute | solution.py:72
  19.9 3.7 %collective-permute-start.6 = (f32[136,128]{1,0:T(8,128)S(1)}, f32[136,128]{1,0:T(8,128)S(1)}, u32[]{:S(2)}, u32[]{:S(2)}) collective-permute-start(f32[136,128]{1,0:T(8,128)S(1)} %add_add_fusion.1), channel_id=1, source_target_pairs={{0,24},{1,25},{2,26},{3,27},{4,28},{5,29},{6,30},{7,31},{8,16},{9,... | collective-permute-start | bytes 208904 | tf_op jit(solution)/shard_map/ppermute | solution.py:72
  23.6 0.8 %collective-permute-start.4 = (f32[136,128]{1,0:T(8,128)S(1)}, f32[136,128]{1,0:T(8,128)S(1)}, u32[]{:S(2)}, u32[]{:S(2)}) collective-permute-start(f32[136,128]{1,0:T(8,128)S(1)} %add_add_fusion.1), channel_id=1, source_target_pairs={{0,8},{1,9},{2,10},{3,11},{4,12},{5,13},{6,14},{7,15},{8,0},{9,1},... | collective-permute-start | bytes 208904 | tf_op jit(solution)/shard_map/ppermute | solution.py:72
  24.4 2.0 %collective-permute-done.6 = f32[136,128]{1,0:T(8,128)S(1)} collective-permute-done((f32[136,128]{1,0:T(8,128)S(1)}, f32[136,128]{1,0:T(8,128)S(1)}, u32[]{:S(2)}, u32[]{:S(2)}) %collective-permute-start.6) | collective-permute-done | bytes 69664 | tf_op jit(solution)/shard_map/ppermute | solution.py:72
  26.4 2.7 %collective-permute-done.5 = f32[136,128]{1,0:T(8,128)S(1)} collective-permute-done((f32[136,128]{1,0:T(8,128)S(1)}, f32[136,128]{1,0:T(8,128)S(1)}, u32[]{:S(2)}, u32[]{:S(2)}) %collective-permute-start.5) | collective-permute-done | bytes 69664 | tf_op jit(solution)/shard_map/ppermute | solution.py:72
  29.2 1.2 %collective-permute-done.7 = f32[136,128]{1,0:T(8,128)S(1)} collective-permute-done((f32[136,128]{1,0:T(8,128)S(1)}, f32[136,128]{1,0:T(8,128)S(1)}, u32[]{:S(2)}, u32[]{:S(2)}) %collective-permute-start.7) | collective-permute-done | bytes 69664 | tf_op jit(solution)/shard_map/ppermute | solution.py:72
  30.6 11.7 %custom-call.8 = f32[128,128]{1,0:T(8,128)S(1)} custom-call(f32[128,128]{1,0:T(8,128)S(1)} %bitcast_select_fusion.1), custom_call_target="Cholesky" | custom-call | tf_op jit(solution)/shard_map/cholesky/custom-call.1 | solution.py:33
  42.3 0.6 compare_reduce_fusion.1
  43.0 0.7 select_select_fusion.1
  43.7 4.9 %custom-call.9 = f32[1,64,64]{1,2,0:T(8,128)S(1)} custom-call(f32[1,64,64]{2,1,0:T(8,128)S(1)} %fusion.61), custom_call_target="InvertDiagBlocksLowerTriangular" | custom-call | tf_op jit(solution)/shard_map/triangular_solve/custom-call.0 | solution.py:21
  49.1 1.0 %collective-permute-done.8 = f32[64,64]{1,0:T(8,128)S(1)} collective-permute-done((f32[64,64]{1,0:T(8,128)S(1)}, f32[64,64]{1,0:T(8,128)S(1)}, u32[]{:S(2)}, u32[]{:S(2)}) %collective-permute-start.8) | collective-permute-done | bytes 16416 | tf_op jit(solution)/shard_map/ppermute | solution.py:72
  51.7 11.7 %custom-call.10 = f32[128,128]{1,0:T(8,128)S(1)} custom-call(f32[128,128]{1,0:T(8,128)S(1)} %fusion.47), custom_call_target="Cholesky" | custom-call | tf_op jit(solution)/shard_map/cholesky/custom-call.1 | solution.py:36
  63.4 0.6 compare_reduce_fusion
  64.1 0.7 select_select_fusion
  64.8 4.9 %custom-call.11 = f32[1,64,64]{1,2,0:T(8,128)S(1)} custom-call(f32[1,64,64]{2,1,0:T(8,128)S(1)} %fusion.57), custom_call_target="InvertDiagBlocksLowerTriangular" | custom-call | tf_op jit(solution)/shard_map/triangular_solve/custom-call.0 | solution.py:21
  70.2 0.8 %copy.13 = f32[256,256]{1,0:T(8,128)} copy(f32[256,256]{0,1:T(8,128)S(1)} %fusion.25) | data formatting | bytes 524288
  71.9 3.2 %convolution_multiply_fusion = f32[2048,256]{1,0:T(8,128)} fusion(f32[2048,256]{1,0:T(8,128)S(1)} %fusion.1, f32[128,128]{1,0:T(8,128)S(1)} %select_maximum_fusion.3, f32[64,64]{1,0:T(8,128)S(1)} %get-tuple-element.10, f32[64,64]{1,0:T(8,128)S(1)} %convolution_negate_fusion.1, f32[64,128]{1,0:T(8,128)S(1)} %concatenate.57, ...), kind=kOutput, calls=%fused_computation.2 | convolution fusion | flops 1611530240 | bytes 4390912 | tf_op jit(solution)/shard_map/dot_general | solution.py:143
  (50 shorter events, 7.3 us)
Async XLA Ops:
  0.6 1.4 %copy-start = (f32[2048,64]{0,1:T(8,128)S(1)}, f32[2048,64]{0,1:T(8,128)}, u32[]{:S(2)}) copy-start(f32[2048,64]{0,1:T(8,128)} %param.9) | copy-start | bytes 1572868
  7.9 1.0 %copy-start.1 = (f32[1,256,256]{2,1,0:T(8,128)S(1)}, f32[1,256,256]{2,1,0:T(8,128)}, u32[]{:S(2)}) copy-start(f32[1,256,256]{2,1,0:T(8,128)} %param.13) | copy-start | bytes 786436
  9.7 1.5 %collective-permute-start = (f32[136,128]{1,0:T(8,128)S(1)}, f32[136,128]{1,0:T(8,128)S(1)}, u32[]{:S(2)}, u32[]{:S(2)}) collective-permute-start(f32[136,128]{1,0:T(8,128)S(1)} %pad_select_fusion), channel_id=1, source_target_pairs={{0,1},{1,0},{2,3},{3,2},{4,5},{5,4},{6,7},{7,6},{8,9},{9,8},{10,11... | collective-permute-start | bytes 208904 | tf_op jit(solution)/shard_map/ppermute | solution.py:72
  11.2 6.4 %collective-permute-start.3 = (f32[136,128]{1,0:T(8,128)S(1)}, f32[136,128]{1,0:T(8,128)S(1)}, u32[]{:S(2)}, u32[]{:S(2)}) collective-permute-start(f32[136,128]{1,0:T(8,128)S(1)} %select_add_fusion), channel_id=1, source_target_pairs={{0,6},{1,7},{2,4},{3,5},{4,2},{5,3},{6,0},{7,1},{8,14},{9,15},{10,... | collective-permute-start | bytes 208904 | tf_op jit(solution)/shard_map/ppermute | solution.py:72
  15.1 4.3 %collective-permute-start.2 = (f32[136,128]{1,0:T(8,128)S(1)}, f32[136,128]{1,0:T(8,128)S(1)}, u32[]{:S(2)}, u32[]{:S(2)}) collective-permute-start(f32[136,128]{1,0:T(8,128)S(1)} %select_add_fusion), channel_id=1, source_target_pairs={{0,4},{1,5},{2,6},{3,7},{4,0},{5,1},{6,2},{7,3},{8,12},{9,13},{10,... | collective-permute-start | bytes 208904 | tf_op jit(solution)/shard_map/ppermute | solution.py:72
  15.6 4.3 %collective-permute-start.1 = (f32[136,128]{1,0:T(8,128)S(1)}, f32[136,128]{1,0:T(8,128)S(1)}, u32[]{:S(2)}, u32[]{:S(2)}) collective-permute-start(f32[136,128]{1,0:T(8,128)S(1)} %select_add_fusion), channel_id=1, source_target_pairs={{0,2},{1,3},{2,0},{3,1},{4,6},{5,7},{6,4},{7,5},{8,10},{9,11},{10,... | collective-permute-start | bytes 208904 | tf_op jit(solution)/shard_map/ppermute | solution.py:72
  19.9 6.4 %collective-permute-start.6 = (f32[136,128]{1,0:T(8,128)S(1)}, f32[136,128]{1,0:T(8,128)S(1)}, u32[]{:S(2)}, u32[]{:S(2)}) collective-permute-start(f32[136,128]{1,0:T(8,128)S(1)} %add_add_fusion.1), channel_id=1, source_target_pairs={{0,24},{1,25},{2,26},{3,27},{4,28},{5,29},{6,30},{7,31},{8,16},{9,... | collective-permute-start | bytes 208904 | tf_op jit(solution)/shard_map/ppermute | solution.py:72
  23.6 5.5 %collective-permute-start.5 = (f32[136,128]{1,0:T(8,128)S(1)}, f32[136,128]{1,0:T(8,128)S(1)}, u32[]{:S(2)}, u32[]{:S(2)}) collective-permute-start(f32[136,128]{1,0:T(8,128)S(1)} %add_add_fusion.1), channel_id=1, source_target_pairs={{0,16},{1,17},{2,18},{3,19},{4,20},{5,21},{6,22},{7,23},{8,24},{9,... | collective-permute-start | bytes 208904 | tf_op jit(solution)/shard_map/ppermute | solution.py:72
  23.6 5.5 %collective-permute-start.4 = (f32[136,128]{1,0:T(8,128)S(1)}, f32[136,128]{1,0:T(8,128)S(1)}, u32[]{:S(2)}, u32[]{:S(2)}) collective-permute-start(f32[136,128]{1,0:T(8,128)S(1)} %add_add_fusion.1), channel_id=1, source_target_pairs={{0,8},{1,9},{2,10},{3,11},{4,12},{5,13},{6,14},{7,15},{8,0},{9,1},... | collective-permute-start | bytes 208904 | tf_op jit(solution)/shard_map/ppermute | solution.py:72
  29.1 1.3 %collective-permute-start.7 = (f32[136,128]{1,0:T(8,128)S(1)}, f32[136,128]{1,0:T(8,128)S(1)}, u32[]{:S(2)}, u32[]{:S(2)}) collective-permute-start(f32[136,128]{1,0:T(8,128)S(1)} %add_add_fusion), channel_id=1, source_target_pairs={{0,1},{1,0},{2,3},{3,2},{4,5},{5,4},{6,7},{7,6},{8,9},{9,8},{10,11... | collective-permute-start | bytes 208904 | tf_op jit(solution)/shard_map/ppermute | solution.py:72
  48.9 1.3 %collective-permute-start.8 = (f32[64,64]{1,0:T(8,128)S(1)}, f32[64,64]{1,0:T(8,128)S(1)}, u32[]{:S(2)}, u32[]{:S(2)}) collective-permute-start(f32[64,64]{1,0:T(8,128)S(1)} %fusion.52), channel_id=1, source_target_pairs={{0,1},{1,0},{2,3},{3,2},{4,5},{5,4},{6,7},{7,6},{8,9},{9,8},{10,11... | collective-permute-start | bytes 49160 | tf_op jit(solution)/shard_map/ppermute | solution.py:72
  70.0 1.3 %collective-permute-start.9 = (f32[64,64]{1,0:T(8,128)S(1)}, f32[64,64]{1,0:T(8,128)S(1)}, u32[]{:S(2)}, u32[]{:S(2)}) collective-permute-start(f32[64,64]{1,0:T(8,128)S(1)} %fusion.50), channel_id=1, source_target_pairs={{0,1},{1,0},{2,3},{3,2},{4,5},{5,4},{6,7},{7,6},{8,9},{9,8},{10,11... | collective-permute-start | bytes 49160 | tf_op jit(solution)/shard_map/ppermute | solution.py:72

commit v12 on v11

--- a/solution.py
+++ b/solution.py
@@ -119,10 +119,12 @@
     def tdot(a, b):
         return lax.dot_general(a, b, (((0,), (0,)), ((), ())), preferred_element_type=jnp.float32)
 
-    high = f.astype(jnp.bfloat16)
-    rest = f - high.astype(jnp.float32)
-    mid = rest.astype(jnp.bfloat16)
-    low = (rest - mid.astype(jnp.float32)).astype(jnp.bfloat16)
+    top = lax.reduce_precision(f, exponent_bits=8, mantissa_bits=7)
+    rest = f - top
+    middle = lax.reduce_precision(rest, exponent_bits=8, mantissa_bits=7)
+    high = top.astype(jnp.bfloat16)
+    mid = middle.astype(jnp.bfloat16)
+    low = (rest - middle).astype(jnp.bfloat16)
     cross = tdot(high, mid) + tdot(high, low)
     return tdot(high, high) + (cross + cross.T) + tdot(mid, mid)
 

time: 75.3 us -> 75.4 us (level)
  no operation moved by 1% of the time
where the time goes in v12:
time: 75.4 us; the launch traced here: 75.2 us
  other arithmetic  36.4 us (48%)
  matrix products  12.7 us (17%)
  waiting for transfers between devices  12.3 us (16%)
  starting transfers between devices  10.2 us (14%)
  local copies, waits for them, and re-layouts  1.95 us (3%)
  between operations  1.62 us (2%)
    another operation x3, other arithmetic, cholesky_and_inverse(): l22 = lax.linalg.cholesky(g22 - mm(l21, l21.T), symmetrize_input=False)  12.4 us
    another operation x3, other arithmetic, cholesky_and_inverse(): l11 = lax.linalg.cholesky(g11, symmetrize_input=False)  12.4 us
    ppermute x10, waiting for transfers between devices, flip(): return lax.ppermute(array, axes, [(i, i ^ mask) for i in range(count)])  12.3 us
    ppermute x10, starting transfers between devices, flip(): return lax.ppermute(array, axes, [(i, i ^ mask) for i in range(count)])  10.2 us
    another operation x4, other arithmetic, shared_inverse(): lax.linalg.triangular_solve(block, jnp.eye(q, dtype=lower.dtype), left_si...  9.95 us
    dot_general x1, matrix products, per_device(): jnp.dot(inputs, freqs, precision=lax.Precision.HIGHEST) + phases[None, :]  4.59 us
    dot_general x1, matrix products, per_device(): lax.dot_general(features, inverse, (((1,), (1,)), ((), ())), precision=la...  3.18 us
    dot_general x4, matrix products, tdot(): lax.dot_general(a, b, (((0,), (0,)), ((), ())), preferred_element_type=jn...  2.09 us
  transfers between devices with their start and end apart: 10, of which 9 were waited for; matrix products, arithmetic and copies ran while one was open for 1% of the time, Pallas kernels for 0%

profile of v12, /device:TPU:0, one launch (start us, length us, event | category | flops | bytes accessed | tf_op | source)
XLA Modules:
  0.0 75.2 jit_solution(12067912849806342217)
XLA Ops:
  1.4 0.7 sqrt.3
  2.1 4.6 %fusion.2 = f32[2048,256]{1,0:T(8,128)S(1)} fusion(f32[2048,64]{0,1:T(8,128)S(1)} %copy-done, f32[64,256]{1,0:T(8,128)} %param.10, f32[256]{0:T(256)} %param.11, f32[2048]{0:T(1024)S(1)} %sqrt.3), kind=kOutput, calls=%fused_computation.10 | convolution fusion | flops 417857536 | bytes 2696192 | tf_op jit(solution)/shard_map/dot_general | solution.py:135
  7.2 0.6 convolution_add_fusion.3
  8.9 0.6 convolution_add_fusion.1
  10.3 0.9 %collective-permute-done = f32[136,128]{1,0:T(8,128)S(1)} collective-permute-done((f32[136,128]{1,0:T(8,128)S(1)}, f32[136,128]{1,0:T(8,128)S(1)}, u32[]{:S(2)}, u32[]{:S(2)}) %collective-permute-start) | collective-permute-done | bytes 69664 | tf_op jit(solution)/shard_map/ppermute | solution.py:72
  11.3 3.9 %collective-permute-start.3 = (f32[136,128]{1,0:T(8,128)S(1)}, f32[136,128]{1,0:T(8,128)S(1)}, u32[]{:S(2)}, u32[]{:S(2)}) collective-permute-start(f32[136,128]{1,0:T(8,128)S(1)} %select_add_fusion), channel_id=1, source_target_pairs={{0,6},{1,7},{2,4},{3,5},{4,2},{5,3},{6,0},{7,1},{8,14},{9,15},{10,... | collective-permute-start | bytes 208904 | tf_op jit(solution)/shard_map/ppermute | solution.py:72
  15.8 1.9 %collective-permute-done.3 = f32[136,128]{1,0:T(8,128)S(1)} collective-permute-done((f32[136,128]{1,0:T(8,128)S(1)}, f32[136,128]{1,0:T(8,128)S(1)}, u32[]{:S(2)}, u32[]{:S(2)}) %collective-permute-start.3) | collective-permute-done | bytes 69664 | tf_op jit(solution)/shard_map/ppermute | solution.py:72
  17.8 1.7 %collective-permute-done.2 = f32[136,128]{1,0:T(8,128)S(1)} collective-permute-done((f32[136,128]{1,0:T(8,128)S(1)}, f32[136,128]{1,0:T(8,128)S(1)}, u32[]{:S(2)}, u32[]{:S(2)}) %collective-permute-start.2) | collective-permute-done | bytes 69664 | tf_op jit(solution)/shard_map/ppermute | solution.py:72
  20.0 3.7 %collective-permute-start.6 = (f32[136,128]{1,0:T(8,128)S(1)}, f32[136,128]{1,0:T(8,128)S(1)}, u32[]{:S(2)}, u32[]{:S(2)}) collective-permute-start(f32[136,128]{1,0:T(8,128)S(1)} %add_add_fusion.1), channel_id=1, source_target_pairs={{0,24},{1,25},{2,26},{3,27},{4,28},{5,29},{6,30},{7,31},{8,16},{9,... | collective-permute-start | bytes 208904 | tf_op jit(solution)/shard_map/ppermute | solution.py:72
  23.7 0.8 %collective-permute-start.4 = (f32[136,128]{1,0:T(8,128)S(1)}, f32[136,128]{1,0:T(8,128)S(1)}, u32[]{:S(2)}, u32[]{:S(2)}) collective-permute-start(f32[136,128]{1,0:T(8,128)S(1)} %add_add_fusion.1), channel_id=1, source_target_pairs={{0,8},{1,9},{2,10},{3,11},{4,12},{5,13},{6,14},{7,15},{8,0},{9,1},... | collective-permute-start | bytes 208904 | tf_op jit(solution)/shard_map/ppermute | solution.py:72
  24.5 2.0 %collective-permute-done.6 = f32[136,128]{1,0:T(8,128)S(1)} collective-permute-done((f32[136,128]{1,0:T(8,128)S(1)}, f32[136,128]{1,0:T(8,128)S(1)}, u32[]{:S(2)}, u32[]{:S(2)}) %collective-permute-start.6) | collective-permute-done | bytes 69664 | tf_op jit(solution)/shard_map/ppermute | solution.py:72
  26.4 2.7 %collective-permute-done.5 = f32[136,128]{1,0:T(8,128)S(1)} collective-permute-done((f32[136,128]{1,0:T(8,128)S(1)}, f32[136,128]{1,0:T(8,128)S(1)}, u32[]{:S(2)}, u32[]{:S(2)}) %collective-permute-start.5) | collective-permute-done | bytes 69664 | tf_op jit(solution)/shard_map/ppermute | solution.py:72
  29.3 1.2 %collective-permute-done.7 = f32[136,128]{1,0:T(8,128)S(1)} collective-permute-done((f32[136,128]{1,0:T(8,128)S(1)}, f32[136,128]{1,0:T(8,128)S(1)}, u32[]{:S(2)}, u32[]{:S(2)}) %collective-permute-start.7) | collective-permute-done | bytes 69664 | tf_op jit(solution)/shard_map/ppermute | solution.py:72
  30.6 11.7 %custom-call.8 = f32[128,128]{1,0:T(8,128)S(1)} custom-call(f32[128,128]{1,0:T(8,128)S(1)} %bitcast_select_fusion.1), custom_call_target="Cholesky" | custom-call | tf_op jit(solution)/shard_map/cholesky/custom-call.1 | solution.py:33
  42.4 0.6 compare_reduce_fusion.1
  43.0 0.7 select_select_fusion.1
  43.8 4.9 %custom-call.9 = f32[1,64,64]{1,2,0:T(8,128)S(1)} custom-call(f32[1,64,64]{2,1,0:T(8,128)S(1)} %fusion.42), custom_call_target="InvertDiagBlocksLowerTriangular" | custom-call | tf_op jit(solution)/shard_map/triangular_solve/custom-call.0 | solution.py:21
  49.3 1.0 %collective-permute-done.8 = f32[64,64]{1,0:T(8,128)S(1)} collective-permute-done((f32[64,64]{1,0:T(8,128)S(1)}, f32[64,64]{1,0:T(8,128)S(1)}, u32[]{:S(2)}, u32[]{:S(2)}) %collective-permute-start.8) | collective-permute-done | bytes 16416 | tf_op jit(solution)/shard_map/ppermute | solution.py:72
  51.8 11.7 %custom-call.10 = f32[128,128]{1,0:T(8,128)S(1)} custom-call(f32[128,128]{1,0:T(8,128)S(1)} %fusion.28), custom_call_target="Cholesky" | custom-call | tf_op jit(solution)/shard_map/cholesky/custom-call.1 | solution.py:36
  63.5 0.6 compare_reduce_fusion
  64.2 0.7 select_select_fusion
  64.9 4.9 %custom-call.11 = f32[1,64,64]{1,2,0:T(8,128)S(1)} custom-call(f32[1,64,64]{2,1,0:T(8,128)S(1)} %fusion.38), custom_call_target="InvertDiagBlocksLowerTriangular" | custom-call | tf_op jit(solution)/shard_map/triangular_solve/custom-call.0 | solution.py:21
  70.3 0.8 %copy.13 = f32[256,256]{1,0:T(8,128)} copy(f32[256,256]{0,1:T(8,128)S(1)} %fusion.5) | data formatting | bytes 524288
  72.0 3.2 %convolution_multiply_fusion = f32[2048,256]{1,0:T(8,128)} fusion(f32[2048,256]{1,0:T(8,128)S(1)} %fusion.2, f32[128,128]{1,0:T(8,128)S(1)} %select_maximum_fusion.3, f32[64,64]{1,0:T(8,128)S(1)} %get-tuple-element.10, f32[64,64]{1,0:T(8,128)S(1)} %convolution_negate_fusion.1, f32[64,128]{1,0:T(8,128)S(1)} %concatenate.57, ...), kind=kOutput, calls=%fused_computation.6 | convolution fusion | flops 1611530240 | bytes 4390912 | tf_op jit(solution)/shard_map/dot_general | solution.py:145
  (50 shorter events, 7.4 us)
Async XLA Ops:
  0.6 1.4 %copy-start = (f32[2048,64]{0,1:T(8,128)S(1)}, f32[2048,64]{0,1:T(8,128)}, u32[]{:S(2)}) copy-start(f32[2048,64]{0,1:T(8,128)} %param.9) | copy-start | bytes 1572868
  8.0 1.0 %copy-start.1 = (f32[1,256,256]{2,1,0:T(8,128)S(1)}, f32[1,256,256]{2,1,0:T(8,128)}, u32[]{:S(2)}) copy-start(f32[1,256,256]{2,1,0:T(8,128)} %param.13) | copy-start | bytes 786436
  9.8 1.5 %collective-permute-start = (f32[136,128]{1,0:T(8,128)S(1)}, f32[136,128]{1,0:T(8,128)S(1)}, u32[]{:S(2)}, u32[]{:S(2)}) collective-permute-start(f32[136,128]{1,0:T(8,128)S(1)} %pad_select_fusion), channel_id=1, source_target_pairs={{0,1},{1,0},{2,3},{3,2},{4,5},{5,4},{6,7},{7,6},{8,9},{9,8},{10,11... | collective-permute-start | bytes 208904 | tf_op jit(solution)/shard_map/ppermute | solution.py:72
  11.3 6.4 %collective-permute-start.3 = (f32[136,128]{1,0:T(8,128)S(1)}, f32[136,128]{1,0:T(8,128)S(1)}, u32[]{:S(2)}, u32[]{:S(2)}) collective-permute-start(f32[136,128]{1,0:T(8,128)S(1)} %select_add_fusion), channel_id=1, source_target_pairs={{0,6},{1,7},{2,4},{3,5},{4,2},{5,3},{6,0},{7,1},{8,14},{9,15},{10,... | collective-permute-start | bytes 208904 | tf_op jit(solution)/shard_map/ppermute | solution.py:72
  15.2 4.3 %collective-permute-start.2 = (f32[136,128]{1,0:T(8,128)S(1)}, f32[136,128]{1,0:T(8,128)S(1)}, u32[]{:S(2)}, u32[]{:S(2)}) collective-permute-start(f32[136,128]{1,0:T(8,128)S(1)} %select_add_fusion), channel_id=1, source_target_pairs={{0,4},{1,5},{2,6},{3,7},{4,0},{5,1},{6,2},{7,3},{8,12},{9,13},{10,... | collective-permute-start | bytes 208904 | tf_op jit(solution)/shard_map/ppermute | solution.py:72
  15.7 4.3 %collective-permute-start.1 = (f32[136,128]{1,0:T(8,128)S(1)}, f32[136,128]{1,0:T(8,128)S(1)}, u32[]{:S(2)}, u32[]{:S(2)}) collective-permute-start(f32[136,128]{1,0:T(8,128)S(1)} %select_add_fusion), channel_id=1, source_target_pairs={{0,2},{1,3},{2,0},{3,1},{4,6},{5,7},{6,4},{7,5},{8,10},{9,11},{10,... | collective-permute-start | bytes 208904 | tf_op jit(solution)/shard_map/ppermute | solution.py:72
  20.0 6.4 %collective-permute-start.6 = (f32[136,128]{1,0:T(8,128)S(1)}, f32[136,128]{1,0:T(8,128)S(1)}, u32[]{:S(2)}, u32[]{:S(2)}) collective-permute-start(f32[136,128]{1,0:T(8,128)S(1)} %add_add_fusion.1), channel_id=1, source_target_pairs={{0,24},{1,25},{2,26},{3,27},{4,28},{5,29},{6,30},{7,31},{8,16},{9,... | collective-permute-start | bytes 208904 | tf_op jit(solution)/shard_map/ppermute | solution.py:72
  23.7 5.5 %collective-permute-start.5 = (f32[136,128]{1,0:T(8,128)S(1)}, f32[136,128]{1,0:T(8,128)S(1)}, u32[]{:S(2)}, u32[]{:S(2)}) collective-permute-start(f32[136,128]{1,0:T(8,128)S(1)} %add_add_fusion.1), channel_id=1, source_target_pairs={{0,16},{1,17},{2,18},{3,19},{4,20},{5,21},{6,22},{7,23},{8,24},{9,... | collective-permute-start | bytes 208904 | tf_op jit(solution)/shard_map/ppermute | solution.py:72
  23.7 5.5 %collective-permute-start.4 = (f32[136,128]{1,0:T(8,128)S(1)}, f32[136,128]{1,0:T(8,128)S(1)}, u32[]{:S(2)}, u32[]{:S(2)}) collective-permute-start(f32[136,128]{1,0:T(8,128)S(1)} %add_add_fusion.1), channel_id=1, source_target_pairs={{0,8},{1,9},{2,10},{3,11},{4,12},{5,13},{6,14},{7,15},{8,0},{9,1},... | collective-permute-start | bytes 208904 | tf_op jit(solution)/shard_map/ppermute | solution.py:72
  29.2 1.3 %collective-permute-start.7 = (f32[136,128]{1,0:T(8,128)S(1)}, f32[136,128]{1,0:T(8,128)S(1)}, u32[]{:S(2)}, u32[]{:S(2)}) collective-permute-start(f32[136,128]{1,0:T(8,128)S(1)} %add_add_fusion), channel_id=1, source_target_pairs={{0,1},{1,0},{2,3},{3,2},{4,5},{5,4},{6,7},{7,6},{8,9},{9,8},{10,11... | collective-permute-start | bytes 208904 | tf_op jit(solution)/shard_map/ppermute | solution.py:72
  48.9 1.5 %collective-permute-start.8 = (f32[64,64]{1,0:T(8,128)S(1)}, f32[64,64]{1,0:T(8,128)S(1)}, u32[]{:S(2)}, u32[]{:S(2)}) collective-permute-start(f32[64,64]{1,0:T(8,128)S(1)} %fusion.33), channel_id=1, source_target_pairs={{0,1},{1,0},{2,3},{3,2},{4,5},{5,4},{6,7},{7,6},{8,9},{9,8},{10,11... | collective-permute-start | bytes 49160 | tf_op jit(solution)/shard_map/ppermute | solution.py:72
  70.1 1.3 %collective-permute-start.9 = (f32[64,64]{1,0:T(8,128)S(1)}, f32[64,64]{1,0:T(8,128)S(1)}, u32[]{:S(2)}, u32[]{:S(2)}) collective-permute-start(f32[64,64]{1,0:T(8,128)S(1)} %fusion.31), channel_id=1, source_target_pairs={{0,1},{1,0},{2,3},{3,2},{4,5},{5,4},{6,7},{7,6},{8,9},{9,8},{10,11... | collective-permute-start | bytes 49160 | tf_op jit(solution)/shard_map/ppermute | solution.py:72

commit v13 on v12

--- a/solution.py
+++ b/solution.py
@@ -83,6 +83,7 @@
     send = jnp.where(low, second, first)
     keep = keep + flip(send, 1)
     rest = list(range(1, bits))
+    rest = rest[2:4] + rest[:2] + rest[4:]
     while rest:
         if len(rest) == 1:
             keep = keep + flip(keep, 1 << rest[0])

time: 75.4 us -> 76.1 us (level)
  no operation moved by 1% of the time
where the time goes in v13:
time: 76.1 us; the launch traced here: 75.9 us
  other arithmetic  36.4 us (48%)
  matrix products  12.7 us (17%)
  waiting for transfers between devices  12.7 us (17%)
  starting transfers between devices  10.5 us (14%)
  local copies, waits for them, and re-layouts  1.95 us (3%)
  between operations  1.61 us (2%)
    ppermute x10, waiting for transfers between devices, flip(): return lax.ppermute(array, axes, [(i, i ^ mask) for i in range(count)])  12.7 us
    another operation x3, other arithmetic, cholesky_and_inverse(): l22 = lax.linalg.cholesky(g22 - mm(l21, l21.T), symmetrize_input=False)  12.4 us
    another operation x3, other arithmetic, cholesky_and_inverse(): l11 = lax.linalg.cholesky(g11, symmetrize_input=False)  12.4 us
    ppermute x10, starting transfers between devices, flip(): return lax.ppermute(array, axes, [(i, i ^ mask) for i in range(count)])  10.5 us
    another operation x4, other arithmetic, shared_inverse(): lax.linalg.triangular_solve(block, jnp.eye(q, dtype=lower.dtype), left_si...  9.95 us
    dot_general x1, matrix products, per_device(): jnp.dot(inputs, freqs, precision=lax.Precision.HIGHEST) + phases[None, :]  4.59 us
    dot_general x1, matrix products, per_device(): lax.dot_general(features, inverse, (((1,), (1,)), ((), ())), precision=la...  3.18 us
    dot_general x4, matrix products, tdot(): lax.dot_general(a, b, (((0,), (0,)), ((), ())), preferred_element_type=jn...  2.09 us
  transfers between devices with their start and end apart: 10, of which 9 were waited for; matrix products, arithmetic and copies ran while one was open for 1% of the time, Pallas kernels for 0%

profile of v13, /device:TPU:0, one launch (start us, length us, event | category | flops | bytes accessed | tf_op | source)
XLA Modules:
  0.0 75.9 jit_solution(13158892515298514706)
XLA Ops:
  1.4 0.7 sqrt.3
  2.1 4.6 %fusion.2 = f32[2048,256]{1,0:T(8,128)S(1)} fusion(f32[2048,64]{0,1:T(8,128)S(1)} %copy-done, f32[64,256]{1,0:T(8,128)} %param.10, f32[256]{0:T(256)} %param.11, f32[2048]{0:T(1024)S(1)} %sqrt.3), kind=kOutput, calls=%fused_computation.10 | convolution fusion | flops 417857536 | bytes 2696192 | tf_op jit(solution)/shard_map/dot_general | solution.py:136
  7.2 0.6 convolution_add_fusion.3
  8.9 0.6 convolution_add_fusion.1
  10.3 0.9 %collective-permute-done = f32[136,128]{1,0:T(8,128)S(1)} collective-permute-done((f32[136,128]{1,0:T(8,128)S(1)}, f32[136,128]{1,0:T(8,128)S(1)}, u32[]{:S(2)}, u32[]{:S(2)}) %collective-permute-start) | collective-permute-done | bytes 69664 | tf_op jit(solution)/shard_map/ppermute | solution.py:72
  11.3 5.0 %collective-permute-start.3 = (f32[136,128]{1,0:T(8,128)S(1)}, f32[136,128]{1,0:T(8,128)S(1)}, u32[]{:S(2)}, u32[]{:S(2)}) collective-permute-start(f32[136,128]{1,0:T(8,128)S(1)} %select_add_fusion), channel_id=1, source_target_pairs={{0,24},{1,25},{2,26},{3,27},{4,28},{5,29},{6,30},{7,31},{8,16},{9,... | collective-permute-start | bytes 208904 | tf_op jit(solution)/shard_map/ppermute | solution.py:72
  16.3 0.6 collective-permute-start.1
  17.0 2.1 %collective-permute-done.3 = f32[136,128]{1,0:T(8,128)S(1)} collective-permute-done((f32[136,128]{1,0:T(8,128)S(1)}, f32[136,128]{1,0:T(8,128)S(1)}, u32[]{:S(2)}, u32[]{:S(2)}) %collective-permute-start.3) | collective-permute-done | bytes 69664 | tf_op jit(solution)/shard_map/ppermute | solution.py:72
  19.1 3.4 %collective-permute-done.2 = f32[136,128]{1,0:T(8,128)S(1)} collective-permute-done((f32[136,128]{1,0:T(8,128)S(1)}, f32[136,128]{1,0:T(8,128)S(1)}, u32[]{:S(2)}, u32[]{:S(2)}) %collective-permute-start.2) | collective-permute-done | bytes 69664 | tf_op jit(solution)/shard_map/ppermute | solution.py:72
  22.5 2.5 %collective-permute-start.6 = (f32[136,128]{1,0:T(8,128)S(1)}, f32[136,128]{1,0:T(8,128)S(1)}, u32[]{:S(2)}, u32[]{:S(2)}) collective-permute-start(f32[136,128]{1,0:T(8,128)S(1)} %add_add_fusion.1), channel_id=1, source_target_pairs={{0,6},{1,7},{2,4},{3,5},{4,2},{5,3},{6,0},{7,1},{8,14},{9,15},{10,... | collective-permute-start | bytes 208904 | tf_op jit(solution)/shard_map/ppermute | solution.py:72
  26.1 2.3 %collective-permute-done.6 = f32[136,128]{1,0:T(8,128)S(1)} collective-permute-done((f32[136,128]{1,0:T(8,128)S(1)}, f32[136,128]{1,0:T(8,128)S(1)}, u32[]{:S(2)}, u32[]{:S(2)}) %collective-permute-start.6) | collective-permute-done | bytes 69664 | tf_op jit(solution)/shard_map/ppermute | solution.py:72
  28.4 0.9 %collective-permute-done.5 = f32[136,128]{1,0:T(8,128)S(1)} collective-permute-done((f32[136,128]{1,0:T(8,128)S(1)}, f32[136,128]{1,0:T(8,128)S(1)}, u32[]{:S(2)}, u32[]{:S(2)}) %collective-permute-start.5) | collective-permute-done | bytes 69664 | tf_op jit(solution)/shard_map/ppermute | solution.py:72
  30.0 1.2 %collective-permute-done.7 = f32[136,128]{1,0:T(8,128)S(1)} collective-permute-done((f32[136,128]{1,0:T(8,128)S(1)}, f32[136,128]{1,0:T(8,128)S(1)}, u32[]{:S(2)}, u32[]{:S(2)}) %collective-permute-start.7) | collective-permute-done | bytes 69664 | tf_op jit(solution)/shard_map/ppermute | solution.py:72
  31.4 11.7 %custom-call.8 = f32[128,128]{1,0:T(8,128)S(1)} custom-call(f32[128,128]{1,0:T(8,128)S(1)} %bitcast_select_fusion.1), custom_call_target="Cholesky" | custom-call | tf_op jit(solution)/shard_map/cholesky/custom-call.1 | solution.py:33
  43.1 0.6 compare_reduce_fusion.1
  43.8 0.7 select_select_fusion.1
  44.5 4.9 %custom-call.9 = f32[1,64,64]{1,2,0:T(8,128)S(1)} custom-call(f32[1,64,64]{2,1,0:T(8,128)S(1)} %fusion.42), custom_call_target="InvertDiagBlocksLowerTriangular" | custom-call | tf_op jit(solution)/shard_map/triangular_solve/custom-call.0 | solution.py:21
  50.1 1.0 %collective-permute-done.8 = f32[64,64]{1,0:T(8,128)S(1)} collective-permute-done((f32[64,64]{1,0:T(8,128)S(1)}, f32[64,64]{1,0:T(8,128)S(1)}, u32[]{:S(2)}, u32[]{:S(2)}) %collective-permute-start.8) | collective-permute-done | bytes 16416 | tf_op jit(solution)/shard_map/ppermute | solution.py:72
  52.5 11.7 %custom-call.10 = f32[128,128]{1,0:T(8,128)S(1)} custom-call(f32[128,128]{1,0:T(8,128)S(1)} %fusion.28), custom_call_target="Cholesky" | custom-call | tf_op jit(solution)/shard_map/cholesky/custom-call.1 | solution.py:36
  64.3 0.6 compare_reduce_fusion
  64.9 0.7 select_select_fusion
  65.7 4.9 %custom-call.11 = f32[1,64,64]{1,2,0:T(8,128)S(1)} custom-call(f32[1,64,64]{2,1,0:T(8,128)S(1)} %fusion.38), custom_call_target="InvertDiagBlocksLowerTriangular" | custom-call | tf_op jit(solution)/shard_map/triangular_solve/custom-call.0 | solution.py:21
  71.1 0.8 %copy.13 = f32[256,256]{1,0:T(8,128)} copy(f32[256,256]{0,1:T(8,128)S(1)} %fusion.5) | data formatting | bytes 524288
  72.7 3.2 %convolution_multiply_fusion = f32[2048,256]{1,0:T(8,128)} fusion(f32[2048,256]{1,0:T(8,128)S(1)} %fusion.2, f32[128,128]{1,0:T(8,128)S(1)} %select_maximum_fusion.3, f32[64,64]{1,0:T(8,128)S(1)} %get-tuple-element.10, f32[64,64]{1,0:T(8,128)S(1)} %convolution_negate_fusion.1, f32[64,128]{1,0:T(8,128)S(1)} %concatenate.57, ...), kind=kOutput, calls=%fused_computation.6 | convolution fusion | flops 1611530240 | bytes 4390912 | tf_op jit(solution)/shard_map/dot_general | solution.py:146
  (50 shorter events, 7.8 us)
Async XLA Ops:
  0.6 1.4 %copy-start = (f32[2048,64]{0,1:T(8,128)S(1)}, f32[2048,64]{0,1:T(8,128)}, u32[]{:S(2)}) copy-start(f32[2048,64]{0,1:T(8,128)} %param.9) | copy-start | bytes 1572868
  8.0 1.0 %copy-start.1 = (f32[1,256,256]{2,1,0:T(8,128)S(1)}, f32[1,256,256]{2,1,0:T(8,128)}, u32[]{:S(2)}) copy-start(f32[1,256,256]{2,1,0:T(8,128)} %param.13) | copy-start | bytes 786436
  9.8 1.5 %collective-permute-start = (f32[136,128]{1,0:T(8,128)S(1)}, f32[136,128]{1,0:T(8,128)S(1)}, u32[]{:S(2)}, u32[]{:S(2)}) collective-permute-start(f32[136,128]{1,0:T(8,128)S(1)} %pad_select_fusion), channel_id=1, source_target_pairs={{0,1},{1,0},{2,3},{3,2},{4,5},{5,4},{6,7},{7,6},{8,9},{9,8},{10,11... | collective-permute-start | bytes 208904 | tf_op jit(solution)/shard_map/ppermute | solution.py:72
  11.3 7.8 %collective-permute-start.3 = (f32[136,128]{1,0:T(8,128)S(1)}, f32[136,128]{1,0:T(8,128)S(1)}, u32[]{:S(2)}, u32[]{:S(2)}) collective-permute-start(f32[136,128]{1,0:T(8,128)S(1)} %select_add_fusion), channel_id=1, source_target_pairs={{0,24},{1,25},{2,26},{3,27},{4,28},{5,29},{6,30},{7,31},{8,16},{9,... | collective-permute-start | bytes 208904 | tf_op jit(solution)/shard_map/ppermute | solution.py:72
  16.3 6.2 %collective-permute-start.2 = (f32[136,128]{1,0:T(8,128)S(1)}, f32[136,128]{1,0:T(8,128)S(1)}, u32[]{:S(2)}, u32[]{:S(2)}) collective-permute-start(f32[136,128]{1,0:T(8,128)S(1)} %select_add_fusion), channel_id=1, source_target_pairs={{0,16},{1,17},{2,18},{3,19},{4,20},{5,21},{6,22},{7,23},{8,24},{9,... | collective-permute-start | bytes 208904 | tf_op jit(solution)/shard_map/ppermute | solution.py:72
  16.3 6.2 %collective-permute-start.1 = (f32[136,128]{1,0:T(8,128)S(1)}, f32[136,128]{1,0:T(8,128)S(1)}, u32[]{:S(2)}, u32[]{:S(2)}) collective-permute-start(f32[136,128]{1,0:T(8,128)S(1)} %select_add_fusion), channel_id=1, source_target_pairs={{0,8},{1,9},{2,10},{3,11},{4,12},{5,13},{6,14},{7,15},{8,0},{9,1},... | collective-permute-start | bytes 208904 | tf_op jit(solution)/shard_map/ppermute | solution.py:72
  22.5 5.9 %collective-permute-start.6 = (f32[136,128]{1,0:T(8,128)S(1)}, f32[136,128]{1,0:T(8,128)S(1)}, u32[]{:S(2)}, u32[]{:S(2)}) collective-permute-start(f32[136,128]{1,0:T(8,128)S(1)} %add_add_fusion.1), channel_id=1, source_target_pairs={{0,6},{1,7},{2,4},{3,5},{4,2},{5,3},{6,0},{7,1},{8,14},{9,15},{10,... | collective-permute-start | bytes 208904 | tf_op jit(solution)/shard_map/ppermute | solution.py:72
  25.1 4.3 %collective-permute-start.5 = (f32[136,128]{1,0:T(8,128)S(1)}, f32[136,128]{1,0:T(8,128)S(1)}, u32[]{:S(2)}, u32[]{:S(2)}) collective-permute-start(f32[136,128]{1,0:T(8,128)S(1)} %add_add_fusion.1), channel_id=1, source_target_pairs={{0,4},{1,5},{2,6},{3,7},{4,0},{5,1},{6,2},{7,3},{8,12},{9,13},{10,... | collective-permute-start | bytes 208904 | tf_op jit(solution)/shard_map/ppermute | solution.py:72
  25.6 4.3 %collective-permute-start.4 = (f32[136,128]{1,0:T(8,128)S(1)}, f32[136,128]{1,0:T(8,128)S(1)}, u32[]{:S(2)}, u32[]{:S(2)}) collective-permute-start(f32[136,128]{1,0:T(8,128)S(1)} %add_add_fusion.1), channel_id=1, source_target_pairs={{0,2},{1,3},{2,0},{3,1},{4,6},{5,7},{6,4},{7,5},{8,10},{9,11},{10,... | collective-permute-start | bytes 208904 | tf_op jit(solution)/shard_map/ppermute | solution.py:72
  29.9 1.3 %collective-permute-start.7 = (f32[136,128]{1,0:T(8,128)S(1)}, f32[136,128]{1,0:T(8,128)S(1)}, u32[]{:S(2)}, u32[]{:S(2)}) collective-permute-start(f32[136,128]{1,0:T(8,128)S(1)} %add_add_fusion), channel_id=1, source_target_pairs={{0,1},{1,0},{2,3},{3,2},{4,5},{5,4},{6,7},{7,6},{8,9},{9,8},{10,11... | collective-permute-start | bytes 208904 | tf_op jit(solution)/shard_map/ppermute | solution.py:72
  49.7 1.5 %collective-permute-start.8 = (f32[64,64]{1,0:T(8,128)S(1)}, f32[64,64]{1,0:T(8,128)S(1)}, u32[]{:S(2)}, u32[]{:S(2)}) collective-permute-start(f32[64,64]{1,0:T(8,128)S(1)} %fusion.33), channel_id=1, source_target_pairs={{0,1},{1,0},{2,3},{3,2},{4,5},{5,4},{6,7},{7,6},{8,9},{9,8},{10,11... | collective-permute-start | bytes 49160 | tf_op jit(solution)/shard_map/ppermute | solution.py:72
  70.8 1.3 %collective-permute-start.9 = (f32[64,64]{1,0:T(8,128)S(1)}, f32[64,64]{1,0:T(8,128)S(1)}, u32[]{:S(2)}, u32[]{:S(2)}) collective-permute-start(f32[64,64]{1,0:T(8,128)S(1)} %fusion.31), channel_id=1, source_target_pairs={{0,1},{1,0},{2,3},{3,2},{4,5},{5,4},{6,7},{7,6},{8,9},{9,8},{10,11... | collective-permute-start | bytes 49160 | tf_op jit(solution)/shard_map/ppermute | solution.py:72

commit v14 on v12

--- a/solution.py
+++ b/solution.py
@@ -77,11 +77,9 @@
     first, second = pack(gram)
     if bits == 0:
         return unpack(first, second)
-    me = lax.axis_index("grp") * lax.axis_size("leaf") + lax.axis_index("leaf")
-    low = me % 2 == 0
-    keep = jnp.where(low, first, second)
-    send = jnp.where(low, second, first)
-    keep = keep + flip(send, 1)
+    h = first.shape[0]
+    keep = jnp.concatenate([first, second], axis=0)
+    keep = keep + flip(keep, 1)
     rest = list(range(1, bits))
     while rest:
         if len(rest) == 1:
@@ -93,9 +91,7 @@
             far = flip(keep, mb) + flip(keep, ma | mb)
             keep = near + far
             rest = rest[2:]
-    other = flip(keep, 1)
-    first = jnp.where(low, keep, other)
-    second = jnp.where(low, other, keep)
+    first, second = keep[:h], keep[h:]
     return unpack(first, second)
 
 

time: 75.4 us -> 82.2 us (1.090)
  waiting for transfers between devices: 12.3 us -> 19.8 us
    ppermute x10 -> x9, waiting for transfers between devices: 12.3 us -> 19.8 us  [flip(): return lax.ppermute(array, axes, [(i, i ^ mask) for i in range(count)])]
    ppermute x10 -> x9, starting transfers between devices: 10.2 us -> 9.8 us  [flip(): return lax.ppermute(array, axes, [(i, i ^ mask) for i in range(count)])]
  transfers between devices with their start and end apart: 10 -> 9, of which waited for: 9 -> 7; matrix products, arithmetic and copies ran while one was open for 1% -> 1% of each run, Pallas kernels for 0% -> 0%
where the time goes in v14:
time: 82.2 us; the launch traced here: 82 us
  other arithmetic  36.3 us (44%)
  waiting for transfers between devices  19.8 us (24%)
  matrix products  12.9 us (16%)
  starting transfers between devices  9.8 us (12%)
  local copies, waits for them, and re-layouts  2.25 us (3%)
  between operations  0.95 us (1%)
    ppermute x9, waiting for transfers between devices, flip(): return lax.ppermute(array, axes, [(i, i ^ mask) for i in range(count)])  19.8 us
    another operation x3, other arithmetic, cholesky_and_inverse(): l11 = lax.linalg.cholesky(g11, symmetrize_input=False)  12.4 us
    another operation x3, other arithmetic, cholesky_and_inverse(): l22 = lax.linalg.cholesky(g22 - mm(l21, l21.T), symmetrize_input=False)  12.4 us
    another operation x4, other arithmetic, shared_inverse(): lax.linalg.triangular_solve(block, jnp.eye(q, dtype=lower.dtype), left_si...  9.95 us
    ppermute x9, starting transfers between devices, flip(): return lax.ppermute(array, axes, [(i, i ^ mask) for i in range(count)])  9.8 us
    dot_general x1, matrix products, per_device(): jnp.dot(inputs, freqs, precision=lax.Precision.HIGHEST) + phases[None, :]  4.58 us
    dot_general x1, matrix products, per_device(): lax.dot_general(features, inverse, (((1,), (1,)), ((), ())), precision=la...  3.18 us
    dot_general x4, matrix products, tdot(): lax.dot_general(a, b, (((0,), (0,)), ((), ())), preferred_element_type=jn...  2.09 us
  transfers between devices with their start and end apart: 9, of which 7 were waited for; matrix products, arithmetic and copies ran while one was open for 1% of the time, Pallas kernels for 0%

profile of v14, /device:TPU:0, one launch (start us, length us, event | category | flops | bytes accessed | tf_op | source)
XLA Modules:
  0.0 82.0 jit_solution(6254695868111948906)
XLA Ops:
  0.6 0.8 sqrt.3
  1.7 4.6 %fusion.2 = f32[2048,256]{1,0:T(8,128)S(1)} fusion(f32[2048,64]{0,1:T(8,128)S(1)} %copy-done, f32[64,256]{1,0:T(8,128)} %param.10, f32[256]{0:T(256)} %param.11, f32[2048]{0:T(1024)S(1)} %sqrt.3), kind=kOutput, calls=%fused_computation.10 | convolution fusion | flops 417857536 | bytes 2696192 | tf_op jit(solution)/shard_map/dot_general | solution.py:131
  6.8 0.6 convolution_add_fusion.3
  8.6 0.6 convolution_add_fusion.1
  9.3 0.6 collective-permute-start
  9.9 1.0 %collective-permute-done = f32[272,128]{1,0:T(8,128)S(1)} collective-permute-done((f32[272,128]{1,0:T(8,128)S(1)}, f32[272,128]{1,0:T(8,128)S(1)}, u32[]{:S(2)}, u32[]{:S(2)}) %collective-permute-start) | collective-permute-done | bytes 139296 | tf_op jit(solution)/shard_map/ppermute | solution.py:72
  10.9 3.9 %collective-permute-start.3 = (f32[272,128]{1,0:T(8,128)S(1)}, f32[272,128]{1,0:T(8,128)S(1)}, u32[]{:S(2)}, u32[]{:S(2)}) collective-permute-start(f32[272,128]{1,0:T(8,128)S(1)} %add.101), channel_id=1, source_target_pairs={{0,6},{1,7},{2,4},{3,5},{4,2},{5,3},{6,0},{7,1},{8,14},{9,15},{10,... | collective-permute-start | bytes 417800 | tf_op jit(solution)/shard_map/ppermute | solution.py:72
  15.4 3.9 %collective-permute-done.3 = f32[272,128]{1,0:T(8,128)S(1)} collective-permute-done((f32[272,128]{1,0:T(8,128)S(1)}, f32[272,128]{1,0:T(8,128)S(1)}, u32[]{:S(2)}, u32[]{:S(2)}) %collective-permute-start.3) | collective-permute-done | bytes 139296 | tf_op jit(solution)/shard_map/ppermute | solution.py:72
  19.3 2.7 %collective-permute-done.2 = f32[272,128]{1,0:T(8,128)S(1)} collective-permute-done((f32[272,128]{1,0:T(8,128)S(1)}, f32[272,128]{1,0:T(8,128)S(1)}, u32[]{:S(2)}, u32[]{:S(2)}) %collective-permute-start.2) | collective-permute-done | bytes 139296 | tf_op jit(solution)/shard_map/ppermute | solution.py:72
  22.0 3.6 %collective-permute-start.6 = (f32[272,128]{1,0:T(8,128)S(1)}, f32[272,128]{1,0:T(8,128)S(1)}, u32[]{:S(2)}, u32[]{:S(2)}) collective-permute-start(f32[272,128]{1,0:T(8,128)S(1)} %add_add_fusion.1), channel_id=1, source_target_pairs={{0,24},{1,25},{2,26},{3,27},{4,28},{5,29},{6,30},{7,31},{8,16},{9,... | collective-permute-start | bytes 417800 | tf_op jit(solution)/shard_map/ppermute | solution.py:72
  25.7 0.8 collective-permute-start.4
  26.5 4.0 %collective-permute-done.6 = f32[272,128]{1,0:T(8,128)S(1)} collective-permute-done((f32[272,128]{1,0:T(8,128)S(1)}, f32[272,128]{1,0:T(8,128)S(1)}, u32[]{:S(2)}, u32[]{:S(2)}) %collective-permute-start.6) | collective-permute-done | bytes 139296 | tf_op jit(solution)/shard_map/ppermute | solution.py:72
  30.5 6.8 %collective-permute-done.5 = f32[272,128]{1,0:T(8,128)S(1)} collective-permute-done((f32[272,128]{1,0:T(8,128)S(1)}, f32[272,128]{1,0:T(8,128)S(1)}, u32[]{:S(2)}, u32[]{:S(2)}) %collective-permute-start.5) | collective-permute-done | bytes 139296 | tf_op jit(solution)/shard_map/ppermute | solution.py:72
  37.5 11.7 %custom-call.8 = f32[128,128]{1,0:T(8,128)S(1)} custom-call(f32[128,128]{1,0:T(8,128)S(1)} %bitcast_select_fusion.1), custom_call_target="Cholesky" | custom-call | tf_op jit(solution)/shard_map/cholesky/custom-call.1 | solution.py:33
  49.2 0.6 compare_reduce_fusion.1
  49.9 0.7 select_select_fusion.1
  50.6 4.9 %custom-call.9 = f32[1,64,64]{1,2,0:T(8,128)S(1)} custom-call(f32[1,64,64]{2,1,0:T(8,128)S(1)} %fusion.42), custom_call_target="InvertDiagBlocksLowerTriangular" | custom-call | tf_op jit(solution)/shard_map/triangular_solve/custom-call.0 | solution.py:21
  55.9 1.2 %collective-permute-done.7 = f32[64,64]{1,0:T(8,128)S(1)} collective-permute-done((f32[64,64]{1,0:T(8,128)S(1)}, f32[64,64]{1,0:T(8,128)S(1)}, u32[]{:S(2)}, u32[]{:S(2)}) %collective-permute-start.7) | collective-permute-done | bytes 16416 | tf_op jit(solution)/shard_map/ppermute | solution.py:72
  58.6 11.7 %custom-call.10 = f32[128,128]{1,0:T(8,128)S(1)} custom-call(f32[128,128]{1,0:T(8,128)S(1)} %fusion.28), custom_call_target="Cholesky" | custom-call | tf_op jit(solution)/shard_map/cholesky/custom-call.1 | solution.py:36
  70.4 0.6 compare_reduce_fusion
  71.0 0.7 select_select_fusion
  71.7 4.9 %custom-call.11 = f32[1,64,64]{1,2,0:T(8,128)S(1)} custom-call(f32[1,64,64]{2,1,0:T(8,128)S(1)} %fusion.38), custom_call_target="InvertDiagBlocksLowerTriangular" | custom-call | tf_op jit(solution)/shard_map/triangular_solve/custom-call.0 | solution.py:21
  77.1 0.8 %copy.13 = f32[256,256]{1,0:T(8,128)} copy(f32[256,256]{0,1:T(8,128)S(1)} %fusion.5) | data formatting | bytes 524288
  78.8 3.2 %convolution_multiply_fusion = f32[2048,256]{1,0:T(8,128)} fusion(f32[2048,256]{1,0:T(8,128)S(1)} %fusion.2, f32[128,128]{1,0:T(8,128)S(1)} %select_maximum_fusion.3, f32[64,64]{1,0:T(8,128)S(1)} %get-tuple-element.10, f32[64,64]{1,0:T(8,128)S(1)} %convolution_negate_fusion.1, f32[64,128]{1,0:T(8,128)S(1)} %concatenate.53, ...), kind=kOutput, calls=%fused_computation.6 | convolution fusion | flops 1611530240 | bytes 4390912 | tf_op jit(solution)/shard_map/dot_general | solution.py:141
  (49 shorter events, 6.2 us)
Async XLA Ops:
  0.6 1.1 %copy-start = (f32[2048,64]{0,1:T(8,128)S(1)}, f32[2048,64]{0,1:T(8,128)}, u32[]{:S(2)}) copy-start(f32[2048,64]{0,1:T(8,128)} %param.9) | copy-start | bytes 1572868
  7.6 1.0 %copy-start.2 = (s32[32]{0:T(128)S(1)}, s32[32]{0:T(128)}, u32[]{:S(2)}) copy-start(s32[32]{0:T(128)} %param.14) | copy-start | bytes 388
  7.6 1.0 %copy-start.1 = (f32[1,256,256]{2,1,0:T(8,128)S(1)}, f32[1,256,256]{2,1,0:T(8,128)}, u32[]{:S(2)}) copy-start(f32[1,256,256]{2,1,0:T(8,128)} %param.13) | copy-start | bytes 786436
  9.3 1.6 %collective-permute-start = (f32[272,128]{1,0:T(8,128)S(1)}, f32[272,128]{1,0:T(8,128)S(1)}, u32[]{:S(2)}, u32[]{:S(2)}) collective-permute-start(f32[272,128]{1,0:T(8,128)S(1)} %concatenate.45), channel_id=1, source_target_pairs={{0,1},{1,0},{2,3},{3,2},{4,5},{5,4},{6,7},{7,6},{8,9},{9,8},{10,11... | collective-permute-start | bytes 417800 | tf_op jit(solution)/shard_map/ppermute | solution.py:72
  10.9 8.4 %collective-permute-start.3 = (f32[272,128]{1,0:T(8,128)S(1)}, f32[272,128]{1,0:T(8,128)S(1)}, u32[]{:S(2)}, u32[]{:S(2)}) collective-permute-start(f32[272,128]{1,0:T(8,128)S(1)} %add.101), channel_id=1, source_target_pairs={{0,6},{1,7},{2,4},{3,5},{4,2},{5,3},{6,0},{7,1},{8,14},{9,15},{10,... | collective-permute-start | bytes 417800 | tf_op jit(solution)/shard_map/ppermute | solution.py:72
  14.7 7.3 %collective-permute-start.2 = (f32[272,128]{1,0:T(8,128)S(1)}, f32[272,128]{1,0:T(8,128)S(1)}, u32[]{:S(2)}, u32[]{:S(2)}) collective-permute-start(f32[272,128]{1,0:T(8,128)S(1)} %add.101), channel_id=1, source_target_pairs={{0,4},{1,5},{2,6},{3,7},{4,0},{5,1},{6,2},{7,3},{8,12},{9,13},{10,... | collective-permute-start | bytes 417800 | tf_op jit(solution)/shard_map/ppermute | solution.py:72
  15.3 6.7 %collective-permute-start.1 = (f32[272,128]{1,0:T(8,128)S(1)}, f32[272,128]{1,0:T(8,128)S(1)}, u32[]{:S(2)}, u32[]{:S(2)}) collective-permute-start(f32[272,128]{1,0:T(8,128)S(1)} %add.101), channel_id=1, source_target_pairs={{0,2},{1,3},{2,0},{3,1},{4,6},{5,7},{6,4},{7,5},{8,10},{9,11},{10,... | collective-permute-start | bytes 417800 | tf_op jit(solution)/shard_map/ppermute | solution.py:72
  22.0 8.5 %collective-permute-start.6 = (f32[272,128]{1,0:T(8,128)S(1)}, f32[272,128]{1,0:T(8,128)S(1)}, u32[]{:S(2)}, u32[]{:S(2)}) collective-permute-start(f32[272,128]{1,0:T(8,128)S(1)} %add_add_fusion.1), channel_id=1, source_target_pairs={{0,24},{1,25},{2,26},{3,27},{4,28},{5,29},{6,30},{7,31},{8,16},{9,... | collective-permute-start | bytes 417800 | tf_op jit(solution)/shard_map/ppermute | solution.py:72
  25.7 11.6 %collective-permute-start.5 = (f32[272,128]{1,0:T(8,128)S(1)}, f32[272,128]{1,0:T(8,128)S(1)}, u32[]{:S(2)}, u32[]{:S(2)}) collective-permute-start(f32[272,128]{1,0:T(8,128)S(1)} %add_add_fusion.1), channel_id=1, source_target_pairs={{0,16},{1,17},{2,18},{3,19},{4,20},{5,21},{6,22},{7,23},{8,24},{9,... | collective-permute-start | bytes 417800 | tf_op jit(solution)/shard_map/ppermute | solution.py:72
  25.7 11.6 %collective-permute-start.4 = (f32[272,128]{1,0:T(8,128)S(1)}, f32[272,128]{1,0:T(8,128)S(1)}, u32[]{:S(2)}, u32[]{:S(2)}) collective-permute-start(f32[272,128]{1,0:T(8,128)S(1)} %add_add_fusion.1), channel_id=1, source_target_pairs={{0,8},{1,9},{2,10},{3,11},{4,12},{5,13},{6,14},{7,15},{8,0},{9,1},... | collective-permute-start | bytes 417800 | tf_op jit(solution)/shard_map/ppermute | solution.py:72
  55.8 1.3 %collective-permute-start.7 = (f32[64,64]{1,0:T(8,128)S(1)}, f32[64,64]{1,0:T(8,128)S(1)}, u32[]{:S(2)}, u32[]{:S(2)}) collective-permute-start(f32[64,64]{1,0:T(8,128)S(1)} %fusion.33), channel_id=1, source_target_pairs={{0,1},{1,0},{2,3},{3,2},{4,5},{5,4},{6,7},{7,6},{8,9},{9,8},{10,11... | collective-permute-start | bytes 49160 | tf_op jit(solution)/shard_map/ppermute | solution.py:72
  76.9 1.3 %collective-permute-start.8 = (f32[64,64]{1,0:T(8,128)S(1)}, f32[64,64]{1,0:T(8,128)S(1)}, u32[]{:S(2)}, u32[]{:S(2)}) collective-permute-start(f32[64,64]{1,0:T(8,128)S(1)} %fusion.31), channel_id=1, source_target_pairs={{0,1},{1,0},{2,3},{3,2},{4,5},{5,4},{6,7},{7,6},{8,9},{9,8},{10,11... | collective-permute-start | bytes 49160 | tf_op jit(solution)/shard_map/ppermute | solution.py:72

commit v15 on v12

--- a/solution.py
+++ b/solution.py
@@ -134,12 +134,9 @@
     norm_scale = 1.0 / math.sqrt(total_rows)
     proj = jnp.dot(inputs, freqs, precision=lax.Precision.HIGHEST) + phases[None, :]
     features = jnp.sqrt(sample_weight)[:, None] * bounded_cos(proj) * norm_scale
-    gram = split_gram(features)
     slot = lax.axis_index("grp") * lax.axis_size("leaf") + lax.axis_index("leaf")
     running = jnp.where(slot == root[0], stored[0], jnp.zeros_like(stored[0]))
-    gram = gram + lax.dot_general(
-        running, running, (((0,), (0,)), ((), ())), precision=lax.Precision.HIGHEST
-    )
+    gram = split_gram(jnp.concatenate([features, running], axis=0))
     gram = all_reduce_symmetric(gram)
     lower, inverse = cholesky_and_inverse(*gram)
     basis = lax.dot_general(

time: 75.4 us -> 75.2 us (level)
  waiting for transfers between devices: 12.3 us -> 11.5 us
    ppermute x10, waiting for transfers between devices: 12.3 us -> 11.5 us  [flip(): return lax.ppermute(array, axes, [(i, i ^ mask) for i in range(count)])]
where the time goes in v15:
time: 75.2 us; the launch traced here: 74.8 us
  other arithmetic  36.4 us (48%)
  matrix products  12.5 us (17%)
  waiting for transfers between devices  11.5 us (15%)
  starting transfers between devices  10.9 us (14%)
  local copies, waits for them, and re-layouts  1.95 us (3%)
  between operations  1.61 us (2%)
    another operation x3, other arithmetic, cholesky_and_inverse(): l22 = lax.linalg.cholesky(g22 - mm(l21, l21.T), symmetrize_input=False)  12.4 us
    another operation x3, other arithmetic, cholesky_and_inverse(): l11 = lax.linalg.cholesky(g11, symmetrize_input=False)  12.4 us
    ppermute x10, waiting for transfers between devices, flip(): return lax.ppermute(array, axes, [(i, i ^ mask) for i in range(count)])  11.5 us
    ppermute x10, starting transfers between devices, flip(): return lax.ppermute(array, axes, [(i, i ^ mask) for i in range(count)])  10.9 us
    another operation x4, other arithmetic, shared_inverse(): lax.linalg.triangular_solve(block, jnp.eye(q, dtype=lower.dtype), left_si...  9.95 us
    dot_general x1, matrix products, per_device(): jnp.dot(inputs, freqs, precision=lax.Precision.HIGHEST) + phases[None, :]  4.59 us
    dot_general x1, matrix products, per_device(): lax.dot_general(features, inverse, (((1,), (1,)), ((), ())), precision=la...  3.18 us
    dot_general x4, matrix products, tdot(): lax.dot_general(a, b, (((0,), (0,)), ((), ())), preferred_element_type=jn...  2.32 us
  transfers between devices with their start and end apart: 10, of which 9 were waited for; matrix products, arithmetic and copies ran while one was open for 1% of the time, Pallas kernels for 0%

profile of v15, /device:TPU:0, one launch (start us, length us, event | category | flops | bytes accessed | tf_op | source)
XLA Modules:
  0.0 74.8 jit_solution(17203422231594182560)
XLA Ops:
  1.4 0.7 sqrt.3
  2.1 4.6 %fusion.2 = f32[2048,256]{1,0:T(8,128)S(1)} fusion(f32[2048,64]{0,1:T(8,128)S(1)} %copy-done, f32[64,256]{1,0:T(8,128)} %param.10, f32[256]{0:T(256)} %param.11, f32[2048]{0:T(1024)S(1)} %sqrt.3), kind=kOutput, calls=%fused_computation.11 | convolution fusion | flops 417857536 | bytes 2696192 | tf_op jit(solution)/shard_map/dot_general | solution.py:135
  6.7 0.7 fusion.3
  10.0 0.9 %collective-permute-done = f32[136,128]{1,0:T(8,128)S(1)} collective-permute-done((f32[136,128]{1,0:T(8,128)S(1)}, f32[136,128]{1,0:T(8,128)S(1)}, u32[]{:S(2)}, u32[]{:S(2)}) %collective-permute-start) | collective-permute-done | bytes 69664 | tf_op jit(solution)/shard_map/ppermute | solution.py:72
  11.0 3.8 %collective-permute-start.3 = (f32[136,128]{1,0:T(8,128)S(1)}, f32[136,128]{1,0:T(8,128)S(1)}, u32[]{:S(2)}, u32[]{:S(2)}) collective-permute-start(f32[136,128]{1,0:T(8,128)S(1)} %select_add_fusion), channel_id=1, source_target_pairs={{0,6},{1,7},{2,4},{3,5},{4,2},{5,3},{6,0},{7,1},{8,14},{9,15},{10,... | collective-permute-start | bytes 208904 | tf_op jit(solution)/shard_map/ppermute | solution.py:72
  14.8 1.5 %collective-permute-start.2 = (f32[136,128]{1,0:T(8,128)S(1)}, f32[136,128]{1,0:T(8,128)S(1)}, u32[]{:S(2)}, u32[]{:S(2)}) collective-permute-start(f32[136,128]{1,0:T(8,128)S(1)} %select_add_fusion), channel_id=1, source_target_pairs={{0,4},{1,5},{2,6},{3,7},{4,0},{5,1},{6,2},{7,3},{8,12},{9,13},{10,... | collective-permute-start | bytes 208904 | tf_op jit(solution)/shard_map/ppermute | solution.py:72
  16.3 1.1 %collective-permute-done.3 = f32[136,128]{1,0:T(8,128)S(1)} collective-permute-done((f32[136,128]{1,0:T(8,128)S(1)}, f32[136,128]{1,0:T(8,128)S(1)}, u32[]{:S(2)}, u32[]{:S(2)}) %collective-permute-start.3) | collective-permute-done | bytes 69664 | tf_op jit(solution)/shard_map/ppermute | solution.py:72
  17.4 2.6 %collective-permute-done.2 = f32[136,128]{1,0:T(8,128)S(1)} collective-permute-done((f32[136,128]{1,0:T(8,128)S(1)}, f32[136,128]{1,0:T(8,128)S(1)}, u32[]{:S(2)}, u32[]{:S(2)}) %collective-permute-start.2) | collective-permute-done | bytes 69664 | tf_op jit(solution)/shard_map/ppermute | solution.py:72
  20.6 2.7 %collective-permute-start.6 = (f32[136,128]{1,0:T(8,128)S(1)}, f32[136,128]{1,0:T(8,128)S(1)}, u32[]{:S(2)}, u32[]{:S(2)}) collective-permute-start(f32[136,128]{1,0:T(8,128)S(1)} %add_add_fusion.1), channel_id=1, source_target_pairs={{0,24},{1,25},{2,26},{3,27},{4,28},{5,29},{6,30},{7,31},{8,16},{9,... | collective-permute-start | bytes 208904 | tf_op jit(solution)/shard_map/ppermute | solution.py:72
  23.3 1.7 %collective-permute-start.4 = (f32[136,128]{1,0:T(8,128)S(1)}, f32[136,128]{1,0:T(8,128)S(1)}, u32[]{:S(2)}, u32[]{:S(2)}) collective-permute-start(f32[136,128]{1,0:T(8,128)S(1)} %add_add_fusion.1), channel_id=1, source_target_pairs={{0,8},{1,9},{2,10},{3,11},{4,12},{5,13},{6,14},{7,15},{8,0},{9,1},... | collective-permute-start | bytes 208904 | tf_op jit(solution)/shard_map/ppermute | solution.py:72
  25.1 1.8 %collective-permute-done.6 = f32[136,128]{1,0:T(8,128)S(1)} collective-permute-done((f32[136,128]{1,0:T(8,128)S(1)}, f32[136,128]{1,0:T(8,128)S(1)}, u32[]{:S(2)}, u32[]{:S(2)}) %collective-permute-start.6) | collective-permute-done | bytes 69664 | tf_op jit(solution)/shard_map/ppermute | solution.py:72
  26.9 1.9 %collective-permute-done.5 = f32[136,128]{1,0:T(8,128)S(1)} collective-permute-done((f32[136,128]{1,0:T(8,128)S(1)}, f32[136,128]{1,0:T(8,128)S(1)}, u32[]{:S(2)}, u32[]{:S(2)}) %collective-permute-start.5) | collective-permute-done | bytes 69664 | tf_op jit(solution)/shard_map/ppermute | solution.py:72
  29.0 1.2 %collective-permute-done.7 = f32[136,128]{1,0:T(8,128)S(1)} collective-permute-done((f32[136,128]{1,0:T(8,128)S(1)}, f32[136,128]{1,0:T(8,128)S(1)}, u32[]{:S(2)}, u32[]{:S(2)}) %collective-permute-start.7) | collective-permute-done | bytes 69664 | tf_op jit(solution)/shard_map/ppermute | solution.py:72
  30.3 11.7 %custom-call.8 = f32[128,128]{1,0:T(8,128)S(1)} custom-call(f32[128,128]{1,0:T(8,128)S(1)} %bitcast_select_fusion.1), custom_call_target="Cholesky" | custom-call | tf_op jit(solution)/shard_map/cholesky/custom-call.1 | solution.py:33
  42.1 0.6 compare_reduce_fusion.1
  42.7 0.7 select_select_fusion.1
  43.5 4.9 %custom-call.9 = f32[1,64,64]{1,2,0:T(8,128)S(1)} custom-call(f32[1,64,64]{2,1,0:T(8,128)S(1)} %fusion.38), custom_call_target="InvertDiagBlocksLowerTriangular" | custom-call | tf_op jit(solution)/shard_map/triangular_solve/custom-call.0 | solution.py:21
  48.9 1.0 %collective-permute-done.8 = f32[64,64]{1,0:T(8,128)S(1)} collective-permute-done((f32[64,64]{1,0:T(8,128)S(1)}, f32[64,64]{1,0:T(8,128)S(1)}, u32[]{:S(2)}, u32[]{:S(2)}) %collective-permute-start.8) | collective-permute-done | bytes 16416 | tf_op jit(solution)/shard_map/ppermute | solution.py:72
  51.5 11.7 %custom-call.10 = f32[128,128]{1,0:T(8,128)S(1)} custom-call(f32[128,128]{1,0:T(8,128)S(1)} %fusion.24), custom_call_target="Cholesky" | custom-call | tf_op jit(solution)/shard_map/cholesky/custom-call.1 | solution.py:36
  63.2 0.6 compare_reduce_fusion
  63.9 0.7 select_select_fusion
  64.6 4.9 %custom-call.11 = f32[1,64,64]{1,2,0:T(8,128)S(1)} custom-call(f32[1,64,64]{2,1,0:T(8,128)S(1)} %fusion.34), custom_call_target="InvertDiagBlocksLowerTriangular" | custom-call | tf_op jit(solution)/shard_map/triangular_solve/custom-call.0 | solution.py:21
  70.0 0.8 %copy.13 = f32[256,256]{1,0:T(8,128)} copy(f32[256,256]{0,1:T(8,128)S(1)} %fusion.6) | data formatting | bytes 524288
  71.7 3.2 %convolution_multiply_fusion = f32[2048,256]{1,0:T(8,128)} fusion(f32[2048,256]{1,0:T(8,128)S(1)} %fusion.2, f32[128,128]{1,0:T(8,128)S(1)} %select_maximum_fusion.3, f32[64,64]{1,0:T(8,128)S(1)} %get-tuple-element.10, f32[64,64]{1,0:T(8,128)S(1)} %convolution_negate_fusion.1, f32[64,128]{1,0:T(8,128)S(1)} %concatenate.61, ...), kind=kOutput, calls=%fused_computation.6 | convolution fusion | flops 1611530240 | bytes 4390912 | tf_op jit(solution)/shard_map/dot_general | solution.py:142
  (48 shorter events, 7.0 us)
Async XLA Ops:
  0.6 1.5 %copy-start = (f32[2048,64]{0,1:T(8,128)S(1)}, f32[2048,64]{0,1:T(8,128)}, u32[]{:S(2)}) copy-start(f32[2048,64]{0,1:T(8,128)} %param.9) | copy-start | bytes 1572868
  9.4 1.5 %collective-permute-start = (f32[136,128]{1,0:T(8,128)S(1)}, f32[136,128]{1,0:T(8,128)S(1)}, u32[]{:S(2)}, u32[]{:S(2)}) collective-permute-start(f32[136,128]{1,0:T(8,128)S(1)} %pad_select_fusion), channel_id=1, source_target_pairs={{0,1},{1,0},{2,3},{3,2},{4,5},{5,4},{6,7},{7,6},{8,9},{9,8},{10,11... | collective-permute-start | bytes 208904 | tf_op jit(solution)/shard_map/ppermute | solution.py:72
  11.0 6.4 %collective-permute-start.3 = (f32[136,128]{1,0:T(8,128)S(1)}, f32[136,128]{1,0:T(8,128)S(1)}, u32[]{:S(2)}, u32[]{:S(2)}) collective-permute-start(f32[136,128]{1,0:T(8,128)S(1)} %select_add_fusion), channel_id=1, source_target_pairs={{0,6},{1,7},{2,4},{3,5},{4,2},{5,3},{6,0},{7,1},{8,14},{9,15},{10,... | collective-permute-start | bytes 208904 | tf_op jit(solution)/shard_map/ppermute | solution.py:72
  14.8 5.2 %collective-permute-start.2 = (f32[136,128]{1,0:T(8,128)S(1)}, f32[136,128]{1,0:T(8,128)S(1)}, u32[]{:S(2)}, u32[]{:S(2)}) collective-permute-start(f32[136,128]{1,0:T(8,128)S(1)} %select_add_fusion), channel_id=1, source_target_pairs={{0,4},{1,5},{2,6},{3,7},{4,0},{5,1},{6,2},{7,3},{8,12},{9,13},{10,... | collective-permute-start | bytes 208904 | tf_op jit(solution)/shard_map/ppermute | solution.py:72
  16.3 4.3 %collective-permute-start.1 = (f32[136,128]{1,0:T(8,128)S(1)}, f32[136,128]{1,0:T(8,128)S(1)}, u32[]{:S(2)}, u32[]{:S(2)}) collective-permute-start(f32[136,128]{1,0:T(8,128)S(1)} %select_add_fusion), channel_id=1, source_target_pairs={{0,2},{1,3},{2,0},{3,1},{4,6},{5,7},{6,4},{7,5},{8,10},{9,11},{10,... | collective-permute-start | bytes 208904 | tf_op jit(solution)/shard_map/ppermute | solution.py:72
  20.6 6.3 %collective-permute-start.6 = (f32[136,128]{1,0:T(8,128)S(1)}, f32[136,128]{1,0:T(8,128)S(1)}, u32[]{:S(2)}, u32[]{:S(2)}) collective-permute-start(f32[136,128]{1,0:T(8,128)S(1)} %add_add_fusion.1), channel_id=1, source_target_pairs={{0,24},{1,25},{2,26},{3,27},{4,28},{5,29},{6,30},{7,31},{8,16},{9,... | collective-permute-start | bytes 208904 | tf_op jit(solution)/shard_map/ppermute | solution.py:72
  23.3 5.5 %collective-permute-start.5 = (f32[136,128]{1,0:T(8,128)S(1)}, f32[136,128]{1,0:T(8,128)S(1)}, u32[]{:S(2)}, u32[]{:S(2)}) collective-permute-start(f32[136,128]{1,0:T(8,128)S(1)} %add_add_fusion.1), channel_id=1, source_target_pairs={{0,16},{1,17},{2,18},{3,19},{4,20},{5,21},{6,22},{7,23},{8,24},{9,... | collective-permute-start | bytes 208904 | tf_op jit(solution)/shard_map/ppermute | solution.py:72
  23.3 5.5 %collective-permute-start.4 = (f32[136,128]{1,0:T(8,128)S(1)}, f32[136,128]{1,0:T(8,128)S(1)}, u32[]{:S(2)}, u32[]{:S(2)}) collective-permute-start(f32[136,128]{1,0:T(8,128)S(1)} %add_add_fusion.1), channel_id=1, source_target_pairs={{0,8},{1,9},{2,10},{3,11},{4,12},{5,13},{6,14},{7,15},{8,0},{9,1},... | collective-permute-start | bytes 208904 | tf_op jit(solution)/shard_map/ppermute | solution.py:72
  28.9 1.3 %collective-permute-start.7 = (f32[136,128]{1,0:T(8,128)S(1)}, f32[136,128]{1,0:T(8,128)S(1)}, u32[]{:S(2)}, u32[]{:S(2)}) collective-permute-start(f32[136,128]{1,0:T(8,128)S(1)} %add_add_fusion), channel_id=1, source_target_pairs={{0,1},{1,0},{2,3},{3,2},{4,5},{5,4},{6,7},{7,6},{8,9},{9,8},{10,11... | collective-permute-start | bytes 208904 | tf_op jit(solution)/shard_map/ppermute | solution.py:72
  48.6 1.3 %collective-permute-start.8 = (f32[64,64]{1,0:T(8,128)S(1)}, f32[64,64]{1,0:T(8,128)S(1)}, u32[]{:S(2)}, u32[]{:S(2)}) collective-permute-start(f32[64,64]{1,0:T(8,128)S(1)} %fusion.29), channel_id=1, source_target_pairs={{0,1},{1,0},{2,3},{3,2},{4,5},{5,4},{6,7},{7,6},{8,9},{9,8},{10,11... | collective-permute-start | bytes 49160 | tf_op jit(solution)/shard_map/ppermute | solution.py:72
  69.8 1.3 %collective-permute-start.9 = (f32[64,64]{1,0:T(8,128)S(1)}, f32[64,64]{1,0:T(8,128)S(1)}, u32[]{:S(2)}, u32[]{:S(2)}) collective-permute-start(f32[64,64]{1,0:T(8,128)S(1)} %fusion.27), channel_id=1, source_target_pairs={{0,1},{1,0},{2,3},{3,2},{4,5},{5,4},{6,7},{7,6},{8,9},{9,8},{10,11... | collective-permute-start | bytes 49160 | tf_op jit(solution)/shard_map/ppermute | solution.py:72

commit v16 on v15

--- a/solution.py
+++ b/solution.py
@@ -102,8 +102,7 @@
 def bounded_cos(x):
     k = jnp.round(x * (1.0 / math.pi))
     r = x - k * 3.140625
-    r = r - k * 0.0009675025939941406
-    r = r - k * 1.5099580252808664e-07
+    r = r - k * 0.0009676535846665502
     r2 = r * r
     poly = -1.0 / 479001600.0 * r2 + 1.0 / 3628800.0
     poly = poly * r2 - 1.0 / 40320.0

time: 75.2 us -> 75 us (level)
  starting transfers between devices: 10.9 us -> 10 us
  waiting for transfers between devices: 11.5 us -> 12.4 us
    ppermute x10, waiting for transfers between devices: 11.5 us -> 12.4 us  [flip(): return lax.ppermute(array, axes, [(i, i ^ mask) for i in range(count)])]
    ppermute x10, starting transfers between devices: 10.9 us -> 10 us  [flip(): return lax.ppermute(array, axes, [(i, i ^ mask) for i in range(count)])]
where the time goes in v16:
time: 75 us; the launch traced here: 74.7 us
  other arithmetic  36.4 us (49%)
  waiting for transfers between devices  12.4 us (17%)
  matrix products  12.3 us (16%)
  starting transfers between devices  10 us (13%)
  local copies, waits for them, and re-layouts  1.95 us (3%)
  between operations  1.6 us (2%)
    ppermute x10, waiting for transfers between devices, flip(): return lax.ppermute(array, axes, [(i, i ^ mask) for i in range(count)])  12.4 us
    another operation x3, other arithmetic, cholesky_and_inverse(): l22 = lax.linalg.cholesky(g22 - mm(l21, l21.T), symmetrize_input=False)  12.4 us
    another operation x3, other arithmetic, cholesky_and_inverse(): l11 = lax.linalg.cholesky(g11, symmetrize_input=False)  12.4 us
    ppermute x10, starting transfers between devices, flip(): return lax.ppermute(array, axes, [(i, i ^ mask) for i in range(count)])  10 us
    another operation x4, other arithmetic, shared_inverse(): lax.linalg.triangular_solve(block, jnp.eye(q, dtype=lower.dtype), left_si...  9.95 us
    dot_general x1, matrix products, per_device(): jnp.dot(inputs, freqs, precision=lax.Precision.HIGHEST) + phases[None, :]  4.46 us
    dot_general x1, matrix products, per_device(): lax.dot_general(features, inverse, (((1,), (1,)), ((), ())), precision=la...  3.18 us
    dot_general x4, matrix products, tdot(): lax.dot_general(a, b, (((0,), (0,)), ((), ())), preferred_element_type=jn...  2.32 us
  transfers between devices with their start and end apart: 10, of which 9 were waited for; matrix products, arithmetic and copies ran while one was open for 1% of the time, Pallas kernels for 0%

profile of v16, /device:TPU:0, one launch (start us, length us, event | category | flops | bytes accessed | tf_op | source)
XLA Modules:
  0.0 74.7 jit_solution(1218129974902452248)
XLA Ops:
  1.4 0.7 sqrt.3
  2.1 4.5 %fusion.2 = f32[2048,256]{1,0:T(8,128)S(1)} fusion(f32[2048,64]{0,1:T(8,128)S(1)} %copy-done, f32[64,256]{1,0:T(8,128)} %param.10, f32[256]{0:T(256)} %param.11, f32[2048]{0:T(1024)S(1)} %sqrt.3), kind=kOutput, calls=%fused_computation.11 | convolution fusion | flops 416808960 | bytes 2696192 | tf_op jit(solution)/shard_map/dot_general | solution.py:134
  6.6 0.7 fusion.3
  7.3 0.6 convolution_add_fusion.2
  9.8 0.9 %collective-permute-done = f32[136,128]{1,0:T(8,128)S(1)} collective-permute-done((f32[136,128]{1,0:T(8,128)S(1)}, f32[136,128]{1,0:T(8,128)S(1)}, u32[]{:S(2)}, u32[]{:S(2)}) %collective-permute-start) | collective-permute-done | bytes 69664 | tf_op jit(solution)/shard_map/ppermute | solution.py:72
  10.8 3.8 %collective-permute-start.3 = (f32[136,128]{1,0:T(8,128)S(1)}, f32[136,128]{1,0:T(8,128)S(1)}, u32[]{:S(2)}, u32[]{:S(2)}) collective-permute-start(f32[136,128]{1,0:T(8,128)S(1)} %select_add_fusion), channel_id=1, source_target_pairs={{0,6},{1,7},{2,4},{3,5},{4,2},{5,3},{6,0},{7,1},{8,14},{9,15},{10,... | collective-permute-start | bytes 208904 | tf_op jit(solution)/shard_map/ppermute | solution.py:72
  15.3 1.9 %collective-permute-done.3 = f32[136,128]{1,0:T(8,128)S(1)} collective-permute-done((f32[136,128]{1,0:T(8,128)S(1)}, f32[136,128]{1,0:T(8,128)S(1)}, u32[]{:S(2)}, u32[]{:S(2)}) %collective-permute-start.3) | collective-permute-done | bytes 69664 | tf_op jit(solution)/shard_map/ppermute | solution.py:72
  17.3 1.7 %collective-permute-done.2 = f32[136,128]{1,0:T(8,128)S(1)} collective-permute-done((f32[136,128]{1,0:T(8,128)S(1)}, f32[136,128]{1,0:T(8,128)S(1)}, u32[]{:S(2)}, u32[]{:S(2)}) %collective-permute-start.2) | collective-permute-done | bytes 69664 | tf_op jit(solution)/shard_map/ppermute | solution.py:72
  19.5 3.7 %collective-permute-start.6 = (f32[136,128]{1,0:T(8,128)S(1)}, f32[136,128]{1,0:T(8,128)S(1)}, u32[]{:S(2)}, u32[]{:S(2)}) collective-permute-start(f32[136,128]{1,0:T(8,128)S(1)} %add_add_fusion.1), channel_id=1, source_target_pairs={{0,24},{1,25},{2,26},{3,27},{4,28},{5,29},{6,30},{7,31},{8,16},{9,... | collective-permute-start | bytes 208904 | tf_op jit(solution)/shard_map/ppermute | solution.py:72
  23.2 0.8 %collective-permute-start.4 = (f32[136,128]{1,0:T(8,128)S(1)}, f32[136,128]{1,0:T(8,128)S(1)}, u32[]{:S(2)}, u32[]{:S(2)}) collective-permute-start(f32[136,128]{1,0:T(8,128)S(1)} %add_add_fusion.1), channel_id=1, source_target_pairs={{0,8},{1,9},{2,10},{3,11},{4,12},{5,13},{6,14},{7,15},{8,0},{9,1},... | collective-permute-start | bytes 208904 | tf_op jit(solution)/shard_map/ppermute | solution.py:72
  24.0 2.0 %collective-permute-done.6 = f32[136,128]{1,0:T(8,128)S(1)} collective-permute-done((f32[136,128]{1,0:T(8,128)S(1)}, f32[136,128]{1,0:T(8,128)S(1)}, u32[]{:S(2)}, u32[]{:S(2)}) %collective-permute-start.6) | collective-permute-done | bytes 69664 | tf_op jit(solution)/shard_map/ppermute | solution.py:72
  26.0 2.9 %collective-permute-done.5 = f32[136,128]{1,0:T(8,128)S(1)} collective-permute-done((f32[136,128]{1,0:T(8,128)S(1)}, f32[136,128]{1,0:T(8,128)S(1)}, u32[]{:S(2)}, u32[]{:S(2)}) %collective-permute-start.5) | collective-permute-done | bytes 69664 | tf_op jit(solution)/shard_map/ppermute | solution.py:72
  28.9 1.2 %collective-permute-done.7 = f32[136,128]{1,0:T(8,128)S(1)} collective-permute-done((f32[136,128]{1,0:T(8,128)S(1)}, f32[136,128]{1,0:T(8,128)S(1)}, u32[]{:S(2)}, u32[]{:S(2)}) %collective-permute-start.7) | collective-permute-done | bytes 69664 | tf_op jit(solution)/shard_map/ppermute | solution.py:72
  30.3 11.7 %custom-call.8 = f32[128,128]{1,0:T(8,128)S(1)} custom-call(f32[128,128]{1,0:T(8,128)S(1)} %bitcast_select_fusion.1), custom_call_target="Cholesky" | custom-call | tf_op jit(solution)/shard_map/cholesky/custom-call.1 | solution.py:33
  42.1 0.6 compare_reduce_fusion.1
  42.7 0.7 select_select_fusion.1
  43.4 4.9 %custom-call.9 = f32[1,64,64]{1,2,0:T(8,128)S(1)} custom-call(f32[1,64,64]{2,1,0:T(8,128)S(1)} %fusion.38), custom_call_target="InvertDiagBlocksLowerTriangular" | custom-call | tf_op jit(solution)/shard_map/triangular_solve/custom-call.0 | solution.py:21
  48.8 1.0 %collective-permute-done.8 = f32[64,64]{1,0:T(8,128)S(1)} collective-permute-done((f32[64,64]{1,0:T(8,128)S(1)}, f32[64,64]{1,0:T(8,128)S(1)}, u32[]{:S(2)}, u32[]{:S(2)}) %collective-permute-start.8) | collective-permute-done | bytes 16416 | tf_op jit(solution)/shard_map/ppermute | solution.py:72
  51.4 11.7 %custom-call.10 = f32[128,128]{1,0:T(8,128)S(1)} custom-call(f32[128,128]{1,0:T(8,128)S(1)} %fusion.24), custom_call_target="Cholesky" | custom-call | tf_op jit(solution)/shard_map/cholesky/custom-call.1 | solution.py:36
  63.1 0.6 compare_reduce_fusion
  63.8 0.7 select_select_fusion
  64.5 4.9 %custom-call.11 = f32[1,64,64]{1,2,0:T(8,128)S(1)} custom-call(f32[1,64,64]{2,1,0:T(8,128)S(1)} %fusion.34), custom_call_target="InvertDiagBlocksLowerTriangular" | custom-call | tf_op jit(solution)/shard_map/triangular_solve/custom-call.0 | solution.py:21
  69.9 0.8 %copy.13 = f32[256,256]{1,0:T(8,128)} copy(f32[256,256]{0,1:T(8,128)S(1)} %fusion.6) | data formatting | bytes 524288
  71.6 3.2 %convolution_multiply_fusion = f32[2048,256]{1,0:T(8,128)} fusion(f32[2048,256]{1,0:T(8,128)S(1)} %fusion.2, f32[128,128]{1,0:T(8,128)S(1)} %select_maximum_fusion.3, f32[64,64]{1,0:T(8,128)S(1)} %get-tuple-element.10, f32[64,64]{1,0:T(8,128)S(1)} %convolution_negate_fusion.1, f32[64,128]{1,0:T(8,128)S(1)} %concatenate.61, ...), kind=kOutput, calls=%fused_computation.6 | convolution fusion | flops 1611530240 | bytes 4390912 | tf_op jit(solution)/shard_map/dot_general | solution.py:141
  (48 shorter events, 6.9 us)
Async XLA Ops:
  0.6 1.5 %copy-start = (f32[2048,64]{0,1:T(8,128)S(1)}, f32[2048,64]{0,1:T(8,128)}, u32[]{:S(2)}) copy-start(f32[2048,64]{0,1:T(8,128)} %param.9) | copy-start | bytes 1572868
  9.3 1.5 %collective-permute-start = (f32[136,128]{1,0:T(8,128)S(1)}, f32[136,128]{1,0:T(8,128)S(1)}, u32[]{:S(2)}, u32[]{:S(2)}) collective-permute-start(f32[136,128]{1,0:T(8,128)S(1)} %pad_select_fusion), channel_id=1, source_target_pairs={{0,1},{1,0},{2,3},{3,2},{4,5},{5,4},{6,7},{7,6},{8,9},{9,8},{10,11... | collective-permute-start | bytes 208904 | tf_op jit(solution)/shard_map/ppermute | solution.py:72
  10.8 6.4 %collective-permute-start.3 = (f32[136,128]{1,0:T(8,128)S(1)}, f32[136,128]{1,0:T(8,128)S(1)}, u32[]{:S(2)}, u32[]{:S(2)}) collective-permute-start(f32[136,128]{1,0:T(8,128)S(1)} %select_add_fusion), channel_id=1, source_target_pairs={{0,6},{1,7},{2,4},{3,5},{4,2},{5,3},{6,0},{7,1},{8,14},{9,15},{10,... | collective-permute-start | bytes 208904 | tf_op jit(solution)/shard_map/ppermute | solution.py:72
  14.7 4.3 %collective-permute-start.2 = (f32[136,128]{1,0:T(8,128)S(1)}, f32[136,128]{1,0:T(8,128)S(1)}, u32[]{:S(2)}, u32[]{:S(2)}) collective-permute-start(f32[136,128]{1,0:T(8,128)S(1)} %select_add_fusion), channel_id=1, source_target_pairs={{0,4},{1,5},{2,6},{3,7},{4,0},{5,1},{6,2},{7,3},{8,12},{9,13},{10,... | collective-permute-start | bytes 208904 | tf_op jit(solution)/shard_map/ppermute | solution.py:72
  15.2 4.3 %collective-permute-start.1 = (f32[136,128]{1,0:T(8,128)S(1)}, f32[136,128]{1,0:T(8,128)S(1)}, u32[]{:S(2)}, u32[]{:S(2)}) collective-permute-start(f32[136,128]{1,0:T(8,128)S(1)} %select_add_fusion), channel_id=1, source_target_pairs={{0,2},{1,3},{2,0},{3,1},{4,6},{5,7},{6,4},{7,5},{8,10},{9,11},{10,... | collective-permute-start | bytes 208904 | tf_op jit(solution)/shard_map/ppermute | solution.py:72
  19.5 6.4 %collective-permute-start.6 = (f32[136,128]{1,0:T(8,128)S(1)}, f32[136,128]{1,0:T(8,128)S(1)}, u32[]{:S(2)}, u32[]{:S(2)}) collective-permute-start(f32[136,128]{1,0:T(8,128)S(1)} %add_add_fusion.1), channel_id=1, source_target_pairs={{0,24},{1,25},{2,26},{3,27},{4,28},{5,29},{6,30},{7,31},{8,16},{9,... | collective-permute-start | bytes 208904 | tf_op jit(solution)/shard_map/ppermute | solution.py:72
  23.2 5.6 %collective-permute-start.5 = (f32[136,128]{1,0:T(8,128)S(1)}, f32[136,128]{1,0:T(8,128)S(1)}, u32[]{:S(2)}, u32[]{:S(2)}) collective-permute-start(f32[136,128]{1,0:T(8,128)S(1)} %add_add_fusion.1), channel_id=1, source_target_pairs={{0,16},{1,17},{2,18},{3,19},{4,20},{5,21},{6,22},{7,23},{8,24},{9,... | collective-permute-start | bytes 208904 | tf_op jit(solution)/shard_map/ppermute | solution.py:72
  23.2 5.6 %collective-permute-start.4 = (f32[136,128]{1,0:T(8,128)S(1)}, f32[136,128]{1,0:T(8,128)S(1)}, u32[]{:S(2)}, u32[]{:S(2)}) collective-permute-start(f32[136,128]{1,0:T(8,128)S(1)} %add_add_fusion.1), channel_id=1, source_target_pairs={{0,8},{1,9},{2,10},{3,11},{4,12},{5,13},{6,14},{7,15},{8,0},{9,1},... | collective-permute-start | bytes 208904 | tf_op jit(solution)/shard_map/ppermute | solution.py:72
  28.8 1.3 %collective-permute-start.7 = (f32[136,128]{1,0:T(8,128)S(1)}, f32[136,128]{1,0:T(8,128)S(1)}, u32[]{:S(2)}, u32[]{:S(2)}) collective-permute-start(f32[136,128]{1,0:T(8,128)S(1)} %add_add_fusion), channel_id=1, source_target_pairs={{0,1},{1,0},{2,3},{3,2},{4,5},{5,4},{6,7},{7,6},{8,9},{9,8},{10,11... | collective-permute-start | bytes 208904 | tf_op jit(solution)/shard_map/ppermute | solution.py:72
  48.6 1.3 %collective-permute-start.8 = (f32[64,64]{1,0:T(8,128)S(1)}, f32[64,64]{1,0:T(8,128)S(1)}, u32[]{:S(2)}, u32[]{:S(2)}) collective-permute-start(f32[64,64]{1,0:T(8,128)S(1)} %fusion.29), channel_id=1, source_target_pairs={{0,1},{1,0},{2,3},{3,2},{4,5},{5,4},{6,7},{7,6},{8,9},{9,8},{10,11... | collective-permute-start | bytes 49160 | tf_op jit(solution)/shard_map/ppermute | solution.py:72
  69.7 1.3 %collective-permute-start.9 = (f32[64,64]{1,0:T(8,128)S(1)}, f32[64,64]{1,0:T(8,128)S(1)}, u32[]{:S(2)}, u32[]{:S(2)}) collective-permute-start(f32[64,64]{1,0:T(8,128)S(1)} %fusion.27), channel_id=1, source_target_pairs={{0,1},{1,0},{2,3},{3,2},{4,5},{5,4},{6,7},{7,6},{8,9},{9,8},{10,11... | collective-permute-start | bytes 49160 | tf_op jit(solution)/shard_map/ppermute | solution.py:72

commit v17 on v16

--- a/solution.py
+++ b/solution.py
@@ -104,12 +104,11 @@
     r = x - k * 3.140625
     r = r - k * 0.0009676535846665502
     r2 = r * r
-    poly = -1.0 / 479001600.0 * r2 + 1.0 / 3628800.0
-    poly = poly * r2 - 1.0 / 40320.0
-    poly = poly * r2 + 1.0 / 720.0
-    poly = poly * r2 - 1.0 / 24.0
-    poly = poly * r2 + 0.5
-    value = 1.0 - poly * r2
+    poly = -2.61909292476048e-07 * r2 + 2.4769165975158103e-05
+    poly = poly * r2 - 0.0013888566754758358
+    poly = poly * r2 + 0.041666656732559204
+    poly = poly * r2 - 0.5
+    value = poly * r2 + 1.0
     half = k * 0.5
     return jnp.where(jnp.floor(half) == half, value, -value)
 

time: 75 us -> 74.8 us (level)
  no operation moved by 1% of the time
where the time goes in v17:
time: 74.8 us; the launch traced here: 74.5 us
  other arithmetic  36.4 us (49%)
  matrix products  12.3 us (16%)
  waiting for transfers between devices  12.3 us (16%)
  starting transfers between devices  10 us (13%)
  local copies, waits for them, and re-layouts  1.95 us (3%)
  between operations  1.6 us (2%)
    another operation x3, other arithmetic, cholesky_and_inverse(): l22 = lax.linalg.cholesky(g22 - mm(l21, l21.T), symmetrize_input=False)  12.4 us
    another operation x3, other arithmetic, cholesky_and_inverse(): l11 = lax.linalg.cholesky(g11, symmetrize_input=False)  12.4 us
    ppermute x10, waiting for transfers between devices, flip(): return lax.ppermute(array, axes, [(i, i ^ mask) for i in range(count)])  12.3 us
    ppermute x10, starting transfers between devices, flip(): return lax.ppermute(array, axes, [(i, i ^ mask) for i in range(count)])  10 us
    another operation x4, other arithmetic, shared_inverse(): lax.linalg.triangular_solve(block, jnp.eye(q, dtype=lower.dtype), left_si...  9.95 us
    dot_general x1, matrix products, per_device(): jnp.dot(inputs, freqs, precision=lax.Precision.HIGHEST) + phases[None, :]  4.34 us
    dot_general x1, matrix products, per_device(): lax.dot_general(features, inverse, (((1,), (1,)), ((), ())), precision=la...  3.18 us
    dot_general x4, matrix products, tdot(): lax.dot_general(a, b, (((0,), (0,)), ((), ())), preferred_element_type=jn...  2.32 us
  transfers between devices with their start and end apart: 10, of which 9 were waited for; matrix products, arithmetic and copies ran while one was open for 1% of the time, Pallas kernels for 0%

profile of v17, /device:TPU:0, one launch (start us, length us, event | category | flops | bytes accessed | tf_op | source)
XLA Modules:
  0.0 74.5 jit_solution(12229463396572827385)
XLA Ops:
  1.4 0.7 sqrt.3
  2.1 4.3 %fusion.2 = f32[2048,256]{1,0:T(8,128)S(1)} fusion(f32[2048,64]{0,1:T(8,128)S(1)} %copy-done, f32[64,256]{1,0:T(8,128)} %param.10, f32[256]{0:T(256)} %param.11, f32[2048]{0:T(1024)S(1)} %sqrt.3), kind=kOutput, calls=%fused_computation.11 | convolution fusion | flops 415760384 | bytes 2696192 | tf_op jit(solution)/shard_map/dot_general | solution.py:133
  6.5 0.7 fusion.3
  7.1 0.6 convolution_add_fusion.2
  9.7 0.9 %collective-permute-done = f32[136,128]{1,0:T(8,128)S(1)} collective-permute-done((f32[136,128]{1,0:T(8,128)S(1)}, f32[136,128]{1,0:T(8,128)S(1)}, u32[]{:S(2)}, u32[]{:S(2)}) %collective-permute-start) | collective-permute-done | bytes 69664 | tf_op jit(solution)/shard_map/ppermute | solution.py:72
  10.7 3.9 %collective-permute-start.3 = (f32[136,128]{1,0:T(8,128)S(1)}, f32[136,128]{1,0:T(8,128)S(1)}, u32[]{:S(2)}, u32[]{:S(2)}) collective-permute-start(f32[136,128]{1,0:T(8,128)S(1)} %select_add_fusion), channel_id=1, source_target_pairs={{0,6},{1,7},{2,4},{3,5},{4,2},{5,3},{6,0},{7,1},{8,14},{9,15},{10,... | collective-permute-start | bytes 208904 | tf_op jit(solution)/shard_map/ppermute | solution.py:72
  15.2 1.9 %collective-permute-done.3 = f32[136,128]{1,0:T(8,128)S(1)} collective-permute-done((f32[136,128]{1,0:T(8,128)S(1)}, f32[136,128]{1,0:T(8,128)S(1)}, u32[]{:S(2)}, u32[]{:S(2)}) %collective-permute-start.3) | collective-permute-done | bytes 69664 | tf_op jit(solution)/shard_map/ppermute | solution.py:72
  17.2 1.7 %collective-permute-done.2 = f32[136,128]{1,0:T(8,128)S(1)} collective-permute-done((f32[136,128]{1,0:T(8,128)S(1)}, f32[136,128]{1,0:T(8,128)S(1)}, u32[]{:S(2)}, u32[]{:S(2)}) %collective-permute-start.2) | collective-permute-done | bytes 69664 | tf_op jit(solution)/shard_map/ppermute | solution.py:72
  19.4 3.7 %collective-permute-start.6 = (f32[136,128]{1,0:T(8,128)S(1)}, f32[136,128]{1,0:T(8,128)S(1)}, u32[]{:S(2)}, u32[]{:S(2)}) collective-permute-start(f32[136,128]{1,0:T(8,128)S(1)} %add_add_fusion.1), channel_id=1, source_target_pairs={{0,24},{1,25},{2,26},{3,27},{4,28},{5,29},{6,30},{7,31},{8,16},{9,... | collective-permute-start | bytes 208904 | tf_op jit(solution)/shard_map/ppermute | solution.py:72
  23.1 0.8 %collective-permute-start.4 = (f32[136,128]{1,0:T(8,128)S(1)}, f32[136,128]{1,0:T(8,128)S(1)}, u32[]{:S(2)}, u32[]{:S(2)}) collective-permute-start(f32[136,128]{1,0:T(8,128)S(1)} %add_add_fusion.1), channel_id=1, source_target_pairs={{0,8},{1,9},{2,10},{3,11},{4,12},{5,13},{6,14},{7,15},{8,0},{9,1},... | collective-permute-start | bytes 208904 | tf_op jit(solution)/shard_map/ppermute | solution.py:72
  23.9 2.0 %collective-permute-done.6 = f32[136,128]{1,0:T(8,128)S(1)} collective-permute-done((f32[136,128]{1,0:T(8,128)S(1)}, f32[136,128]{1,0:T(8,128)S(1)}, u32[]{:S(2)}, u32[]{:S(2)}) %collective-permute-start.6) | collective-permute-done | bytes 69664 | tf_op jit(solution)/shard_map/ppermute | solution.py:72
  25.9 2.6 %collective-permute-done.5 = f32[136,128]{1,0:T(8,128)S(1)} collective-permute-done((f32[136,128]{1,0:T(8,128)S(1)}, f32[136,128]{1,0:T(8,128)S(1)}, u32[]{:S(2)}, u32[]{:S(2)}) %collective-permute-start.5) | collective-permute-done | bytes 69664 | tf_op jit(solution)/shard_map/ppermute | solution.py:72
  28.6 1.2 %collective-permute-done.7 = f32[136,128]{1,0:T(8,128)S(1)} collective-permute-done((f32[136,128]{1,0:T(8,128)S(1)}, f32[136,128]{1,0:T(8,128)S(1)}, u32[]{:S(2)}, u32[]{:S(2)}) %collective-permute-start.7) | collective-permute-done | bytes 69664 | tf_op jit(solution)/shard_map/ppermute | solution.py:72
  30.0 11.7 %custom-call.8 = f32[128,128]{1,0:T(8,128)S(1)} custom-call(f32[128,128]{1,0:T(8,128)S(1)} %bitcast_select_fusion.1), custom_call_target="Cholesky" | custom-call | tf_op jit(solution)/shard_map/cholesky/custom-call.1 | solution.py:33
  41.8 0.6 compare_reduce_fusion.1
  42.4 0.7 select_select_fusion.1
  43.2 4.9 %custom-call.9 = f32[1,64,64]{1,2,0:T(8,128)S(1)} custom-call(f32[1,64,64]{2,1,0:T(8,128)S(1)} %fusion.38), custom_call_target="InvertDiagBlocksLowerTriangular" | custom-call | tf_op jit(solution)/shard_map/triangular_solve/custom-call.0 | solution.py:21
  48.6 1.0 %collective-permute-done.8 = f32[64,64]{1,0:T(8,128)S(1)} collective-permute-done((f32[64,64]{1,0:T(8,128)S(1)}, f32[64,64]{1,0:T(8,128)S(1)}, u32[]{:S(2)}, u32[]{:S(2)}) %collective-permute-start.8) | collective-permute-done | bytes 16416 | tf_op jit(solution)/shard_map/ppermute | solution.py:72
  51.2 11.7 %custom-call.10 = f32[128,128]{1,0:T(8,128)S(1)} custom-call(f32[128,128]{1,0:T(8,128)S(1)} %fusion.24), custom_call_target="Cholesky" | custom-call | tf_op jit(solution)/shard_map/cholesky/custom-call.1 | solution.py:36
  62.9 0.6 compare_reduce_fusion
  63.6 0.7 select_select_fusion
  64.3 4.9 %custom-call.11 = f32[1,64,64]{1,2,0:T(8,128)S(1)} custom-call(f32[1,64,64]{2,1,0:T(8,128)S(1)} %fusion.34), custom_call_target="InvertDiagBlocksLowerTriangular" | custom-call | tf_op jit(solution)/shard_map/triangular_solve/custom-call.0 | solution.py:21
  69.7 0.8 %copy.13 = f32[256,256]{1,0:T(8,128)} copy(f32[256,256]{0,1:T(8,128)S(1)} %fusion.6) | data formatting | bytes 524288
  71.3 3.2 %convolution_multiply_fusion = f32[2048,256]{1,0:T(8,128)} fusion(f32[2048,256]{1,0:T(8,128)S(1)} %fusion.2, f32[128,128]{1,0:T(8,128)S(1)} %select_maximum_fusion.3, f32[64,64]{1,0:T(8,128)S(1)} %get-tuple-element.10, f32[64,64]{1,0:T(8,128)S(1)} %convolution_negate_fusion.1, f32[64,128]{1,0:T(8,128)S(1)} %concatenate.61, ...), kind=kOutput, calls=%fused_computation.6 | convolution fusion | flops 1611530240 | bytes 4390912 | tf_op jit(solution)/shard_map/dot_general | solution.py:140
  (48 shorter events, 6.9 us)
Async XLA Ops:
  0.6 1.5 %copy-start = (f32[2048,64]{0,1:T(8,128)S(1)}, f32[2048,64]{0,1:T(8,128)}, u32[]{:S(2)}) copy-start(f32[2048,64]{0,1:T(8,128)} %param.9) | copy-start | bytes 1572868
  9.1 1.5 %collective-permute-start = (f32[136,128]{1,0:T(8,128)S(1)}, f32[136,128]{1,0:T(8,128)S(1)}, u32[]{:S(2)}, u32[]{:S(2)}) collective-permute-start(f32[136,128]{1,0:T(8,128)S(1)} %pad_select_fusion), channel_id=1, source_target_pairs={{0,1},{1,0},{2,3},{3,2},{4,5},{5,4},{6,7},{7,6},{8,9},{9,8},{10,11... | collective-permute-start | bytes 208904 | tf_op jit(solution)/shard_map/ppermute | solution.py:72
  10.7 6.4 %collective-permute-start.3 = (f32[136,128]{1,0:T(8,128)S(1)}, f32[136,128]{1,0:T(8,128)S(1)}, u32[]{:S(2)}, u32[]{:S(2)}) collective-permute-start(f32[136,128]{1,0:T(8,128)S(1)} %select_add_fusion), channel_id=1, source_target_pairs={{0,6},{1,7},{2,4},{3,5},{4,2},{5,3},{6,0},{7,1},{8,14},{9,15},{10,... | collective-permute-start | bytes 208904 | tf_op jit(solution)/shard_map/ppermute | solution.py:72
  14.6 4.3 %collective-permute-start.2 = (f32[136,128]{1,0:T(8,128)S(1)}, f32[136,128]{1,0:T(8,128)S(1)}, u32[]{:S(2)}, u32[]{:S(2)}) collective-permute-start(f32[136,128]{1,0:T(8,128)S(1)} %select_add_fusion), channel_id=1, source_target_pairs={{0,4},{1,5},{2,6},{3,7},{4,0},{5,1},{6,2},{7,3},{8,12},{9,13},{10,... | collective-permute-start | bytes 208904 | tf_op jit(solution)/shard_map/ppermute | solution.py:72
  15.1 4.3 %collective-permute-start.1 = (f32[136,128]{1,0:T(8,128)S(1)}, f32[136,128]{1,0:T(8,128)S(1)}, u32[]{:S(2)}, u32[]{:S(2)}) collective-permute-start(f32[136,128]{1,0:T(8,128)S(1)} %select_add_fusion), channel_id=1, source_target_pairs={{0,2},{1,3},{2,0},{3,1},{4,6},{5,7},{6,4},{7,5},{8,10},{9,11},{10,... | collective-permute-start | bytes 208904 | tf_op jit(solution)/shard_map/ppermute | solution.py:72
  19.4 6.5 %collective-permute-start.6 = (f32[136,128]{1,0:T(8,128)S(1)}, f32[136,128]{1,0:T(8,128)S(1)}, u32[]{:S(2)}, u32[]{:S(2)}) collective-permute-start(f32[136,128]{1,0:T(8,128)S(1)} %add_add_fusion.1), channel_id=1, source_target_pairs={{0,24},{1,25},{2,26},{3,27},{4,28},{5,29},{6,30},{7,31},{8,16},{9,... | collective-permute-start | bytes 208904 | tf_op jit(solution)/shard_map/ppermute | solution.py:72
  23.1 5.4 %collective-permute-start.5 = (f32[136,128]{1,0:T(8,128)S(1)}, f32[136,128]{1,0:T(8,128)S(1)}, u32[]{:S(2)}, u32[]{:S(2)}) collective-permute-start(f32[136,128]{1,0:T(8,128)S(1)} %add_add_fusion.1), channel_id=1, source_target_pairs={{0,16},{1,17},{2,18},{3,19},{4,20},{5,21},{6,22},{7,23},{8,24},{9,... | collective-permute-start | bytes 208904 | tf_op jit(solution)/shard_map/ppermute | solution.py:72
  23.1 5.4 %collective-permute-start.4 = (f32[136,128]{1,0:T(8,128)S(1)}, f32[136,128]{1,0:T(8,128)S(1)}, u32[]{:S(2)}, u32[]{:S(2)}) collective-permute-start(f32[136,128]{1,0:T(8,128)S(1)} %add_add_fusion.1), channel_id=1, source_target_pairs={{0,8},{1,9},{2,10},{3,11},{4,12},{5,13},{6,14},{7,15},{8,0},{9,1},... | collective-permute-start | bytes 208904 | tf_op jit(solution)/shard_map/ppermute | solution.py:72
  28.6 1.3 %collective-permute-start.7 = (f32[136,128]{1,0:T(8,128)S(1)}, f32[136,128]{1,0:T(8,128)S(1)}, u32[]{:S(2)}, u32[]{:S(2)}) collective-permute-start(f32[136,128]{1,0:T(8,128)S(1)} %add_add_fusion), channel_id=1, source_target_pairs={{0,1},{1,0},{2,3},{3,2},{4,5},{5,4},{6,7},{7,6},{8,9},{9,8},{10,11... | collective-permute-start | bytes 208904 | tf_op jit(solution)/shard_map/ppermute | solution.py:72
  48.3 1.3 %collective-permute-start.8 = (f32[64,64]{1,0:T(8,128)S(1)}, f32[64,64]{1,0:T(8,128)S(1)}, u32[]{:S(2)}, u32[]{:S(2)}) collective-permute-start(f32[64,64]{1,0:T(8,128)S(1)} %fusion.29), channel_id=1, source_target_pairs={{0,1},{1,0},{2,3},{3,2},{4,5},{5,4},{6,7},{7,6},{8,9},{9,8},{10,11... | collective-permute-start | bytes 49160 | tf_op jit(solution)/shard_map/ppermute | solution.py:72
  69.5 1.3 %collective-permute-start.9 = (f32[64,64]{1,0:T(8,128)S(1)}, f32[64,64]{1,0:T(8,128)S(1)}, u32[]{:S(2)}, u32[]{:S(2)}) collective-permute-start(f32[64,64]{1,0:T(8,128)S(1)} %fusion.27), channel_id=1, source_target_pairs={{0,1},{1,0},{2,3},{3,2},{4,5},{5,4},{6,7},{7,6},{8,9},{9,8},{10,11... | collective-permute-start | bytes 49160 | tf_op jit(solution)/shard_map/ppermute | solution.py:72

commit v18 on v17

--- a/solution.py
+++ b/solution.py
@@ -131,7 +131,7 @@
     total_rows = inputs.shape[0] * lax.axis_size("grp") * lax.axis_size("leaf")
     norm_scale = 1.0 / math.sqrt(total_rows)
     proj = jnp.dot(inputs, freqs, precision=lax.Precision.HIGHEST) + phases[None, :]
-    features = jnp.sqrt(sample_weight)[:, None] * bounded_cos(proj) * norm_scale
+    features = (jnp.sqrt(sample_weight) * norm_scale)[:, None] * bounded_cos(proj)
     slot = lax.axis_index("grp") * lax.axis_size("leaf") + lax.axis_index("leaf")
     running = jnp.where(slot == root[0], stored[0], jnp.zeros_like(stored[0]))
     gram = split_gram(jnp.concatenate([features, running], axis=0))

time: 74.8 us -> 74.9 us (level)
  no operation moved by 1% of the time
where the time goes in v18:
time: 74.9 us; the launch traced here: 74.6 us
  other arithmetic  37.1 us (50%)
  waiting for transfers between devices  12.4 us (17%)
  matrix products  12.2 us (16%)
  starting transfers between devices  10 us (13%)
  between operations  1.61 us (2%)
  local copies, waits for them, and re-layouts  1.24 us (2%)
    ppermute x10, waiting for transfers between devices, flip(): return lax.ppermute(array, axes, [(i, i ^ mask) for i in range(count)])  12.4 us
    another operation x3, other arithmetic, cholesky_and_inverse(): l22 = lax.linalg.cholesky(g22 - mm(l21, l21.T), symmetrize_input=False)  12.4 us
    another operation x3, other arithmetic, cholesky_and_inverse(): l11 = lax.linalg.cholesky(g11, symmetrize_input=False)  12.4 us
    ppermute x10, starting transfers between devices, flip(): return lax.ppermute(array, axes, [(i, i ^ mask) for i in range(count)])  10 us
    another operation x4, other arithmetic, shared_inverse(): lax.linalg.triangular_solve(block, jnp.eye(q, dtype=lower.dtype), left_si...  9.95 us
    dot_general x1, matrix products, per_device(): jnp.dot(inputs, freqs, precision=lax.Precision.HIGHEST) + phases[None, :]  4.27 us
    dot_general x1, matrix products, per_device(): lax.dot_general(features, inverse, (((1,), (1,)), ((), ())), precision=la...  3.18 us
    dot_general x4, matrix products, tdot(): lax.dot_general(a, b, (((0,), (0,)), ((), ())), preferred_element_type=jn...  2.32 us
  transfers between devices with their start and end apart: 10, of which 9 were waited for; matrix products, arithmetic and copies ran while one was open for 1% of the time, Pallas kernels for 0%

profile of v18, /device:TPU:0, one launch (start us, length us, event | category | flops | bytes accessed | tf_op | source)
XLA Modules:
  0.0 74.6 jit_solution(17652914198825305710)
XLA Ops:
  1.4 0.7 sqrt_multiply_fusion
  2.1 4.3 %fusion.1 = f32[2048,256]{1,0:T(8,128)S(1)} fusion(f32[2048,64]{0,1:T(8,128)S(1)} %copy-done, f32[64,256]{1,0:T(8,128)} %param.10, f32[256]{0:T(256)} %param.11, f32[2048]{0:T(1024)S(1)} %sqrt_multiply_fusion), kind=kOutput, calls=%fused_computation.10 | convolution fusion | flops 415236096 | bytes 2696192 | tf_op jit(solution)/shard_map/dot_general | solution.py:133
  6.4 0.7 fusion.2
  7.1 0.6 convolution_add_fusion.2
  9.6 0.9 %collective-permute-done = f32[136,128]{1,0:T(8,128)S(1)} collective-permute-done((f32[136,128]{1,0:T(8,128)S(1)}, f32[136,128]{1,0:T(8,128)S(1)}, u32[]{:S(2)}, u32[]{:S(2)}) %collective-permute-start) | collective-permute-done | bytes 69664 | tf_op jit(solution)/shard_map/ppermute | solution.py:72
  10.6 3.8 %collective-permute-start.3 = (f32[136,128]{1,0:T(8,128)S(1)}, f32[136,128]{1,0:T(8,128)S(1)}, u32[]{:S(2)}, u32[]{:S(2)}) collective-permute-start(f32[136,128]{1,0:T(8,128)S(1)} %select_add_fusion), channel_id=1, source_target_pairs={{0,6},{1,7},{2,4},{3,5},{4,2},{5,3},{6,0},{7,1},{8,14},{9,15},{10,... | collective-permute-start | bytes 208904 | tf_op jit(solution)/shard_map/ppermute | solution.py:72
  15.1 1.9 %collective-permute-done.3 = f32[136,128]{1,0:T(8,128)S(1)} collective-permute-done((f32[136,128]{1,0:T(8,128)S(1)}, f32[136,128]{1,0:T(8,128)S(1)}, u32[]{:S(2)}, u32[]{:S(2)}) %collective-permute-start.3) | collective-permute-done | bytes 69664 | tf_op jit(solution)/shard_map/ppermute | solution.py:72
  17.1 1.7 %collective-permute-done.2 = f32[136,128]{1,0:T(8,128)S(1)} collective-permute-done((f32[136,128]{1,0:T(8,128)S(1)}, f32[136,128]{1,0:T(8,128)S(1)}, u32[]{:S(2)}, u32[]{:S(2)}) %collective-permute-start.2) | collective-permute-done | bytes 69664 | tf_op jit(solution)/shard_map/ppermute | solution.py:72
  19.4 3.7 %collective-permute-start.6 = (f32[136,128]{1,0:T(8,128)S(1)}, f32[136,128]{1,0:T(8,128)S(1)}, u32[]{:S(2)}, u32[]{:S(2)}) collective-permute-start(f32[136,128]{1,0:T(8,128)S(1)} %add_add_fusion.1), channel_id=1, source_target_pairs={{0,24},{1,25},{2,26},{3,27},{4,28},{5,29},{6,30},{7,31},{8,16},{9,... | collective-permute-start | bytes 208904 | tf_op jit(solution)/shard_map/ppermute | solution.py:72
  23.0 0.8 %collective-permute-start.4 = (f32[136,128]{1,0:T(8,128)S(1)}, f32[136,128]{1,0:T(8,128)S(1)}, u32[]{:S(2)}, u32[]{:S(2)}) collective-permute-start(f32[136,128]{1,0:T(8,128)S(1)} %add_add_fusion.1), channel_id=1, source_target_pairs={{0,8},{1,9},{2,10},{3,11},{4,12},{5,13},{6,14},{7,15},{8,0},{9,1},... | collective-permute-start | bytes 208904 | tf_op jit(solution)/shard_map/ppermute | solution.py:72
  23.8 2.0 %collective-permute-done.6 = f32[136,128]{1,0:T(8,128)S(1)} collective-permute-done((f32[136,128]{1,0:T(8,128)S(1)}, f32[136,128]{1,0:T(8,128)S(1)}, u32[]{:S(2)}, u32[]{:S(2)}) %collective-permute-start.6) | collective-permute-done | bytes 69664 | tf_op jit(solution)/shard_map/ppermute | solution.py:72
  25.8 2.9 %collective-permute-done.5 = f32[136,128]{1,0:T(8,128)S(1)} collective-permute-done((f32[136,128]{1,0:T(8,128)S(1)}, f32[136,128]{1,0:T(8,128)S(1)}, u32[]{:S(2)}, u32[]{:S(2)}) %collective-permute-start.5) | collective-permute-done | bytes 69664 | tf_op jit(solution)/shard_map/ppermute | solution.py:72
  28.7 1.2 %collective-permute-done.7 = f32[136,128]{1,0:T(8,128)S(1)} collective-permute-done((f32[136,128]{1,0:T(8,128)S(1)}, f32[136,128]{1,0:T(8,128)S(1)}, u32[]{:S(2)}, u32[]{:S(2)}) %collective-permute-start.7) | collective-permute-done | bytes 69664 | tf_op jit(solution)/shard_map/ppermute | solution.py:72
  30.1 11.7 %custom-call.8 = f32[128,128]{1,0:T(8,128)S(1)} custom-call(f32[128,128]{1,0:T(8,128)S(1)} %bitcast_select_fusion.1), custom_call_target="Cholesky" | custom-call | tf_op jit(solution)/shard_map/cholesky/custom-call.1 | solution.py:33
  41.9 0.6 compare_reduce_fusion.1
  42.5 0.7 select_select_fusion.1
  43.3 4.9 %custom-call.9 = f32[1,64,64]{1,2,0:T(8,128)S(1)} custom-call(f32[1,64,64]{2,1,0:T(8,128)S(1)} %fusion.37), custom_call_target="InvertDiagBlocksLowerTriangular" | custom-call | tf_op jit(solution)/shard_map/triangular_solve/custom-call.0 | solution.py:21
  48.6 1.0 %collective-permute-done.8 = f32[64,64]{1,0:T(8,128)S(1)} collective-permute-done((f32[64,64]{1,0:T(8,128)S(1)}, f32[64,64]{1,0:T(8,128)S(1)}, u32[]{:S(2)}, u32[]{:S(2)}) %collective-permute-start.8) | collective-permute-done | bytes 16416 | tf_op jit(solution)/shard_map/ppermute | solution.py:72
  51.3 11.7 %custom-call.10 = f32[128,128]{1,0:T(8,128)S(1)} custom-call(f32[128,128]{1,0:T(8,128)S(1)} %fusion.23), custom_call_target="Cholesky" | custom-call | tf_op jit(solution)/shard_map/cholesky/custom-call.1 | solution.py:36
  63.0 0.6 compare_reduce_fusion
  63.6 0.7 select_select_fusion
  64.4 4.9 %custom-call.11 = f32[1,64,64]{1,2,0:T(8,128)S(1)} custom-call(f32[1,64,64]{2,1,0:T(8,128)S(1)} %fusion.33), custom_call_target="InvertDiagBlocksLowerTriangular" | custom-call | tf_op jit(solution)/shard_map/triangular_solve/custom-call.0 | solution.py:21
  69.8 0.8 %copy.13 = f32[256,256]{1,0:T(8,128)} copy(f32[256,256]{0,1:T(8,128)S(1)} %fusion.5) | data formatting | bytes 524288
  71.5 3.2 %convolution_multiply_fusion = f32[2048,256]{1,0:T(8,128)} fusion(f32[2048,256]{1,0:T(8,128)S(1)} %fusion.1, f32[128,128]{1,0:T(8,128)S(1)} %select_maximum_fusion.3, f32[64,64]{1,0:T(8,128)S(1)} %get-tuple-element.10, f32[64,64]{1,0:T(8,128)S(1)} %convolution_negate_fusion.1, f32[64,128]{1,0:T(8,128)S(1)} %concatenate.61, ...), kind=kOutput, calls=%fused_computation.6 | convolution fusion | flops 1611530240 | bytes 4390912 | tf_op jit(solution)/shard_map/dot_general | solution.py:140
  (48 shorter events, 6.9 us)
Async XLA Ops:
  0.6 1.5 %copy-start = (f32[2048,64]{0,1:T(8,128)S(1)}, f32[2048,64]{0,1:T(8,128)}, u32[]{:S(2)}) copy-start(f32[2048,64]{0,1:T(8,128)} %param.9) | copy-start | bytes 1572868
  9.1 1.5 %collective-permute-start = (f32[136,128]{1,0:T(8,128)S(1)}, f32[136,128]{1,0:T(8,128)S(1)}, u32[]{:S(2)}, u32[]{:S(2)}) collective-permute-start(f32[136,128]{1,0:T(8,128)S(1)} %pad_select_fusion), channel_id=1, source_target_pairs={{0,1},{1,0},{2,3},{3,2},{4,5},{5,4},{6,7},{7,6},{8,9},{9,8},{10,11... | collective-permute-start | bytes 208904 | tf_op jit(solution)/shard_map/ppermute | solution.py:72
  10.6 6.4 %collective-permute-start.3 = (f32[136,128]{1,0:T(8,128)S(1)}, f32[136,128]{1,0:T(8,128)S(1)}, u32[]{:S(2)}, u32[]{:S(2)}) collective-permute-start(f32[136,128]{1,0:T(8,128)S(1)} %select_add_fusion), channel_id=1, source_target_pairs={{0,6},{1,7},{2,4},{3,5},{4,2},{5,3},{6,0},{7,1},{8,14},{9,15},{10,... | collective-permute-start | bytes 208904 | tf_op jit(solution)/shard_map/ppermute | solution.py:72
  14.5 4.3 %collective-permute-start.2 = (f32[136,128]{1,0:T(8,128)S(1)}, f32[136,128]{1,0:T(8,128)S(1)}, u32[]{:S(2)}, u32[]{:S(2)}) collective-permute-start(f32[136,128]{1,0:T(8,128)S(1)} %select_add_fusion), channel_id=1, source_target_pairs={{0,4},{1,5},{2,6},{3,7},{4,0},{5,1},{6,2},{7,3},{8,12},{9,13},{10,... | collective-permute-start | bytes 208904 | tf_op jit(solution)/shard_map/ppermute | solution.py:72
  15.0 4.3 %collective-permute-start.1 = (f32[136,128]{1,0:T(8,128)S(1)}, f32[136,128]{1,0:T(8,128)S(1)}, u32[]{:S(2)}, u32[]{:S(2)}) collective-permute-start(f32[136,128]{1,0:T(8,128)S(1)} %select_add_fusion), channel_id=1, source_target_pairs={{0,2},{1,3},{2,0},{3,1},{4,6},{5,7},{6,4},{7,5},{8,10},{9,11},{10,... | collective-permute-start | bytes 208904 | tf_op jit(solution)/shard_map/ppermute | solution.py:72
  19.4 6.4 %collective-permute-start.6 = (f32[136,128]{1,0:T(8,128)S(1)}, f32[136,128]{1,0:T(8,128)S(1)}, u32[]{:S(2)}, u32[]{:S(2)}) collective-permute-start(f32[136,128]{1,0:T(8,128)S(1)} %add_add_fusion.1), channel_id=1, source_target_pairs={{0,24},{1,25},{2,26},{3,27},{4,28},{5,29},{6,30},{7,31},{8,16},{9,... | collective-permute-start | bytes 208904 | tf_op jit(solution)/shard_map/ppermute | solution.py:72
  23.0 5.6 %collective-permute-start.5 = (f32[136,128]{1,0:T(8,128)S(1)}, f32[136,128]{1,0:T(8,128)S(1)}, u32[]{:S(2)}, u32[]{:S(2)}) collective-permute-start(f32[136,128]{1,0:T(8,128)S(1)} %add_add_fusion.1), channel_id=1, source_target_pairs={{0,16},{1,17},{2,18},{3,19},{4,20},{5,21},{6,22},{7,23},{8,24},{9,... | collective-permute-start | bytes 208904 | tf_op jit(solution)/shard_map/ppermute | solution.py:72
  23.0 5.6 %collective-permute-start.4 = (f32[136,128]{1,0:T(8,128)S(1)}, f32[136,128]{1,0:T(8,128)S(1)}, u32[]{:S(2)}, u32[]{:S(2)}) collective-permute-start(f32[136,128]{1,0:T(8,128)S(1)} %add_add_fusion.1), channel_id=1, source_target_pairs={{0,8},{1,9},{2,10},{3,11},{4,12},{5,13},{6,14},{7,15},{8,0},{9,1},... | collective-permute-start | bytes 208904 | tf_op jit(solution)/shard_map/ppermute | solution.py:72
  28.7 1.3 %collective-permute-start.7 = (f32[136,128]{1,0:T(8,128)S(1)}, f32[136,128]{1,0:T(8,128)S(1)}, u32[]{:S(2)}, u32[]{:S(2)}) collective-permute-start(f32[136,128]{1,0:T(8,128)S(1)} %add_add_fusion), channel_id=1, source_target_pairs={{0,1},{1,0},{2,3},{3,2},{4,5},{5,4},{6,7},{7,6},{8,9},{9,8},{10,11... | collective-permute-start | bytes 208904 | tf_op jit(solution)/shard_map/ppermute | solution.py:72
  48.4 1.3 %collective-permute-start.8 = (f32[64,64]{1,0:T(8,128)S(1)}, f32[64,64]{1,0:T(8,128)S(1)}, u32[]{:S(2)}, u32[]{:S(2)}) collective-permute-start(f32[64,64]{1,0:T(8,128)S(1)} %fusion.28), channel_id=1, source_target_pairs={{0,1},{1,0},{2,3},{3,2},{4,5},{5,4},{6,7},{7,6},{8,9},{9,8},{10,11... | collective-permute-start | bytes 49160 | tf_op jit(solution)/shard_map/ppermute | solution.py:72
  69.5 1.3 %collective-permute-start.9 = (f32[64,64]{1,0:T(8,128)S(1)}, f32[64,64]{1,0:T(8,128)S(1)}, u32[]{:S(2)}, u32[]{:S(2)}) collective-permute-start(f32[64,64]{1,0:T(8,128)S(1)} %fusion.26), channel_id=1, source_target_pairs={{0,1},{1,0},{2,3},{3,2},{4,5},{5,4},{6,7},{7,6},{8,9},{9,8},{10,11... | collective-permute-start | bytes 49160 | tf_op jit(solution)/shard_map/ppermute | solution.py:72

commit v19 on v18

--- a/solution.py
+++ b/solution.py
@@ -100,17 +100,16 @@
 
 
 def bounded_cos(x):
-    k = jnp.round(x * (1.0 / math.pi))
-    r = x - k * 3.140625
-    r = r - k * 0.0009676535846665502
+    k = jnp.round(x * (0.5 / math.pi))
+    r = x - k * 6.28125
+    r = r - k * 0.0019353071693331003
     r2 = r * r
-    poly = -2.61909292476048e-07 * r2 + 2.4769165975158103e-05
-    poly = poly * r2 - 0.0013888566754758358
-    poly = poly * r2 + 0.041666656732559204
-    poly = poly * r2 - 0.5
-    value = poly * r2 + 1.0
-    half = k * 0.5
-    return jnp.where(jnp.floor(half) == half, value, -value)
+    poly = -2.557707934336406e-10 * r2 + 9.675455459046134e-08
+    poly = poly * r2 + -2.1700885554309934e-05
+    poly = poly * r2 + 0.0026041660457849503
+    poly = poly * r2 + -0.125
+    half = poly * r2 + 1.0
+    return 2.0 * (half * half) - 1.0
 
 
 def split_gram(f):

time: 74.9 us -> 74.6 us (level)
  starting transfers between devices: 10 us -> 10.9 us
  waiting for transfers between devices: 12.4 us -> 11.5 us
    ppermute x10, waiting for transfers between devices: 12.4 us -> 11.5 us  [flip(): return lax.ppermute(array, axes, [(i, i ^ mask) for i in range(count)])]
    ppermute x10, starting transfers between devices: 10 us -> 10.9 us  [flip(): return lax.ppermute(array, axes, [(i, i ^ mask) for i in range(count)])]
where the time goes in v19:
time: 74.6 us; the launch traced here: 74.4 us
  other arithmetic  37.3 us (50%)
  matrix products  11.9 us (16%)
  waiting for transfers between devices  11.5 us (15%)
  starting transfers between devices  10.9 us (15%)
  between operations  1.6 us (2%)
  local copies, waits for them, and re-layouts  1.24 us (2%)
    another operation x3, other arithmetic, cholesky_and_inverse(): l22 = lax.linalg.cholesky(g22 - mm(l21, l21.T), symmetrize_input=False)  12.6 us
    another operation x3, other arithmetic, cholesky_and_inverse(): l11 = lax.linalg.cholesky(g11, symmetrize_input=False)  12.4 us
    ppermute x10, waiting for transfers between devices, flip(): return lax.ppermute(array, axes, [(i, i ^ mask) for i in range(count)])  11.5 us
    ppermute x10, starting transfers between devices, flip(): return lax.ppermute(array, axes, [(i, i ^ mask) for i in range(count)])  10.9 us
    another operation x4, other arithmetic, shared_inverse(): lax.linalg.triangular_solve(block, jnp.eye(q, dtype=lower.dtype), left_si...  9.95 us
    dot_general x1, matrix products, per_device(): jnp.dot(inputs, freqs, precision=lax.Precision.HIGHEST) + phases[None, :]  4.13 us
    dot_general x1, matrix products, per_device(): lax.dot_general(features, inverse, (((1,), (1,)), ((), ())), precision=la...  3.18 us
    dot_general x4, matrix products, tdot(): lax.dot_general(a, b, (((0,), (0,)), ((), ())), preferred_element_type=jn...  2.32 us
  transfers between devices with their start and end apart: 10, of which 9 were waited for; matrix products, arithmetic and copies ran while one was open for 1% of the time, Pallas kernels for 0%

profile of v19, /device:TPU:0, one launch (start us, length us, event | category | flops | bytes accessed | tf_op | source)
XLA Modules:
  0.0 74.4 jit_solution(8442065816771860589)
XLA Ops:
  1.4 0.7 sqrt_multiply_fusion
  2.1 4.1 %add_multiply_fusion = f32[2048,256]{1,0:T(8,128)S(1)} fusion(f32[2048,64]{0,1:T(8,128)S(1)} %copy-done, f32[64,256]{1,0:T(8,128)} %param.10, f32[256]{0:T(256)} %param.11, f32[2048]{0:T(1024)S(1)} %sqrt_multiply_fusion), kind=kOutput, calls=%fused_computation.8 | convolution fusion | flops 414187520 | bytes 2696192 | tf_op jit(solution)/shard_map/dot_general | solution.py:132
  6.2 0.7 fusion.1
  9.5 0.9 %collective-permute-done = f32[136,128]{1,0:T(8,128)S(1)} collective-permute-done((f32[136,128]{1,0:T(8,128)S(1)}, f32[136,128]{1,0:T(8,128)S(1)}, u32[]{:S(2)}, u32[]{:S(2)}) %collective-permute-start) | collective-permute-done | bytes 69664 | tf_op jit(solution)/shard_map/ppermute | solution.py:72
  10.5 3.8 %collective-permute-start.3 = (f32[136,128]{1,0:T(8,128)S(1)}, f32[136,128]{1,0:T(8,128)S(1)}, u32[]{:S(2)}, u32[]{:S(2)}) collective-permute-start(f32[136,128]{1,0:T(8,128)S(1)} %select_add_fusion), channel_id=1, source_target_pairs={{0,6},{1,7},{2,4},{3,5},{4,2},{5,3},{6,0},{7,1},{8,14},{9,15},{10,... | collective-permute-start | bytes 208904 | tf_op jit(solution)/shard_map/ppermute | solution.py:72
  14.3 1.5 %collective-permute-start.2 = (f32[136,128]{1,0:T(8,128)S(1)}, f32[136,128]{1,0:T(8,128)S(1)}, u32[]{:S(2)}, u32[]{:S(2)}) collective-permute-start(f32[136,128]{1,0:T(8,128)S(1)} %select_add_fusion), channel_id=1, source_target_pairs={{0,4},{1,5},{2,6},{3,7},{4,0},{5,1},{6,2},{7,3},{8,12},{9,13},{10,... | collective-permute-start | bytes 208904 | tf_op jit(solution)/shard_map/ppermute | solution.py:72
  15.8 1.1 %collective-permute-done.3 = f32[136,128]{1,0:T(8,128)S(1)} collective-permute-done((f32[136,128]{1,0:T(8,128)S(1)}, f32[136,128]{1,0:T(8,128)S(1)}, u32[]{:S(2)}, u32[]{:S(2)}) %collective-permute-start.3) | collective-permute-done | bytes 69664 | tf_op jit(solution)/shard_map/ppermute | solution.py:72
  16.9 2.6 %collective-permute-done.2 = f32[136,128]{1,0:T(8,128)S(1)} collective-permute-done((f32[136,128]{1,0:T(8,128)S(1)}, f32[136,128]{1,0:T(8,128)S(1)}, u32[]{:S(2)}, u32[]{:S(2)}) %collective-permute-start.2) | collective-permute-done | bytes 69664 | tf_op jit(solution)/shard_map/ppermute | solution.py:72
  20.2 2.7 %collective-permute-start.6 = (f32[136,128]{1,0:T(8,128)S(1)}, f32[136,128]{1,0:T(8,128)S(1)}, u32[]{:S(2)}, u32[]{:S(2)}) collective-permute-start(f32[136,128]{1,0:T(8,128)S(1)} %add_add_fusion.1), channel_id=1, source_target_pairs={{0,24},{1,25},{2,26},{3,27},{4,28},{5,29},{6,30},{7,31},{8,16},{9,... | collective-permute-start | bytes 208904 | tf_op jit(solution)/shard_map/ppermute | solution.py:72
  22.9 1.7 %collective-permute-start.4 = (f32[136,128]{1,0:T(8,128)S(1)}, f32[136,128]{1,0:T(8,128)S(1)}, u32[]{:S(2)}, u32[]{:S(2)}) collective-permute-start(f32[136,128]{1,0:T(8,128)S(1)} %add_add_fusion.1), channel_id=1, source_target_pairs={{0,8},{1,9},{2,10},{3,11},{4,12},{5,13},{6,14},{7,15},{8,0},{9,1},... | collective-permute-start | bytes 208904 | tf_op jit(solution)/shard_map/ppermute | solution.py:72
  24.6 1.8 %collective-permute-done.6 = f32[136,128]{1,0:T(8,128)S(1)} collective-permute-done((f32[136,128]{1,0:T(8,128)S(1)}, f32[136,128]{1,0:T(8,128)S(1)}, u32[]{:S(2)}, u32[]{:S(2)}) %collective-permute-start.6) | collective-permute-done | bytes 69664 | tf_op jit(solution)/shard_map/ppermute | solution.py:72
  26.5 1.9 %collective-permute-done.5 = f32[136,128]{1,0:T(8,128)S(1)} collective-permute-done((f32[136,128]{1,0:T(8,128)S(1)}, f32[136,128]{1,0:T(8,128)S(1)}, u32[]{:S(2)}, u32[]{:S(2)}) %collective-permute-start.5) | collective-permute-done | bytes 69664 | tf_op jit(solution)/shard_map/ppermute | solution.py:72
  28.5 1.2 %collective-permute-done.7 = f32[136,128]{1,0:T(8,128)S(1)} collective-permute-done((f32[136,128]{1,0:T(8,128)S(1)}, f32[136,128]{1,0:T(8,128)S(1)}, u32[]{:S(2)}, u32[]{:S(2)}) %collective-permute-start.7) | collective-permute-done | bytes 69664 | tf_op jit(solution)/shard_map/ppermute | solution.py:72
  29.9 11.7 %custom-call.8 = f32[128,128]{1,0:T(8,128)S(1)} custom-call(f32[128,128]{1,0:T(8,128)S(1)} %bitcast_select_fusion.1), custom_call_target="Cholesky" | custom-call | tf_op jit(solution)/shard_map/cholesky/custom-call.1 | solution.py:33
  41.6 0.6 compare_reduce_fusion.1
  42.3 0.7 select_select_fusion.1
  43.0 4.9 %custom-call.9 = f32[1,64,64]{1,2,0:T(8,128)S(1)} custom-call(f32[1,64,64]{2,1,0:T(8,128)S(1)} %fusion.36), custom_call_target="InvertDiagBlocksLowerTriangular" | custom-call | tf_op jit(solution)/shard_map/triangular_solve/custom-call.0 | solution.py:21
  48.4 1.0 %collective-permute-done.8 = f32[64,64]{1,0:T(8,128)S(1)} collective-permute-done((f32[64,64]{1,0:T(8,128)S(1)}, f32[64,64]{1,0:T(8,128)S(1)}, u32[]{:S(2)}, u32[]{:S(2)}) %collective-permute-start.8) | collective-permute-done | bytes 16416 | tf_op jit(solution)/shard_map/ppermute | solution.py:72
  50.8 11.9 %custom-call.10 = f32[128,128]{1,0:T(8,128)S(1)} custom-call(f32[128,128]{1,0:T(8,128)S(1)} %fusion.22), custom_call_target="Cholesky" | custom-call | tf_op jit(solution)/shard_map/cholesky/custom-call.1 | solution.py:36
  62.8 0.6 compare_reduce_fusion
  63.4 0.7 select_select_fusion
  64.1 4.9 %custom-call.11 = f32[1,64,64]{1,2,0:T(8,128)S(1)} custom-call(f32[1,64,64]{2,1,0:T(8,128)S(1)} %fusion.32), custom_call_target="InvertDiagBlocksLowerTriangular" | custom-call | tf_op jit(solution)/shard_map/triangular_solve/custom-call.0 | solution.py:21
  69.5 0.8 %copy.13 = f32[256,256]{1,0:T(8,128)} copy(f32[256,256]{0,1:T(8,128)S(1)} %fusion.4) | data formatting | bytes 524288
  71.2 3.2 %convolution_multiply_fusion = f32[2048,256]{1,0:T(8,128)} fusion(f32[2048,256]{1,0:T(8,128)S(1)} %add_multiply_fusion, f32[128,128]{1,0:T(8,128)S(1)} %select_maximum_fusion.3, f32[64,64]{1,0:T(8,128)S(1)} %get-tuple-element.10, f32[64,64]{1,0:T(8,128)S(1)} %convolution_negate_fusion.1, f32[64,128]{1,0:T(8,128)S(1)} %concatenate.61, ...), kind=kOutput, calls=%fused_computation.4 | convolution fusion | flops 1611530240 | bytes 4390912 | tf_op jit(solution)/shard_map/dot_general | solution.py:139
  (48 shorter events, 6.8 us)
Async XLA Ops:
  0.6 1.5 %copy-start = (f32[2048,64]{0,1:T(8,128)S(1)}, f32[2048,64]{0,1:T(8,128)}, u32[]{:S(2)}) copy-start(f32[2048,64]{0,1:T(8,128)} %param.9) | copy-start | bytes 1572868
  8.9 1.5 %collective-permute-start = (f32[136,128]{1,0:T(8,128)S(1)}, f32[136,128]{1,0:T(8,128)S(1)}, u32[]{:S(2)}, u32[]{:S(2)}) collective-permute-start(f32[136,128]{1,0:T(8,128)S(1)} %pad_select_fusion), channel_id=1, source_target_pairs={{0,1},{1,0},{2,3},{3,2},{4,5},{5,4},{6,7},{7,6},{8,9},{9,8},{10,11... | collective-permute-start | bytes 208904 | tf_op jit(solution)/shard_map/ppermute | solution.py:72
  10.5 6.4 %collective-permute-start.3 = (f32[136,128]{1,0:T(8,128)S(1)}, f32[136,128]{1,0:T(8,128)S(1)}, u32[]{:S(2)}, u32[]{:S(2)}) collective-permute-start(f32[136,128]{1,0:T(8,128)S(1)} %select_add_fusion), channel_id=1, source_target_pairs={{0,6},{1,7},{2,4},{3,5},{4,2},{5,3},{6,0},{7,1},{8,14},{9,15},{10,... | collective-permute-start | bytes 208904 | tf_op jit(solution)/shard_map/ppermute | solution.py:72
  14.3 5.2 %collective-permute-start.2 = (f32[136,128]{1,0:T(8,128)S(1)}, f32[136,128]{1,0:T(8,128)S(1)}, u32[]{:S(2)}, u32[]{:S(2)}) collective-permute-start(f32[136,128]{1,0:T(8,128)S(1)} %select_add_fusion), channel_id=1, source_target_pairs={{0,4},{1,5},{2,6},{3,7},{4,0},{5,1},{6,2},{7,3},{8,12},{9,13},{10,... | collective-permute-start | bytes 208904 | tf_op jit(solution)/shard_map/ppermute | solution.py:72
  15.8 4.3 %collective-permute-start.1 = (f32[136,128]{1,0:T(8,128)S(1)}, f32[136,128]{1,0:T(8,128)S(1)}, u32[]{:S(2)}, u32[]{:S(2)}) collective-permute-start(f32[136,128]{1,0:T(8,128)S(1)} %select_add_fusion), channel_id=1, source_target_pairs={{0,2},{1,3},{2,0},{3,1},{4,6},{5,7},{6,4},{7,5},{8,10},{9,11},{10,... | collective-permute-start | bytes 208904 | tf_op jit(solution)/shard_map/ppermute | solution.py:72
  20.2 6.3 %collective-permute-start.6 = (f32[136,128]{1,0:T(8,128)S(1)}, f32[136,128]{1,0:T(8,128)S(1)}, u32[]{:S(2)}, u32[]{:S(2)}) collective-permute-start(f32[136,128]{1,0:T(8,128)S(1)} %add_add_fusion.1), channel_id=1, source_target_pairs={{0,24},{1,25},{2,26},{3,27},{4,28},{5,29},{6,30},{7,31},{8,16},{9,... | collective-permute-start | bytes 208904 | tf_op jit(solution)/shard_map/ppermute | solution.py:72
  22.9 5.5 %collective-permute-start.5 = (f32[136,128]{1,0:T(8,128)S(1)}, f32[136,128]{1,0:T(8,128)S(1)}, u32[]{:S(2)}, u32[]{:S(2)}) collective-permute-start(f32[136,128]{1,0:T(8,128)S(1)} %add_add_fusion.1), channel_id=1, source_target_pairs={{0,16},{1,17},{2,18},{3,19},{4,20},{5,21},{6,22},{7,23},{8,24},{9,... | collective-permute-start | bytes 208904 | tf_op jit(solution)/shard_map/ppermute | solution.py:72
  22.9 5.5 %collective-permute-start.4 = (f32[136,128]{1,0:T(8,128)S(1)}, f32[136,128]{1,0:T(8,128)S(1)}, u32[]{:S(2)}, u32[]{:S(2)}) collective-permute-start(f32[136,128]{1,0:T(8,128)S(1)} %add_add_fusion.1), channel_id=1, source_target_pairs={{0,8},{1,9},{2,10},{3,11},{4,12},{5,13},{6,14},{7,15},{8,0},{9,1},... | collective-permute-start | bytes 208904 | tf_op jit(solution)/shard_map/ppermute | solution.py:72
  28.4 1.3 %collective-permute-start.7 = (f32[136,128]{1,0:T(8,128)S(1)}, f32[136,128]{1,0:T(8,128)S(1)}, u32[]{:S(2)}, u32[]{:S(2)}) collective-permute-start(f32[136,128]{1,0:T(8,128)S(1)} %add_add_fusion), channel_id=1, source_target_pairs={{0,1},{1,0},{2,3},{3,2},{4,5},{5,4},{6,7},{7,6},{8,9},{9,8},{10,11... | collective-permute-start | bytes 208904 | tf_op jit(solution)/shard_map/ppermute | solution.py:72
  48.2 1.3 %collective-permute-start.8 = (f32[64,64]{1,0:T(8,128)S(1)}, f32[64,64]{1,0:T(8,128)S(1)}, u32[]{:S(2)}, u32[]{:S(2)}) collective-permute-start(f32[64,64]{1,0:T(8,128)S(1)} %fusion.27), channel_id=1, source_target_pairs={{0,1},{1,0},{2,3},{3,2},{4,5},{5,4},{6,7},{7,6},{8,9},{9,8},{10,11... | collective-permute-start | bytes 49160 | tf_op jit(solution)/shard_map/ppermute | solution.py:72
  69.3 1.3 %collective-permute-start.9 = (f32[64,64]{1,0:T(8,128)S(1)}, f32[64,64]{1,0:T(8,128)S(1)}, u32[]{:S(2)}, u32[]{:S(2)}) collective-permute-start(f32[64,64]{1,0:T(8,128)S(1)} %fusion.25), channel_id=1, source_target_pairs={{0,1},{1,0},{2,3},{3,2},{4,5},{5,4},{6,7},{7,6},{8,9},{9,8},{10,11... | collective-permute-start | bytes 49160 | tf_op jit(solution)/shard_map/ppermute | solution.py:72

commit v20 on v18

--- a/solution.py
+++ b/solution.py
@@ -89,9 +89,9 @@
             rest = []
         else:
             ma, mb = 1 << rest[0], 1 << rest[1]
-            near = keep + flip(keep, ma)
-            far = flip(keep, mb) + flip(keep, ma | mb)
-            keep = near + far
+            far = flip(keep, ma | mb) + flip(keep, mb)
+            near = flip(keep, ma) + keep
+            keep = far + near
             rest = rest[2:]
     other = flip(keep, 1)
     first = jnp.where(low, keep, other)

time: 74.9 us -> 76.9 us (1.027)
  waiting for transfers between devices: 12.4 us -> 14.3 us
    ppermute x10, waiting for transfers between devices: 12.4 us -> 14.3 us  [flip(): return lax.ppermute(array, axes, [(i, i ^ mask) for i in range(count)])]
  transfers between devices with their start and end apart: 10 -> 10, of which waited for: 9 -> 10; matrix products, arithmetic and copies ran while one was open for 1% -> 1% of each run, Pallas kernels for 0% -> 0%
where the time goes in v20:
time: 76.9 us; the launch traced here: 76.6 us
  other arithmetic  37.1 us (48%)
  waiting for transfers between devices  14.3 us (19%)
  matrix products  12.2 us (16%)
  starting transfers between devices  10.1 us (13%)
  between operations  1.6 us (2%)
  local copies, waits for them, and re-layouts  1.24 us (2%)
    ppermute x10, waiting for transfers between devices, flip(): return lax.ppermute(array, axes, [(i, i ^ mask) for i in range(count)])  14.3 us
    another operation x3, other arithmetic, cholesky_and_inverse(): l22 = lax.linalg.cholesky(g22 - mm(l21, l21.T), symmetrize_input=False)  12.4 us
    another operation x3, other arithmetic, cholesky_and_inverse(): l11 = lax.linalg.cholesky(g11, symmetrize_input=False)  12.4 us
    ppermute x10, starting transfers between devices, flip(): return lax.ppermute(array, axes, [(i, i ^ mask) for i in range(count)])  10.1 us
    another operation x4, other arithmetic, shared_inverse(): lax.linalg.triangular_solve(block, jnp.eye(q, dtype=lower.dtype), left_si...  9.95 us
    dot_general x1, matrix products, per_device(): jnp.dot(inputs, freqs, precision=lax.Precision.HIGHEST) + phases[None, :]  4.27 us
    dot_general x1, matrix products, per_device(): lax.dot_general(features, inverse, (((1,), (1,)), ((), ())), precision=la...  3.18 us
    dot_general x4, matrix products, tdot(): lax.dot_general(a, b, (((0,), (0,)), ((), ())), preferred_element_type=jn...  2.32 us
  transfers between devices with their start and end apart: 10, of which 10 were waited for; matrix products, arithmetic and copies ran while one was open for 1% of the time, Pallas kernels for 0%

profile of v20, /device:TPU:0, one launch (start us, length us, event | category | flops | bytes accessed | tf_op | source)
XLA Modules:
  0.0 76.6 jit_solution(349997831396247293)
XLA Ops:
  1.4 0.7 sqrt_multiply_fusion
  2.1 4.3 %fusion.1 = f32[2048,256]{1,0:T(8,128)S(1)} fusion(f32[2048,64]{0,1:T(8,128)S(1)} %copy-done, f32[64,256]{1,0:T(8,128)} %param.10, f32[256]{0:T(256)} %param.11, f32[2048]{0:T(1024)S(1)} %sqrt_multiply_fusion), kind=kOutput, calls=%fused_computation.10 | convolution fusion | flops 415236096 | bytes 2696192 | tf_op jit(solution)/shard_map/dot_general | solution.py:133
  6.4 0.7 fusion.2
  9.6 0.9 %collective-permute-done = f32[136,128]{1,0:T(8,128)S(1)} collective-permute-done((f32[136,128]{1,0:T(8,128)S(1)}, f32[136,128]{1,0:T(8,128)S(1)}, u32[]{:S(2)}, u32[]{:S(2)}) %collective-permute-start) | collective-permute-done | bytes 69664 | tf_op jit(solution)/shard_map/ppermute | solution.py:72
  10.6 2.9 %collective-permute-start.3 = (f32[136,128]{1,0:T(8,128)S(1)}, f32[136,128]{1,0:T(8,128)S(1)}, u32[]{:S(2)}, u32[]{:S(2)}) collective-permute-start(f32[136,128]{1,0:T(8,128)S(1)} %select_add_fusion), channel_id=1, source_target_pairs={{0,2},{1,3},{2,0},{3,1},{4,6},{5,7},{6,4},{7,5},{8,10},{9,11},{10,... | collective-permute-start | bytes 208904 | tf_op jit(solution)/shard_map/ppermute | solution.py:72
  13.6 1.5 %collective-permute-start.2 = (f32[136,128]{1,0:T(8,128)S(1)}, f32[136,128]{1,0:T(8,128)S(1)}, u32[]{:S(2)}, u32[]{:S(2)}) collective-permute-start(f32[136,128]{1,0:T(8,128)S(1)} %select_add_fusion), channel_id=1, source_target_pairs={{0,4},{1,5},{2,6},{3,7},{4,0},{5,1},{6,2},{7,3},{8,12},{9,13},{10,... | collective-permute-start | bytes 208904 | tf_op jit(solution)/shard_map/ppermute | solution.py:72
  15.1 1.0 %collective-permute-done.3 = f32[136,128]{1,0:T(8,128)S(1)} collective-permute-done((f32[136,128]{1,0:T(8,128)S(1)}, f32[136,128]{1,0:T(8,128)S(1)}, u32[]{:S(2)}, u32[]{:S(2)}) %collective-permute-start.3) | collective-permute-done | bytes 69664 | tf_op jit(solution)/shard_map/ppermute | solution.py:72
  16.1 2.5 %collective-permute-done.2 = f32[136,128]{1,0:T(8,128)S(1)} collective-permute-done((f32[136,128]{1,0:T(8,128)S(1)}, f32[136,128]{1,0:T(8,128)S(1)}, u32[]{:S(2)}, u32[]{:S(2)}) %collective-permute-start.2) | collective-permute-done | bytes 69664 | tf_op jit(solution)/shard_map/ppermute | solution.py:72
  18.6 1.7 %collective-permute-done.1 = f32[136,128]{1,0:T(8,128)S(1)} collective-permute-done((f32[136,128]{1,0:T(8,128)S(1)}, f32[136,128]{1,0:T(8,128)S(1)}, u32[]{:S(2)}, u32[]{:S(2)}) %collective-permute-start.1) | collective-permute-done | bytes 69664 | tf_op jit(solution)/shard_map/ppermute | solution.py:72
  20.3 1.6 %collective-permute-start.6 = (f32[136,128]{1,0:T(8,128)S(1)}, f32[136,128]{1,0:T(8,128)S(1)}, u32[]{:S(2)}, u32[]{:S(2)}) collective-permute-start(f32[136,128]{1,0:T(8,128)S(1)} %add_add_fusion.1), channel_id=1, source_target_pairs={{0,8},{1,9},{2,10},{3,11},{4,12},{5,13},{6,14},{7,15},{8,0},{9,1},... | collective-permute-start | bytes 208904 | tf_op jit(solution)/shard_map/ppermute | solution.py:72
  21.9 2.6 %collective-permute-start.5 = (f32[136,128]{1,0:T(8,128)S(1)}, f32[136,128]{1,0:T(8,128)S(1)}, u32[]{:S(2)}, u32[]{:S(2)}) collective-permute-start(f32[136,128]{1,0:T(8,128)S(1)} %add_add_fusion.1), channel_id=1, source_target_pairs={{0,16},{1,17},{2,18},{3,19},{4,20},{5,21},{6,22},{7,23},{8,24},{9,... | collective-permute-start | bytes 208904 | tf_op jit(solution)/shard_map/ppermute | solution.py:72
  25.1 2.4 %collective-permute-done.5 = f32[136,128]{1,0:T(8,128)S(1)} collective-permute-done((f32[136,128]{1,0:T(8,128)S(1)}, f32[136,128]{1,0:T(8,128)S(1)}, u32[]{:S(2)}, u32[]{:S(2)}) %collective-permute-start.5) | collective-permute-done | bytes 69664 | tf_op jit(solution)/shard_map/ppermute | solution.py:72
  27.5 3.2 %collective-permute-done.4 = f32[136,128]{1,0:T(8,128)S(1)} collective-permute-done((f32[136,128]{1,0:T(8,128)S(1)}, f32[136,128]{1,0:T(8,128)S(1)}, u32[]{:S(2)}, u32[]{:S(2)}) %collective-permute-start.4) | collective-permute-done | bytes 69664 | tf_op jit(solution)/shard_map/ppermute | solution.py:72
  30.7 1.2 %collective-permute-done.7 = f32[136,128]{1,0:T(8,128)S(1)} collective-permute-done((f32[136,128]{1,0:T(8,128)S(1)}, f32[136,128]{1,0:T(8,128)S(1)}, u32[]{:S(2)}, u32[]{:S(2)}) %collective-permute-start.7) | collective-permute-done | bytes 69664 | tf_op jit(solution)/shard_map/ppermute | solution.py:72
  32.1 11.7 %custom-call.8 = f32[128,128]{1,0:T(8,128)S(1)} custom-call(f32[128,128]{1,0:T(8,128)S(1)} %bitcast_select_fusion.1), custom_call_target="Cholesky" | custom-call | tf_op jit(solution)/shard_map/cholesky/custom-call.1 | solution.py:33
  43.9 0.6 compare_reduce_fusion.1
  44.5 0.7 select_select_fusion.1
  45.2 4.9 %custom-call.9 = f32[1,64,64]{1,2,0:T(8,128)S(1)} custom-call(f32[1,64,64]{2,1,0:T(8,128)S(1)} %fusion.37), custom_call_target="InvertDiagBlocksLowerTriangular" | custom-call | tf_op jit(solution)/shard_map/triangular_solve/custom-call.0 | solution.py:21
  50.6 1.0 %collective-permute-done.8 = f32[64,64]{1,0:T(8,128)S(1)} collective-permute-done((f32[64,64]{1,0:T(8,128)S(1)}, f32[64,64]{1,0:T(8,128)S(1)}, u32[]{:S(2)}, u32[]{:S(2)}) %collective-permute-start.8) | collective-permute-done | bytes 16416 | tf_op jit(solution)/shard_map/ppermute | solution.py:72
  53.2 11.7 %custom-call.10 = f32[128,128]{1,0:T(8,128)S(1)} custom-call(f32[128,128]{1,0:T(8,128)S(1)} %fusion.23), custom_call_target="Cholesky" | custom-call | tf_op jit(solution)/shard_map/cholesky/custom-call.1 | solution.py:36
  65.6 0.7 select_select_fusion
  66.4 4.9 %custom-call.11 = f32[1,64,64]{1,2,0:T(8,128)S(1)} custom-call(f32[1,64,64]{2,1,0:T(8,128)S(1)} %fusion.33), custom_call_target="InvertDiagBlocksLowerTriangular" | custom-call | tf_op jit(solution)/shard_map/triangular_solve/custom-call.0 | solution.py:21
  71.8 0.8 %copy.13 = f32[256,256]{1,0:T(8,128)} copy(f32[256,256]{0,1:T(8,128)S(1)} %fusion.5) | data formatting | bytes 524288
  73.4 3.2 %convolution_multiply_fusion = f32[2048,256]{1,0:T(8,128)} fusion(f32[2048,256]{1,0:T(8,128)S(1)} %fusion.1, f32[128,128]{1,0:T(8,128)S(1)} %select_maximum_fusion.3, f32[64,64]{1,0:T(8,128)S(1)} %get-tuple-element.10, f32[64,64]{1,0:T(8,128)S(1)} %convolution_negate_fusion.1, f32[64,128]{1,0:T(8,128)S(1)} %concatenate.61, ...), kind=kOutput, calls=%fused_computation.6 | convolution fusion | flops 1611530240 | bytes 4390912 | tf_op jit(solution)/shard_map/dot_general | solution.py:140
  (48 shorter events, 7.6 us)
Async XLA Ops:
  0.6 1.5 %copy-start = (f32[2048,64]{0,1:T(8,128)S(1)}, f32[2048,64]{0,1:T(8,128)}, u32[]{:S(2)}) copy-start(f32[2048,64]{0,1:T(8,128)} %param.9) | copy-start | bytes 1572868
  9.1 1.5 %collective-permute-start = (f32[136,128]{1,0:T(8,128)S(1)}, f32[136,128]{1,0:T(8,128)S(1)}, u32[]{:S(2)}, u32[]{:S(2)}) collective-permute-start(f32[136,128]{1,0:T(8,128)S(1)} %pad_select_fusion), channel_id=1, source_target_pairs={{0,1},{1,0},{2,3},{3,2},{4,5},{5,4},{6,7},{7,6},{8,9},{9,8},{10,11... | collective-permute-start | bytes 208904 | tf_op jit(solution)/shard_map/ppermute | solution.py:72
  10.6 5.4 %collective-permute-start.3 = (f32[136,128]{1,0:T(8,128)S(1)}, f32[136,128]{1,0:T(8,128)S(1)}, u32[]{:S(2)}, u32[]{:S(2)}) collective-permute-start(f32[136,128]{1,0:T(8,128)S(1)} %select_add_fusion), channel_id=1, source_target_pairs={{0,2},{1,3},{2,0},{3,1},{4,6},{5,7},{6,4},{7,5},{8,10},{9,11},{10,... | collective-permute-start | bytes 208904 | tf_op jit(solution)/shard_map/ppermute | solution.py:72
  13.6 5.0 %collective-permute-start.2 = (f32[136,128]{1,0:T(8,128)S(1)}, f32[136,128]{1,0:T(8,128)S(1)}, u32[]{:S(2)}, u32[]{:S(2)}) collective-permute-start(f32[136,128]{1,0:T(8,128)S(1)} %select_add_fusion), channel_id=1, source_target_pairs={{0,4},{1,5},{2,6},{3,7},{4,0},{5,1},{6,2},{7,3},{8,12},{9,13},{10,... | collective-permute-start | bytes 208904 | tf_op jit(solution)/shard_map/ppermute | solution.py:72
  15.1 5.2 %collective-permute-start.1 = (f32[136,128]{1,0:T(8,128)S(1)}, f32[136,128]{1,0:T(8,128)S(1)}, u32[]{:S(2)}, u32[]{:S(2)}) collective-permute-start(f32[136,128]{1,0:T(8,128)S(1)} %select_add_fusion), channel_id=1, source_target_pairs={{0,6},{1,7},{2,4},{3,5},{4,2},{5,3},{6,0},{7,1},{8,14},{9,15},{10,... | collective-permute-start | bytes 208904 | tf_op jit(solution)/shard_map/ppermute | solution.py:72
  20.3 4.8 %collective-permute-start.6 = (f32[136,128]{1,0:T(8,128)S(1)}, f32[136,128]{1,0:T(8,128)S(1)}, u32[]{:S(2)}, u32[]{:S(2)}) collective-permute-start(f32[136,128]{1,0:T(8,128)S(1)} %add_add_fusion.1), channel_id=1, source_target_pairs={{0,8},{1,9},{2,10},{3,11},{4,12},{5,13},{6,14},{7,15},{8,0},{9,1},... | collective-permute-start | bytes 208904 | tf_op jit(solution)/shard_map/ppermute | solution.py:72
  21.9 5.5 %collective-permute-start.5 = (f32[136,128]{1,0:T(8,128)S(1)}, f32[136,128]{1,0:T(8,128)S(1)}, u32[]{:S(2)}, u32[]{:S(2)}) collective-permute-start(f32[136,128]{1,0:T(8,128)S(1)} %add_add_fusion.1), channel_id=1, source_target_pairs={{0,16},{1,17},{2,18},{3,19},{4,20},{5,21},{6,22},{7,23},{8,24},{9,... | collective-permute-start | bytes 208904 | tf_op jit(solution)/shard_map/ppermute | solution.py:72
  24.5 6.1 %collective-permute-start.4 = (f32[136,128]{1,0:T(8,128)S(1)}, f32[136,128]{1,0:T(8,128)S(1)}, u32[]{:S(2)}, u32[]{:S(2)}) collective-permute-start(f32[136,128]{1,0:T(8,128)S(1)} %add_add_fusion.1), channel_id=1, source_target_pairs={{0,24},{1,25},{2,26},{3,27},{4,28},{5,29},{6,30},{7,31},{8,16},{9,... | collective-permute-start | bytes 208904 | tf_op jit(solution)/shard_map/ppermute | solution.py:72
  30.6 1.3 %collective-permute-start.7 = (f32[136,128]{1,0:T(8,128)S(1)}, f32[136,128]{1,0:T(8,128)S(1)}, u32[]{:S(2)}, u32[]{:S(2)}) collective-permute-start(f32[136,128]{1,0:T(8,128)S(1)} %add_add_fusion), channel_id=1, source_target_pairs={{0,1},{1,0},{2,3},{3,2},{4,5},{5,4},{6,7},{7,6},{8,9},{9,8},{10,11... | collective-permute-start | bytes 208904 | tf_op jit(solution)/shard_map/ppermute | solution.py:72
  50.4 1.3 %collective-permute-start.8 = (f32[64,64]{1,0:T(8,128)S(1)}, f32[64,64]{1,0:T(8,128)S(1)}, u32[]{:S(2)}, u32[]{:S(2)}) collective-permute-start(f32[64,64]{1,0:T(8,128)S(1)} %fusion.28), channel_id=1, source_target_pairs={{0,1},{1,0},{2,3},{3,2},{4,5},{5,4},{6,7},{7,6},{8,9},{9,8},{10,11... | collective-permute-start | bytes 49160 | tf_op jit(solution)/shard_map/ppermute | solution.py:72
  71.5 1.3 %collective-permute-start.9 = (f32[64,64]{1,0:T(8,128)S(1)}, f32[64,64]{1,0:T(8,128)S(1)}, u32[]{:S(2)}, u32[]{:S(2)}) collective-permute-start(f32[64,64]{1,0:T(8,128)S(1)} %fusion.26), channel_id=1, source_target_pairs={{0,1},{1,0},{2,3},{3,2},{4,5},{5,4},{6,7},{7,6},{8,9},{9,8},{10,11... | collective-permute-start | bytes 49160 | tf_op jit(solution)/shard_map/ppermute | solution.py:72

commit v21 on v18

--- a/solution.py
+++ b/solution.py
@@ -138,8 +138,9 @@
     gram = all_reduce_symmetric(gram)
     lower, inverse = cholesky_and_inverse(*gram)
     basis = lax.dot_general(
-        features, inverse, (((1,), (1,)), ((), ())), precision=lax.Precision.HIGHEST
-    ) * math.sqrt(total_rows)
+        features, inverse * math.sqrt(total_rows), (((1,), (1,)), ((), ())),
+        precision=lax.Precision.HIGHEST,
+    )
     return (lower.T, basis)
 
 

time: 74.9 us -> 74.7 us (level)
  waiting for transfers between devices: 12.4 us -> 11.4 us
  starting transfers between devices: 10 us -> 10.8 us
    ppermute x10, waiting for transfers between devices: 12.4 us -> 11.4 us  [flip(): return lax.ppermute(array, axes, [(i, i ^ mask) for i in range(count)])]
    ppermute x10, starting transfers between devices: 10 us -> 10.8 us  [flip(): return lax.ppermute(array, axes, [(i, i ^ mask) for i in range(count)])]
where the time goes in v21:
time: 74.7 us; the launch traced here: 74.5 us
  other arithmetic  37.1 us (50%)
  matrix products  12.2 us (16%)
  waiting for transfers between devices  11.4 us (15%)
  starting transfers between devices  10.8 us (14%)
  between operations  1.61 us (2%)
  local copies, waits for them, and re-layouts  1.24 us (2%)
    another operation x3, other arithmetic, cholesky_and_inverse(): l22 = lax.linalg.cholesky(g22 - mm(l21, l21.T), symmetrize_input=False)  12.4 us
    another operation x3, other arithmetic, cholesky_and_inverse(): l11 = lax.linalg.cholesky(g11, symmetrize_input=False)  12.4 us
    ppermute x10, waiting for transfers between devices, flip(): return lax.ppermute(array, axes, [(i, i ^ mask) for i in range(count)])  11.4 us
    ppermute x10, starting transfers between devices, flip(): return lax.ppermute(array, axes, [(i, i ^ mask) for i in range(count)])  10.8 us
    another operation x4, other arithmetic, shared_inverse(): lax.linalg.triangular_solve(block, jnp.eye(q, dtype=lower.dtype), left_si...  9.95 us
    dot_general x1, matrix products, per_device(): jnp.dot(inputs, freqs, precision=lax.Precision.HIGHEST) + phases[None, :]  4.27 us
    dot_general x1, matrix products, per_device(): lax.dot_general(features, inverse * math.sqrt(total_rows), (((1,), (1,)),...  3.18 us
    dot_general x4, matrix products, tdot(): lax.dot_general(a, b, (((0,), (0,)), ((), ())), preferred_element_type=jn...  2.32 us
  transfers between devices with their start and end apart: 10, of which 9 were waited for; matrix products, arithmetic and copies ran while one was open for 1% of the time, Pallas kernels for 0%

profile of v21, /device:TPU:0, one launch (start us, length us, event | category | flops | bytes accessed | tf_op | source)
XLA Modules:
  0.0 74.5 jit_solution(11990998345040424348)
XLA Ops:
  1.4 0.7 sqrt_multiply_fusion
  2.1 4.3 %fusion.1 = f32[2048,256]{1,0:T(8,128)S(1)} fusion(f32[2048,64]{0,1:T(8,128)S(1)} %copy-done, f32[64,256]{1,0:T(8,128)} %param.10, f32[256]{0:T(256)} %param.11, f32[2048]{0:T(1024)S(1)} %sqrt_multiply_fusion), kind=kOutput, calls=%fused_computation.9 | convolution fusion | flops 415236096 | bytes 2696192 | tf_op jit(solution)/shard_map/dot_general | solution.py:133
  6.4 0.7 fusion.2
  9.6 0.9 %collective-permute-done = f32[136,128]{1,0:T(8,128)S(1)} collective-permute-done((f32[136,128]{1,0:T(8,128)S(1)}, f32[136,128]{1,0:T(8,128)S(1)}, u32[]{:S(2)}, u32[]{:S(2)}) %collective-permute-start) | collective-permute-done | bytes 69664 | tf_op jit(solution)/shard_map/ppermute | solution.py:72
  10.6 3.8 %collective-permute-start.3 = (f32[136,128]{1,0:T(8,128)S(1)}, f32[136,128]{1,0:T(8,128)S(1)}, u32[]{:S(2)}, u32[]{:S(2)}) collective-permute-start(f32[136,128]{1,0:T(8,128)S(1)} %select_add_fusion), channel_id=1, source_target_pairs={{0,6},{1,7},{2,4},{3,5},{4,2},{5,3},{6,0},{7,1},{8,14},{9,15},{10,... | collective-permute-start | bytes 208904 | tf_op jit(solution)/shard_map/ppermute | solution.py:72
  15.0 0.9 %collective-permute-start.1 = (f32[136,128]{1,0:T(8,128)S(1)}, f32[136,128]{1,0:T(8,128)S(1)}, u32[]{:S(2)}, u32[]{:S(2)}) collective-permute-start(f32[136,128]{1,0:T(8,128)S(1)} %select_add_fusion), channel_id=1, source_target_pairs={{0,2},{1,3},{2,0},{3,1},{4,6},{5,7},{6,4},{7,5},{8,10},{9,11},{10,... | collective-permute-start | bytes 208904 | tf_op jit(solution)/shard_map/ppermute | solution.py:72
  16.0 1.1 %collective-permute-done.3 = f32[136,128]{1,0:T(8,128)S(1)} collective-permute-done((f32[136,128]{1,0:T(8,128)S(1)}, f32[136,128]{1,0:T(8,128)S(1)}, u32[]{:S(2)}, u32[]{:S(2)}) %collective-permute-start.3) | collective-permute-done | bytes 69664 | tf_op jit(solution)/shard_map/ppermute | solution.py:72
  17.0 1.8 %collective-permute-done.2 = f32[136,128]{1,0:T(8,128)S(1)} collective-permute-done((f32[136,128]{1,0:T(8,128)S(1)}, f32[136,128]{1,0:T(8,128)S(1)}, u32[]{:S(2)}, u32[]{:S(2)}) %collective-permute-start.2) | collective-permute-done | bytes 69664 | tf_op jit(solution)/shard_map/ppermute | solution.py:72
  19.4 3.7 %collective-permute-start.6 = (f32[136,128]{1,0:T(8,128)S(1)}, f32[136,128]{1,0:T(8,128)S(1)}, u32[]{:S(2)}, u32[]{:S(2)}) collective-permute-start(f32[136,128]{1,0:T(8,128)S(1)} %add_add_fusion.1), channel_id=1, source_target_pairs={{0,24},{1,25},{2,26},{3,27},{4,28},{5,29},{6,30},{7,31},{8,16},{9,... | collective-permute-start | bytes 208904 | tf_op jit(solution)/shard_map/ppermute | solution.py:72
  23.0 0.8 %collective-permute-start.4 = (f32[136,128]{1,0:T(8,128)S(1)}, f32[136,128]{1,0:T(8,128)S(1)}, u32[]{:S(2)}, u32[]{:S(2)}) collective-permute-start(f32[136,128]{1,0:T(8,128)S(1)} %add_add_fusion.1), channel_id=1, source_target_pairs={{0,8},{1,9},{2,10},{3,11},{4,12},{5,13},{6,14},{7,15},{8,0},{9,1},... | collective-permute-start | bytes 208904 | tf_op jit(solution)/shard_map/ppermute | solution.py:72
  23.8 2.0 %collective-permute-done.6 = f32[136,128]{1,0:T(8,128)S(1)} collective-permute-done((f32[136,128]{1,0:T(8,128)S(1)}, f32[136,128]{1,0:T(8,128)S(1)}, u32[]{:S(2)}, u32[]{:S(2)}) %collective-permute-start.6) | collective-permute-done | bytes 69664 | tf_op jit(solution)/shard_map/ppermute | solution.py:72
  25.8 2.7 %collective-permute-done.5 = f32[136,128]{1,0:T(8,128)S(1)} collective-permute-done((f32[136,128]{1,0:T(8,128)S(1)}, f32[136,128]{1,0:T(8,128)S(1)}, u32[]{:S(2)}, u32[]{:S(2)}) %collective-permute-start.5) | collective-permute-done | bytes 69664 | tf_op jit(solution)/shard_map/ppermute | solution.py:72
  28.6 1.2 %collective-permute-done.7 = f32[136,128]{1,0:T(8,128)S(1)} collective-permute-done((f32[136,128]{1,0:T(8,128)S(1)}, f32[136,128]{1,0:T(8,128)S(1)}, u32[]{:S(2)}, u32[]{:S(2)}) %collective-permute-start.7) | collective-permute-done | bytes 69664 | tf_op jit(solution)/shard_map/ppermute | solution.py:72
  30.0 11.7 %custom-call.8 = f32[128,128]{1,0:T(8,128)S(1)} custom-call(f32[128,128]{1,0:T(8,128)S(1)} %bitcast_select_fusion.1), custom_call_target="Cholesky" | custom-call | tf_op jit(solution)/shard_map/cholesky/custom-call.1 | solution.py:33
  41.7 0.6 compare_reduce_fusion.1
  42.4 0.7 select_select_fusion.1
  43.1 4.9 %custom-call.9 = f32[1,64,64]{1,2,0:T(8,128)S(1)} custom-call(f32[1,64,64]{2,1,0:T(8,128)S(1)} %fusion.41), custom_call_target="InvertDiagBlocksLowerTriangular" | custom-call | tf_op jit(solution)/shard_map/triangular_solve/custom-call.0 | solution.py:21
  48.5 1.0 %collective-permute-done.8 = f32[64,64]{1,0:T(8,128)S(1)} collective-permute-done((f32[64,64]{1,0:T(8,128)S(1)}, f32[64,64]{1,0:T(8,128)S(1)}, u32[]{:S(2)}, u32[]{:S(2)}) %collective-permute-start.8) | collective-permute-done | bytes 16416 | tf_op jit(solution)/shard_map/ppermute | solution.py:72
  51.1 11.7 %custom-call.10 = f32[128,128]{1,0:T(8,128)S(1)} custom-call(f32[128,128]{1,0:T(8,128)S(1)} %fusion.27), custom_call_target="Cholesky" | custom-call | tf_op jit(solution)/shard_map/cholesky/custom-call.1 | solution.py:36
  62.8 0.6 compare_reduce_fusion
  63.5 0.7 select_select_fusion
  64.2 4.9 %custom-call.11 = f32[1,64,64]{1,2,0:T(8,128)S(1)} custom-call(f32[1,64,64]{2,1,0:T(8,128)S(1)} %fusion.37), custom_call_target="InvertDiagBlocksLowerTriangular" | custom-call | tf_op jit(solution)/shard_map/triangular_solve/custom-call.0 | solution.py:21
  69.6 0.8 %copy.13 = f32[256,256]{1,0:T(8,128)} copy(f32[256,256]{0,1:T(8,128)S(1)} %fusion.8) | data formatting | bytes 524288
  71.3 3.2 %fusion.5 = f32[2048,256]{1,0:T(8,128)} fusion(f32[2048,256]{1,0:T(8,128)S(1)} %fusion.1, f32[128,128]{1,0:T(8,128)S(1)} %select_maximum_fusion.2, f32[64,64]{1,0:T(8,128)S(1)} %get-tuple-element.10, f32[64,64]{1,0:T(8,128)S(1)} %convolution_negate_fusion.1, f32[64,128]{1,0:T(8,128)S(1)} %concatenate.61, f32[128,128]{1,0:T(8,128)S(1)} %convolution_negate_fusion), kind=kOutput, calls=%fused_computation.19 | convolution fusion | flops 1611071488 | bytes 4390912 | tf_op jit(solution)/shard_map/dot_general | solution.py:140
  (48 shorter events, 7.4 us)
Async XLA Ops:
  0.6 1.5 %copy-start = (f32[2048,64]{0,1:T(8,128)S(1)}, f32[2048,64]{0,1:T(8,128)}, u32[]{:S(2)}) copy-start(f32[2048,64]{0,1:T(8,128)} %param.9) | copy-start | bytes 1572868
  9.1 1.5 %collective-permute-start = (f32[136,128]{1,0:T(8,128)S(1)}, f32[136,128]{1,0:T(8,128)S(1)}, u32[]{:S(2)}, u32[]{:S(2)}) collective-permute-start(f32[136,128]{1,0:T(8,128)S(1)} %pad_select_fusion), channel_id=1, source_target_pairs={{0,1},{1,0},{2,3},{3,2},{4,5},{5,4},{6,7},{7,6},{8,9},{9,8},{10,11... | collective-permute-start | bytes 208904 | tf_op jit(solution)/shard_map/ppermute | solution.py:72
  10.6 6.4 %collective-permute-start.3 = (f32[136,128]{1,0:T(8,128)S(1)}, f32[136,128]{1,0:T(8,128)S(1)}, u32[]{:S(2)}, u32[]{:S(2)}) collective-permute-start(f32[136,128]{1,0:T(8,128)S(1)} %select_add_fusion), channel_id=1, source_target_pairs={{0,6},{1,7},{2,4},{3,5},{4,2},{5,3},{6,0},{7,1},{8,14},{9,15},{10,... | collective-permute-start | bytes 208904 | tf_op jit(solution)/shard_map/ppermute | solution.py:72
  14.5 4.3 %collective-permute-start.2 = (f32[136,128]{1,0:T(8,128)S(1)}, f32[136,128]{1,0:T(8,128)S(1)}, u32[]{:S(2)}, u32[]{:S(2)}) collective-permute-start(f32[136,128]{1,0:T(8,128)S(1)} %select_add_fusion), channel_id=1, source_target_pairs={{0,4},{1,5},{2,6},{3,7},{4,0},{5,1},{6,2},{7,3},{8,12},{9,13},{10,... | collective-permute-start | bytes 208904 | tf_op jit(solution)/shard_map/ppermute | solution.py:72
  15.0 4.3 %collective-permute-start.1 = (f32[136,128]{1,0:T(8,128)S(1)}, f32[136,128]{1,0:T(8,128)S(1)}, u32[]{:S(2)}, u32[]{:S(2)}) collective-permute-start(f32[136,128]{1,0:T(8,128)S(1)} %select_add_fusion), channel_id=1, source_target_pairs={{0,2},{1,3},{2,0},{3,1},{4,6},{5,7},{6,4},{7,5},{8,10},{9,11},{10,... | collective-permute-start | bytes 208904 | tf_op jit(solution)/shard_map/ppermute | solution.py:72
  19.4 6.4 %collective-permute-start.6 = (f32[136,128]{1,0:T(8,128)S(1)}, f32[136,128]{1,0:T(8,128)S(1)}, u32[]{:S(2)}, u32[]{:S(2)}) collective-permute-start(f32[136,128]{1,0:T(8,128)S(1)} %add_add_fusion.1), channel_id=1, source_target_pairs={{0,24},{1,25},{2,26},{3,27},{4,28},{5,29},{6,30},{7,31},{8,16},{9,... | collective-permute-start | bytes 208904 | tf_op jit(solution)/shard_map/ppermute | solution.py:72
  23.0 5.5 %collective-permute-start.5 = (f32[136,128]{1,0:T(8,128)S(1)}, f32[136,128]{1,0:T(8,128)S(1)}, u32[]{:S(2)}, u32[]{:S(2)}) collective-permute-start(f32[136,128]{1,0:T(8,128)S(1)} %add_add_fusion.1), channel_id=1, source_target_pairs={{0,16},{1,17},{2,18},{3,19},{4,20},{5,21},{6,22},{7,23},{8,24},{9,... | collective-permute-start | bytes 208904 | tf_op jit(solution)/shard_map/ppermute | solution.py:72
  23.0 5.5 %collective-permute-start.4 = (f32[136,128]{1,0:T(8,128)S(1)}, f32[136,128]{1,0:T(8,128)S(1)}, u32[]{:S(2)}, u32[]{:S(2)}) collective-permute-start(f32[136,128]{1,0:T(8,128)S(1)} %add_add_fusion.1), channel_id=1, source_target_pairs={{0,8},{1,9},{2,10},{3,11},{4,12},{5,13},{6,14},{7,15},{8,0},{9,1},... | collective-permute-start | bytes 208904 | tf_op jit(solution)/shard_map/ppermute | solution.py:72
  28.5 1.3 %collective-permute-start.7 = (f32[136,128]{1,0:T(8,128)S(1)}, f32[136,128]{1,0:T(8,128)S(1)}, u32[]{:S(2)}, u32[]{:S(2)}) collective-permute-start(f32[136,128]{1,0:T(8,128)S(1)} %add_add_fusion), channel_id=1, source_target_pairs={{0,1},{1,0},{2,3},{3,2},{4,5},{5,4},{6,7},{7,6},{8,9},{9,8},{10,11... | collective-permute-start | bytes 208904 | tf_op jit(solution)/shard_map/ppermute | solution.py:72
  48.3 1.3 %collective-permute-start.8 = (f32[64,64]{1,0:T(8,128)S(1)}, f32[64,64]{1,0:T(8,128)S(1)}, u32[]{:S(2)}, u32[]{:S(2)}) collective-permute-start(f32[64,64]{1,0:T(8,128)S(1)} %fusion.32), channel_id=1, source_target_pairs={{0,1},{1,0},{2,3},{3,2},{4,5},{5,4},{6,7},{7,6},{8,9},{9,8},{10,11... | collective-permute-start | bytes 49160 | tf_op jit(solution)/shard_map/ppermute | solution.py:72
  69.4 1.3 %collective-permute-start.9 = (f32[64,64]{1,0:T(8,128)S(1)}, f32[64,64]{1,0:T(8,128)S(1)}, u32[]{:S(2)}, u32[]{:S(2)}) collective-permute-start(f32[64,64]{1,0:T(8,128)S(1)} %fusion.30), channel_id=1, source_target_pairs={{0,1},{1,0},{2,3},{3,2},{4,5},{5,4},{6,7},{7,6},{8,9},{9,8},{10,11... | collective-permute-start | bytes 49160 | tf_op jit(solution)/shard_map/ppermute | solution.py:72
